TPU v7x, 256 devices: a whole 4x4x8 slice. The times are simulated.
256 devices in a mesh: space: 8 (over x_hi, y), species: 32 (over z, x_lo, core).
Axes of the slice: x: 4 (x_hi: 2, x_lo: 2; x = x_hi * 2 + x_lo), y: 4, z: 8, core: 2. Of those that a mesh axis runs over, the one named last changes fastest.
Arguments:
- dust_state: float32 [3, 128, 256, 1024], P(None, 'species', 'space'), may hold values from -4 to 4, as said below
- gas_state: float32 [3, 256, 1024], P(None, 'space'), may hold values from -2 to 2, as said below
- species_bin: int32 [128], P('species'), may hold values from 0 to 127, each once
Outputs:
- dust_out: float32 [3, 128, 256, 1024], P(None, 'species', 'space')
- gas_out: float32 [3, 256, 1024], P(None, 'space')
Inputs may be any that keep to these rules, and one draw needn't show every extreme that they name: `dust_state`: component 0 (densities) lies in 0.5 to 2; the velocities lie within -4 to 4. `gas_state`: component 0 (density) lies in 0.5 to 2; the velocities lie within -2 to 2.
All inputs are finite; a program needn't handle non-finite values.
Results may differ from a plain program's by a relative error of at most 0.0003.
Values sent between devices are 32-bit elements; how exact they have to be, the bound alone decides.
No kernel may reach another device: no remote copies, remote signals or barrier semaphores. Data moves between devices by JAX's collectives and lax.ppermute only.
A program may use at most 64 MiB of HBM per device.

v0:
```python
import jax
import jax.numpy as jnp
from jax import lax
from jax.sharding import PartitionSpec as P

STEPS = 2


courant = 0.25
sound_speed = 1.0
sound_sq = 1.0
stop_floor = 0.003
stop_span = 6.907755


def padded(block, sides, width):
    for axis, dim in sides:
        count = lax.axis_size(axis)
        forward = [(i, i + 1) for i in range(count - 1)]
        forward.append((count - 1, 0))
        backward = [(target, source) for source, target in forward]
        low = lax.ppermute(
            lax.slice_in_dim(block, block.shape[dim] - width, None, axis=dim), axis, forward
        )
        high = lax.ppermute(lax.slice_in_dim(block, 0, width, axis=dim), axis, backward)
        block = jnp.concatenate([low, block, high], axis=dim)
    return block


def window(values, start, length, along):
    return lax.slice_in_dim(values, start, start + length, axis=along)


def face_divergence(density, velocity, along):
    faces = density.shape[along] - 3
    back_two = window(density, 0, faces, along)
    here = window(density, 1, faces, along)
    ahead = window(density, 2, faces, along)
    ahead_two = window(density, 3, faces, along)
    face_speed = 0.5 * (window(velocity, 1, faces, along) + window(velocity, 2, faces, along))
    flux = jnp.maximum(face_speed, 0.0) * (1.5 * here - 0.5 * back_two) + jnp.minimum(
        face_speed, 0.0
    ) * (1.5 * ahead - 0.5 * ahead_two)
    return window(flux, 1, faces - 1, along) - window(flux, 0, faces - 1, along)


def moved(fluid, step_time):
    density = fluid[0]
    radial = fluid[1]
    azimuth = fluid[2]
    div_azimuth = face_divergence(density, azimuth, 1)
    inner_density = density[:, 2:-2]
    inner_radial = radial[:, 2:-2]
    zero_pad = ((0, 0), (0, 0), (2, 2))
    div_radial = face_divergence(
        jnp.pad(inner_density, zero_pad), jnp.pad(inner_radial, zero_pad), 2
    )
    new_density = inner_density - step_time * (div_azimuth + div_radial)
    gas_density = density[-1]
    inner_gas = gas_density[2:-2]
    grad_azimuth = 0.5 * (gas_density[3:-1] - gas_density[1:-3])
    edge_gas = jnp.pad(inner_gas, ((0, 0), (1, 1)), mode="edge")
    grad_radial = 0.5 * (edge_gas[:, 2:] - edge_gas[:, :-2])
    push = step_time * sound_sq / inner_gas
    gas_velocity = jnp.stack(
        [inner_radial[-1] - push * grad_radial, azimuth[-1, 2:-2] - push * grad_azimuth]
    )
    dust_velocity = jnp.stack([inner_radial[:-1], azimuth[:-1, 2:-2]])
    return (new_density, gas_velocity, dust_velocity)


def drag_terms(new_density, dust_velocity, stop_times, step_time, total_species):
    gas_new = new_density[-1]
    rate = step_time * gas_new[None] / stop_times[:, None, None]
    weight = new_density[:-1] / (total_species * gas_new[None]) * rate / (1.0 + rate)
    terms = jnp.stack(
        [
            jnp.sum(weight, 0),
            jnp.sum(weight * dust_velocity[0], 0),
            jnp.sum(weight * dust_velocity[1], 0),
        ]
    )
    return (rate, terms)


def coupled_gas(gas_velocity, totals):
    return (gas_velocity + totals[1:]) / (1.0 + totals[0])


def assemble(new_density, dust_velocity, gas_next, rate):
    dust_next = (dust_velocity + rate[None] * gas_next[:, None]) / (1.0 + rate[None])
    radial = jnp.concatenate([dust_next[0], gas_next[0][None]], axis=0)
    azimuth = jnp.concatenate([dust_next[1], gas_next[1][None]], axis=0)
    return jnp.stack([new_density, radial, azimuth])


def advance(wide, margin, tile_rows, stop_times, total_species):
    interior = lax.slice_in_dim(wide, margin, margin + tile_rows, axis=2)
    local_top = jnp.max(jnp.abs(interior[1]) + jnp.abs(interior[2]))
    fastest = lax.pmax(local_top, ("space", "species"))
    step_time = courant / (sound_speed + fastest)
    new_density, gas_velocity, dust_velocity = moved(wide, step_time)
    rate, terms = drag_terms(new_density, dust_velocity, stop_times, step_time, total_species)
    totals = lax.psum(terms, "species")
    gas_next = coupled_gas(gas_velocity, totals)
    return assemble(new_density, dust_velocity, gas_next, rate)


def local(dust_state, gas_state, species_bin):
    local_species = dust_state.shape[1]
    total_species = local_species * lax.axis_size("species")
    tile_rows = dust_state.shape[2]
    fluid = jnp.concatenate([dust_state, gas_state[:, None]], axis=1)
    stop_times = stop_floor * jnp.exp(
        stop_span * species_bin.astype(jnp.float32) / (total_species - 1)
    )
    for iteration in range(STEPS):
        wide = padded(fluid, (("space", 2),), 2)
        fluid = advance(wide, 2, tile_rows, stop_times, total_species)
    return (fluid[:, :local_species], fluid[:, local_species])


def solution(mesh):
    placed = (P(None, "species", "space", None), P(None, "space", None), P("species"))
    return jax.shard_map(
        local,
        mesh=mesh,
        in_specs=placed,
        out_specs=(P(None, "species", "space", None), P(None, "space", None)),
        check_vma=False,
    )
```

profile of v0, /device:TPU:1, one launch (start us, length us, event | category | flops | bytes accessed | tf_op | source)
XLA Modules:
  0.0 625.6 jit_solution(17691212085948421090)
XLA Ops:
  7.2 0.0 copy-start
  7.2 0.0 copy-start.1
  7.2 0.0 all-reduce.7.cloned.1.call-start
  7.2 1.4 pad_maximum_fusion.26
  8.7 2.2 collective-permute-start
  10.9 0.8 fusion.22
  11.7 4.1 collective-permute-start.1
  15.8 78.6 %pmax.14 = f32[]{:T(128)} all-reduce(f32[]{:T(128)} %fusion.22), channel_id=1, replica_groups=mesh['space'=8,'species'=32] {'space','species'}, use_global_device_ids=true, to_apply=%region_1.0 | all-reduce | flops 1 | bytes 8 | tf_op jit(solution)/shard_map/pmax | solution.py:100
  95.1 0.0 collective-permute-done
  95.1 0.0 collective-permute-done.1
  95.1 0.4 pad_maximum_fusion
  95.5 0.2 slice_bitcast_fusion.4
  95.8 0.0 copy-done.11
  95.8 0.1 slice.407
  95.9 0.1 slice.396
  96.0 0.6 fusion.10
  96.6 0.8 multiply_add_fusion.1
  97.4 0.4 fusion.19
  97.8 0.7 slice_bitcast_fusion.16
  98.4 1.2 broadcast_divide_fusion.1
  99.6 1.3 fusion.54
  100.9 0.8 pad_maximum_fusion.6
  101.7 0.0 all-reduce.7.cloned.1.call-update
  101.7 0.0 all-reduce.9.cloned.1.call-start
  101.8 1.4 slice_bitcast_fusion.17
  103.2 0.1 fusion.58
  103.3 1.2 fusion.52
  104.5 205.5 %all-reduce.7.cloned.1.call-done = f32[3,32,1024]{2,1,0:T(8,128)} async-done(((f32[3,32,1024]{2,1,0:T(8,128)}), f32[3,32,1024]{2,1,0:T(8,128)}) %all-reduce.7.cloned.1.call-update) | async-done | bytes 393232 | tf_op jit(solution)/shard_map/psum | solution.py:104
  310.0 0.9 fusion.42
  310.9 1.0 fusion.30
  312.0 0.2 fusion
  312.2 0.1 slice_bitcast_fusion.9
  312.3 0.8 add_reduce_fusion
  313.1 0.1 pad_maximum_fusion.24
  313.2 1.3 collective-permute-start.2
  314.5 3.9 collective-permute-start.3
  318.4 0.8 fusion.57
  319.2 76.9 %pmax.15 = f32[]{:T(128)} all-reduce(f32[]{:T(128)} %get-tuple-element.30), channel_id=1, replica_groups=mesh['space'=8,'species'=32] {'space','species'}, use_global_device_ids=true, to_apply=%region_7.8 | all-reduce | flops 1 | bytes 8 | tf_op jit(solution)/shard_map/pmax | solution.py:100
  396.8 0.0 collective-permute-done.2
  396.8 0.0 collective-permute-done.3
  396.8 0.4 pad_maximum_fusion.1
  397.2 0.2 slice_bitcast_fusion.1
  397.5 0.0 copy-done.9
  397.5 0.1 slice.436
  397.6 0.1 slice.425
  397.7 0.6 fusion.4
  398.3 0.8 multiply_add_fusion
  399.1 0.4 fusion.16
  399.5 1.2 broadcast_divide_fusion
  400.7 1.3 fusion.53
  402.0 0.8 pad_maximum_fusion.7
  402.7 0.0 all-reduce.9.cloned.1.call-update
  402.8 1.9 fusion.41
  404.7 1.4 fusion.36
  406.1 206.2 %all-reduce.9.cloned.1.call-done = f32[3,32,1024]{2,1,0:T(8,128)} async-done(((f32[3,32,1024]{2,1,0:T(8,128)}), f32[3,32,1024]{2,1,0:T(8,128)}) %all-reduce.9.cloned.1.call-update) | async-done | bytes 393232 | tf_op jit(solution)/shard_map/psum | solution.py:104
  612.4 0.9 fusion.31
  613.3 1.1 fusion.29
  614.4 1.8 fusion.1
  616.2 0.1 slice_bitcast_fusion.7
  616.3 0.1 maximum_bitcast_fusion
  616.4 0.8 maximum_bitcast_fusion.2
  617.2 0.2 pad_maximum_fusion.2
  617.4 0.1 slice.454
  617.5 1.2 copy.7
  (27 shorter events, 0.1 us)
Async XLA Ops:
  7.2 3.7 copy-start
  7.2 3.7 copy-start.1
  7.2 87.9 %copy-start.12 = (s32[4]{0:T(128)S(1)}, s32[4]{0:T(128)}, u32[]{:S(2)}) copy-start(s32[4]{0:T(128)} %param.5) | copy-start | bytes 52
  7.2 302.8 %all-reduce.7.cloned.1.call-start = ((), (), s32[]{:S(2)}) async-start(), calls=%async_computation | async-start | bytes 786432 | tf_op jit(solution)/shard_map/psum | solution.py:104
  8.7 86.4 %collective-permute-start = (f32[3,5,2,1024]{3,2,1,0:T(2,128)S(1)}, f32[3,5,2,1024]{3,2,1,0:T(2,128)S(1)}, u32[]{:S(2)}, u32[]{:S(2)}) collective-permute-start(f32[3,5,2,1024]{3,2,1,0:T(2,128)S(1)} %get-tuple-element.18), channel_id=1, source_target_pairs={{0,32},{32,64},{64,96},{96,128},{128,160},{160,192},{192,224},{224... | collective-permute-start | bytes 368648 | tf_op jit(solution)/shard_map/ppermute | solution.py:22
  11.7 83.5 %collective-permute-start.1 = (f32[3,5,2,1024]{3,2,1,0:T(2,128)S(1)}, f32[3,5,2,1024]{3,2,1,0:T(2,128)S(1)}, u32[]{:S(2)}, u32[]{:S(2)}) collective-permute-start(f32[3,5,2,1024]{3,2,1,0:T(2,128)S(1)} %get-tuple-element.19), channel_id=1, source_target_pairs={{32,0},{64,32},{96,64},{128,96},{160,128},{192,160},{224,192},{0,2... | collective-permute-start | bytes 368648 | tf_op jit(solution)/shard_map/ppermute | solution.py:25
  95.1 0.7 copy-start.10
  95.1 0.7 copy-start.11
  95.8 3.8 copy-start.2
  101.7 510.7 %all-reduce.9.cloned.1.call-start = ((), (), s32[]{:S(2)}) async-start(), calls=%async_computation.1 | async-start | bytes 786432 | tf_op jit(solution)/shard_map/psum | solution.py:104
  103.2 208.7 %copy-start.4 = (f32[4,32,1024]{2,1,0:T(8,128)S(1)}, f32[4,32,1024]{2,1,0:T(8,128)}, u32[]{:S(2)}) copy-start(f32[4,32,1024]{2,1,0:T(8,128)} %get-tuple-element.44) | copy-start | bytes 1572868
  103.2 208.8 %copy-start.5 = (f32[4,32,1024]{2,1,0:T(8,128)S(1)}, f32[4,32,1024]{2,1,0:T(8,128)}, u32[]{:S(2)}) copy-start(f32[4,32,1024]{2,1,0:T(8,128)} %get-tuple-element.46) | copy-start | bytes 1572868
  103.2 208.8 %copy-start.6 = (f32[1,4,32,1024]{3,2,1,0:T(8,128)S(1)}, f32[1,4,32,1024]{3,2,1,0:T(8,128)}, u32[]{:S(2)}) copy-start(f32[1,4,32,1024]{3,2,1,0:T(8,128)} %get-tuple-element.26) | copy-start | bytes 1572868
  103.2 208.8 %copy-start.7 = (f32[1,4,32,1024]{3,2,1,0:T(8,128)S(1)}, f32[1,4,32,1024]{3,2,1,0:T(8,128)}, u32[]{:S(2)}) copy-start(f32[1,4,32,1024]{3,2,1,0:T(8,128)} %get-tuple-element.27) | copy-start | bytes 1572868
  313.2 83.6 %collective-permute-start.2 = (f32[3,5,2,1024]{3,2,1,0:T(2,128)S(1)}, f32[3,5,2,1024]{3,2,1,0:T(2,128)S(1)}, u32[]{:S(2)}, u32[]{:S(2)}) collective-permute-start(f32[3,5,2,1024]{3,2,1,0:T(2,128)S(1)} %get-tuple-element.16), channel_id=1, source_target_pairs={{0,32},{32,64},{64,96},{96,128},{128,160},{160,192},{192,224},{224... | collective-permute-start | bytes 368648 | tf_op jit(solution)/shard_map/ppermute | solution.py:22
  314.5 82.3 %collective-permute-start.3 = (f32[3,5,2,1024]{3,2,1,0:T(2,128)S(1)}, f32[3,5,2,1024]{3,2,1,0:T(2,128)S(1)}, u32[]{:S(2)}, u32[]{:S(2)}) collective-permute-start(f32[3,5,2,1024]{3,2,1,0:T(2,128)S(1)} %get-tuple-element.17), channel_id=1, source_target_pairs={{32,0},{64,32},{96,64},{128,96},{160,128},{192,160},{224,192},{0,2... | collective-permute-start | bytes 368648 | tf_op jit(solution)/shard_map/ppermute | solution.py:25
  396.8 0.7 copy-start.8
  396.8 0.7 copy-start.9
  397.5 3.2 copy-start.3
Sparse Core Ops, SparseCore 0:
  101.8 208.1 all-reduce.6
  402.9 209.4 all-reduce.8
where the time goes:
time: 627 us; the launch traced here: 626 us
  waiting for transfers between devices  412 us (66%)
  blocking collectives  156 us (25%)
  other arithmetic  27 us (4%)
  between operations  15.8 us (3%)
  starting transfers between devices  11.5 us (2%)
    psum x2, waiting for transfers between devices, advance(): totals = lax.psum(terms, 'species')  412 us
    pmax x2, blocking collectives, advance(): fastest = lax.pmax(local_top, ('space', 'species'))  156 us
  transfers between devices with their start and end apart: 6, of which 2 were waited for; matrix products, arithmetic and copies ran while one was open for 1% of the time, Pallas kernels for 0%

commit v1 on v0

--- a/solution.py
+++ b/solution.py
@@ -94,14 +94,58 @@
     return jnp.stack([new_density, radial, azimuth])
 
 
+def xor_pairs(count, bit):
+    return [(i, i ^ bit) for i in range(count)]
+
+
+def butterfly_max(value, axes):
+    for axis in axes:
+        count = lax.axis_size(axis)
+        bit = 1
+        while bit < count:
+            value = jnp.maximum(value, lax.ppermute(value, axis, xor_pairs(count, bit)))
+            bit *= 2
+    return value
+
+
+def halving_sum(block, axis):
+    count = lax.axis_size(axis)
+    index = lax.axis_index(axis)
+    rows, lanes = block.shape
+    part = block
+    bits = []
+    bit = 1
+    while bit < count:
+        dim = 0 if part.shape[0] % 2 == 0 and part.shape[0] >= 16 else 1
+        half = part.shape[dim] // 2
+        low = lax.slice_in_dim(part, 0, half, axis=dim)
+        high = lax.slice_in_dim(part, half, None, axis=dim)
+        upper = (index // bit) % 2 == 1
+        keep = jnp.where(upper, high, low)
+        send = jnp.where(upper, low, high)
+        part = keep + lax.ppermute(send, axis, xor_pairs(count, bit))
+        bits.append((bit, dim))
+        bit *= 2
+    for bit, dim in reversed(bits):
+        other = lax.ppermute(part, axis, xor_pairs(count, bit))
+        upper = (index // bit) % 2 == 1
+        part = jnp.where(
+            upper,
+            jnp.concatenate([other, part], axis=dim),
+            jnp.concatenate([part, other], axis=dim),
+        )
+    return part
+
+
 def advance(wide, margin, tile_rows, stop_times, total_species):
     interior = lax.slice_in_dim(wide, margin, margin + tile_rows, axis=2)
     local_top = jnp.max(jnp.abs(interior[1]) + jnp.abs(interior[2]))
-    fastest = lax.pmax(local_top, ("space", "species"))
+    fastest = butterfly_max(jnp.broadcast_to(local_top, (8, 128)), ("species", "space"))[0, 0]
     step_time = courant / (sound_speed + fastest)
     new_density, gas_velocity, dust_velocity = moved(wide, step_time)
     rate, terms = drag_terms(new_density, dust_velocity, stop_times, step_time, total_species)
-    totals = lax.psum(terms, "species")
+    shape = terms.shape
+    totals = halving_sum(terms.reshape(-1, shape[-1]), "species").reshape(shape)
     gas_next = coupled_gas(gas_velocity, totals)
     return assemble(new_density, dust_velocity, gas_next, rate)
 

time: 627 us -> 204 us (0.33)
  waiting for transfers between devices: 412 us -> 63.9 us
  blocking collectives: 156 us -> 0 us
  starting transfers between devices: 11.5 us -> 106 us
  between operations: 15.8 us -> 2.69 us
    psum x2 -> x0, waiting for transfers between devices: 412 us -> none  [advance(): totals = lax.psum(terms, 'species')]
    pmax x2 -> x0, blocking collectives: 156 us -> none  [advance(): fastest = lax.pmax(local_top, ('space', 'species'))]
    ppermute x0 -> x36, starting transfers between devices: none -> 95.9 us  [the longest x10 34.3 us: halving_sum(): other = lax.ppermute(part, axis, xor_pairs(count, bit))]
    ppermute x0 -> x36, waiting for transfers between devices: none -> 63.9 us  [the longest x16 26.3 us: butterfly_max(): value = jnp.maximum(value, lax.ppermute(value, axis, xor_pairs(count, bit)))]
  transfers between devices with their start and end apart: 6 -> 40, of which waited for: 2 -> 33; matrix products, arithmetic and copies ran while one was open for 1% -> 2% of each run, Pallas kernels for 0% -> 0%
where the time goes in v1:
time: 204 us; the launch traced here: 203 us
  starting transfers between devices  106 us (52%)
  waiting for transfers between devices  63.9 us (31%)
  other arithmetic  23.3 us (11%)
  local copies, waits for them, and re-layouts  6.99 us (3%)
  between operations  2.69 us (1%)
    ppermute x10, starting transfers between devices, halving_sum(): other = lax.ppermute(part, axis, xor_pairs(count, bit))  34.3 us
    ppermute x10, starting transfers between devices, halving_sum(): part = keep + lax.ppermute(send, axis, xor_pairs(count, bit))  33.2 us
    ppermute x16, starting transfers between devices, butterfly_max(): value = jnp.maximum(value, lax.ppermute(value, axis, xor_pairs(count, bit)))  28.4 us
    ppermute x16, waiting for transfers between devices, butterfly_max(): value = jnp.maximum(value, lax.ppermute(value, axis, xor_pairs(count, bit)))  26.3 us
    ppermute x10, waiting for transfers between devices, halving_sum(): part = keep + lax.ppermute(send, axis, xor_pairs(count, bit))  20.1 us
    ppermute x10, waiting for transfers between devices, halving_sum(): other = lax.ppermute(part, axis, xor_pairs(count, bit))  17.4 us
    ppermute x2, starting transfers between devices, padded(): lax.ppermute(lax.slice_in_dim(block, 0, width, axis=dim), axis, backward)  9.75 us
  transfers between devices with their start and end apart: 40, of which 33 were waited for; matrix products, arithmetic and copies ran while one was open for 2% of the time, Pallas kernels for 0%

profile of v1, /device:TPU:1, one launch (start us, length us, event | category | flops | bytes accessed | tf_op | source)
XLA Modules:
  0.0 203.1 jit_solution(13232477451878937885)
XLA Ops:
  0.7 2.2 %fusion.22 = f32[]{:T(128)} fusion(f32[3,1,32,1024]{3,2,1,0:T(8,128)} %bitcast.97, f32[3,4,32,1024]{3,2,1,0:T(8,128)} %param.3), kind=kLoop, calls=%fused_computation.50 | loop fusion | flops 983039 | bytes 1966084 | tf_op jit(solution)/shard_map/reduce_max | solution.py:142
  3.6 3.3 %collective-permute-start.2 = (f32[8,128]{1,0:T(8,128)S(1)}, f32[8,128]{1,0:T(8,128)S(1)}, u32[]{:S(2)}, u32[]{:S(2)}) collective-permute-start(f32[8,128]{1,0:T(8,128)S(1)} %broadcast_in_dim.7), channel_id=1, source_target_pairs={{0,1},{1,0},{2,3},{3,2},{4,5},{5,4},{6,7},{7,6},{8,9},{9,8},{10,11... | collective-permute-start | bytes 12296 | tf_op jit(solution)/shard_map/ppermute | solution.py:106
  8.5 2.4 %collective-permute-done.3 = f32[8,128]{1,0:T(8,128)S(1)} collective-permute-done((f32[8,128]{1,0:T(8,128)S(1)}, f32[8,128]{1,0:T(8,128)S(1)}, u32[]{:S(2)}, u32[]{:S(2)}) %collective-permute-start.3) | collective-permute-done | bytes 4128 | tf_op jit(solution)/shard_map/ppermute | solution.py:106
  11.7 2.4 %collective-permute-done.4 = f32[8,128]{1,0:T(8,128)S(1)} collective-permute-done((f32[8,128]{1,0:T(8,128)S(1)}, f32[8,128]{1,0:T(8,128)S(1)}, u32[]{:S(2)}, u32[]{:S(2)}) %collective-permute-start.4) | collective-permute-done | bytes 4128 | tf_op jit(solution)/shard_map/ppermute | solution.py:106
  14.1 1.4 collective-permute-start.5
  15.5 1.9 collective-permute-done.5
  17.5 5.2 %collective-permute-start.6 = (f32[8,128]{1,0:T(8,128)S(1)}, f32[8,128]{1,0:T(8,128)S(1)}, u32[]{:S(2)}, u32[]{:S(2)}) collective-permute-start(f32[8,128]{1,0:T(8,128)S(1)} %max.63), channel_id=1, source_target_pairs={{0,16},{1,17},{2,18},{3,19},{4,20},{5,21},{6,22},{7,23},{8,24},{9,... | collective-permute-start | bytes 12296 | tf_op jit(solution)/shard_map/ppermute | solution.py:106
  22.6 1.2 collective-permute-done.6
  23.8 1.1 collective-permute-start.7
  24.9 1.7 collective-permute-done.7
  26.6 2.7 %collective-permute-start.8 = (f32[8,128]{1,0:T(8,128)S(1)}, f32[8,128]{1,0:T(8,128)S(1)}, u32[]{:S(2)}, u32[]{:S(2)}) collective-permute-start(f32[8,128]{1,0:T(8,128)S(1)} %max.65), channel_id=1, source_target_pairs={{0,64},{32,96},{64,0},{96,32},{128,192},{160,224},{192,128},{224,1... | collective-permute-start | bytes 12296 | tf_op jit(solution)/shard_map/ppermute | solution.py:106
  29.3 1.0 pad_maximum_fusion.26
  30.8 4.7 %collective-permute-start.1 = (f32[3,5,2,1024]{3,2,1,0:T(2,128)S(1)}, f32[3,5,2,1024]{3,2,1,0:T(2,128)S(1)}, u32[]{:S(2)}, u32[]{:S(2)}) collective-permute-start(f32[3,5,2,1024]{3,2,1,0:T(2,128)S(1)} %get-tuple-element.19), channel_id=1, source_target_pairs={{32,0},{64,32},{96,64},{128,96},{160,128},{192,160},{224,192},{0,2... | collective-permute-start | bytes 368648 | tf_op jit(solution)/shard_map/ppermute | solution.py:25
  35.5 2.7 %collective-permute-start.9 = (f32[8,128]{1,0:T(8,128)S(1)}, f32[8,128]{1,0:T(8,128)S(1)}, u32[]{:S(2)}, u32[]{:S(2)}) collective-permute-start(f32[8,128]{1,0:T(8,128)S(1)} %max.66), channel_id=1, source_target_pairs={{0,128},{32,160},{64,192},{96,224},{128,0},{160,32},{192,64},{224,... | collective-permute-start | bytes 12296 | tf_op jit(solution)/shard_map/ppermute | solution.py:106
  38.3 2.3 %collective-permute-done.9 = f32[8,128]{1,0:T(8,128)S(1)} collective-permute-done((f32[8,128]{1,0:T(8,128)S(1)}, f32[8,128]{1,0:T(8,128)S(1)}, u32[]{:S(2)}, u32[]{:S(2)}) %collective-permute-start.9) | collective-permute-done | bytes 4128 | tf_op jit(solution)/shard_map/ppermute | solution.py:106
  44.5 1.2 broadcast_divide_fusion.1
  45.7 1.2 fusion.52
  48.4 7.2 %collective-permute-start.10 = (f32[48,1024]{1,0:T(8,128)}, f32[48,1024]{1,0:T(8,128)}, u32[]{:S(2)}, u32[]{:S(2)}) collective-permute-start(f32[48,1024]{1,0:T(8,128)} %slice_select_fusion.1), channel_id=1, source_target_pairs={{0,1},{1,0},{2,3},{3,2},{4,5},{5,4},{6,7},{7,6},{8,9},{9,8},{10,11... | collective-permute-start | bytes 589832 | tf_op jit(solution)/shard_map/ppermute | solution.py:126
  55.6 1.4 collective-permute-done.10
  57.0 1.1 select_add_fusion.1
  59.4 3.7 %collective-permute-done.11 = f32[24,1024]{1,0:T(8,128)} collective-permute-done((f32[24,1024]{1,0:T(8,128)S(1)}, f32[24,1024]{1,0:T(8,128)}, u32[]{:S(2)}, u32[]{:S(2)}) %collective-permute-start.11) | collective-permute-done | bytes 98336 | tf_op jit(solution)/shard_map/ppermute | solution.py:126
  63.1 1.0 select_add_fusion.3
  65.5 2.7 %collective-permute-done.12 = f32[12,1024]{1,0:T(8,128)} collective-permute-done((f32[12,1024]{1,0:T(8,128)}, f32[12,1024]{1,0:T(8,128)}, u32[]{:S(2)}, u32[]{:S(2)}) %collective-permute-start.12) | collective-permute-done | bytes 49184 | tf_op jit(solution)/shard_map/ppermute | solution.py:126
  69.6 1.9 collective-permute-start.13
  71.5 1.8 collective-permute-done.13
  74.1 5.9 %collective-permute-start.14 = (f32[12,256]{1,0:T(8,128)S(1)}, f32[12,256]{1,0:T(8,128)S(1)}, u32[]{:S(2)}, u32[]{:S(2)}) collective-permute-start(f32[12,256]{1,0:T(8,128)S(1)} %slice_select_fusion.9), channel_id=1, source_target_pairs={{0,16},{1,17},{2,18},{3,19},{4,20},{5,21},{6,22},{7,23},{8,24},{9,... | collective-permute-start | bytes 36872 | tf_op jit(solution)/shard_map/ppermute | solution.py:126
  80.0 1.1 collective-permute-done.14
  81.2 5.4 %collective-permute-start.15 = (f32[12,256]{1,0:T(8,128)S(1)}, f32[12,256]{1,0:T(8,128)S(1)}, u32[]{:S(2)}, u32[]{:S(2)}) collective-permute-start(f32[12,256]{1,0:T(8,128)S(1)} %select_add_fusion.9), channel_id=1, source_target_pairs={{0,16},{1,17},{2,18},{3,19},{4,20},{5,21},{6,22},{7,23},{8,24},{9,... | collective-permute-start | bytes 36872 | tf_op jit(solution)/shard_map/ppermute | solution.py:130
  86.5 1.1 collective-permute-done.15
  87.7 1.6 collective-permute-start.16
  89.3 2.3 %collective-permute-done.16 = f32[12,512]{1,0:T(8,128)S(1)} collective-permute-done((f32[12,512]{1,0:T(8,128)S(1)}, f32[12,512]{1,0:T(8,128)S(1)}, u32[]{:S(2)}, u32[]{:S(2)}) %collective-permute-start.16) | collective-permute-done | bytes 24608 | tf_op jit(solution)/shard_map/ppermute | solution.py:130
  93.3 1.7 collective-permute-done.17
  95.6 3.0 %collective-permute-done.18 = f32[24,1024]{1,0:T(8,128)S(1)} collective-permute-done((f32[24,1024]{1,0:T(8,128)S(1)}, f32[24,1024]{1,0:T(8,128)S(1)}, u32[]{:S(2)}, u32[]{:S(2)}) %collective-permute-start.18) | collective-permute-done | bytes 98336 | tf_op jit(solution)/shard_map/ppermute | solution.py:130
  98.6 8.6 %collective-permute-start.19 = (f32[48,1024]{1,0:T(8,128)S(1)}, f32[48,1024]{1,0:T(8,128)S(1)}, u32[]{:S(2)}, u32[]{:S(2)}) collective-permute-start(f32[48,1024]{1,0:T(8,128)S(1)} %maximum_select_fusion.2), channel_id=1, source_target_pairs={{0,1},{1,0},{2,3},{3,2},{4,5},{5,4},{6,7},{7,6},{8,9},{9,8},{10,11... | collective-permute-start | bytes 589832 | tf_op jit(solution)/shard_map/ppermute | solution.py:130
  107.2 1.1 fusion.50
  112.9 5.1 %collective-permute-start.21 = (f32[3,5,2,1024]{3,2,1,0:T(2,128)S(1)}, f32[3,5,2,1024]{3,2,1,0:T(2,128)S(1)}, u32[]{:S(2)}, u32[]{:S(2)}) collective-permute-start(f32[3,5,2,1024]{3,2,1,0:T(2,128)S(1)} %get-tuple-element.17), channel_id=1, source_target_pairs={{32,0},{64,32},{96,64},{128,96},{160,128},{192,160},{224,192},{0,2... | collective-permute-start | bytes 368648 | tf_op jit(solution)/shard_map/ppermute | solution.py:25
  119.4 2.0 collective-permute-done.24
  121.5 1.9 collective-permute-start.25
  123.4 1.5 collective-permute-done.25
  124.8 5.7 %collective-permute-start.26 = (f32[8,128]{1,0:T(8,128)S(1)}, f32[8,128]{1,0:T(8,128)S(1)}, u32[]{:S(2)}, u32[]{:S(2)}) collective-permute-start(f32[8,128]{1,0:T(8,128)S(1)} %max.73), channel_id=1, source_target_pairs={{0,16},{1,17},{2,18},{3,19},{4,20},{5,21},{6,22},{7,23},{8,24},{9,... | collective-permute-start | bytes 12296 | tf_op jit(solution)/shard_map/ppermute | solution.py:106
  130.5 1.0 collective-permute-done.26
  131.5 2.7 %collective-permute-done.27 = f32[8,128]{1,0:T(8,128)S(1)} collective-permute-done((f32[8,128]{1,0:T(8,128)S(1)}, f32[8,128]{1,0:T(8,128)S(1)}, u32[]{:S(2)}, u32[]{:S(2)}) %collective-permute-start.27) | collective-permute-done | bytes 4128 | tf_op jit(solution)/shard_map/ppermute | solution.py:106
  134.3 4.0 %collective-permute-done.28 = f32[8,128]{1,0:T(8,128)S(1)} collective-permute-done((f32[8,128]{1,0:T(8,128)S(1)}, f32[8,128]{1,0:T(8,128)S(1)}, u32[]{:S(2)}, u32[]{:S(2)}) %collective-permute-start.28) | collective-permute-done | bytes 4128 | tf_op jit(solution)/shard_map/ppermute | solution.py:106
  138.2 2.5 %collective-permute-start.29 = (f32[8,128]{1,0:T(8,128)S(1)}, f32[8,128]{1,0:T(8,128)S(1)}, u32[]{:S(2)}, u32[]{:S(2)}) collective-permute-start(f32[8,128]{1,0:T(8,128)S(1)} %max.76), channel_id=1, source_target_pairs={{0,128},{32,160},{64,192},{96,224},{128,0},{160,32},{192,64},{224,... | collective-permute-start | bytes 12296 | tf_op jit(solution)/shard_map/ppermute | solution.py:106
  140.7 1.5 collective-permute-done.29
  146.7 7.3 %collective-permute-start.30 = (f32[48,1024]{1,0:T(8,128)S(1)}, f32[48,1024]{1,0:T(8,128)S(1)}, u32[]{:S(2)}, u32[]{:S(2)}) collective-permute-start(f32[48,1024]{1,0:T(8,128)S(1)} %slice_select_fusion), channel_id=1, source_target_pairs={{0,1},{1,0},{2,3},{3,2},{4,5},{5,4},{6,7},{7,6},{8,9},{9,8},{10,11... | collective-permute-start | bytes 589832 | tf_op jit(solution)/shard_map/ppermute | solution.py:126
  153.9 1.1 collective-permute-done.30
  155.1 1.1 collective-permute-start.31
  156.2 3.0 %collective-permute-done.31 = f32[24,1024]{1,0:T(8,128)S(1)} collective-permute-done((f32[24,1024]{1,0:T(8,128)S(1)}, f32[24,1024]{1,0:T(8,128)S(1)}, u32[]{:S(2)}, u32[]{:S(2)}) %collective-permute-start.31) | collective-permute-done | bytes 98336 | tf_op jit(solution)/shard_map/ppermute | solution.py:126
  160.0 2.4 %collective-permute-done.32 = f32[12,1024]{1,0:T(8,128)S(1)} collective-permute-done((f32[12,1024]{1,0:T(8,128)S(1)}, f32[12,1024]{1,0:T(8,128)S(1)}, u32[]{:S(2)}, u32[]{:S(2)}) %collective-permute-start.32) | collective-permute-done | bytes 49184 | tf_op jit(solution)/shard_map/ppermute | solution.py:126
  162.4 2.0 collective-permute-start.33
  164.4 1.8 collective-permute-done.33
  166.2 5.7 %collective-permute-start.34 = (f32[12,256]{1,0:T(8,128)S(1)}, f32[12,256]{1,0:T(8,128)S(1)}, u32[]{:S(2)}, u32[]{:S(2)}) collective-permute-start(f32[12,256]{1,0:T(8,128)S(1)} %slice_select_fusion.8), channel_id=1, source_target_pairs={{0,16},{1,17},{2,18},{3,19},{4,20},{5,21},{6,22},{7,23},{8,24},{9,... | collective-permute-start | bytes 36872 | tf_op jit(solution)/shard_map/ppermute | solution.py:126
  172.0 1.2 collective-permute-done.34
  173.2 5.3 %collective-permute-start.35 = (f32[12,256]{1,0:T(8,128)S(1)}, f32[12,256]{1,0:T(8,128)S(1)}, u32[]{:S(2)}, u32[]{:S(2)}) collective-permute-start(f32[12,256]{1,0:T(8,128)S(1)} %select_add_fusion.8), channel_id=1, source_target_pairs={{0,16},{1,17},{2,18},{3,19},{4,20},{5,21},{6,22},{7,23},{8,24},{9,... | collective-permute-start | bytes 36872 | tf_op jit(solution)/shard_map/ppermute | solution.py:130
  178.5 1.2 collective-permute-done.35
  179.7 1.5 collective-permute-start.36
  181.2 2.4 %collective-permute-done.36 = f32[12,512]{1,0:T(8,128)S(1)} collective-permute-done((f32[12,512]{1,0:T(8,128)S(1)}, f32[12,512]{1,0:T(8,128)S(1)}, u32[]{:S(2)}, u32[]{:S(2)}) %collective-permute-start.36) | collective-permute-done | bytes 24608 | tf_op jit(solution)/shard_map/ppermute | solution.py:130
  184.5 2.4 %collective-permute-done.37 = f32[12,1024]{1,0:T(8,128)S(1)} collective-permute-done((f32[12,1024]{1,0:T(8,128)S(1)}, f32[12,1024]{1,0:T(8,128)S(1)}, u32[]{:S(2)}, u32[]{:S(2)}) %collective-permute-start.37) | collective-permute-done | bytes 49184 | tf_op jit(solution)/shard_map/ppermute | solution.py:130
  186.9 1.1 collective-permute-start.38
  188.2 2.3 %collective-permute-done.38 = f32[24,1024]{1,0:T(8,128)S(1)} collective-permute-done((f32[24,1024]{1,0:T(8,128)S(1)}, f32[24,1024]{1,0:T(8,128)S(1)}, u32[]{:S(2)}, u32[]{:S(2)}) %collective-permute-start.38) | collective-permute-done | bytes 98336 | tf_op jit(solution)/shard_map/ppermute | solution.py:130
  190.5 8.6 %collective-permute-start.39 = (f32[48,1024]{1,0:T(8,128)S(1)}, f32[48,1024]{1,0:T(8,128)S(1)}, u32[]{:S(2)}, u32[]{:S(2)}) collective-permute-start(f32[48,1024]{1,0:T(8,128)S(1)} %maximum_select_fusion.3), channel_id=1, source_target_pairs={{0,1},{1,0},{2,3},{3,2},{4,5},{5,4},{6,7},{7,6},{8,9},{9,8},{10,11... | collective-permute-start | bytes 589832 | tf_op jit(solution)/shard_map/ppermute | solution.py:130
  199.2 1.0 collective-permute-done.39
  201.9 1.2 copy.7
  (143 shorter events, 28.5 us)
Async XLA Ops:
  0.6 41.2 %copy-start.1 = (f32[3,32,1024]{2,1,0:T(8,128)S(1)}, f32[3,32,1024]{2,1,0:T(8,128)}, u32[]{:S(2)}) copy-start(f32[3,32,1024]{2,1,0:T(8,128)} %param.4) | copy-start | bytes 1179652
  0.6 28.7 %copy-start = (f32[3,4,32,1024]{3,2,1,0:T(8,128)S(1)}, f32[3,4,32,1024]{3,2,1,0:T(8,128)}, u32[]{:S(2)}) copy-start(f32[3,4,32,1024]{3,2,1,0:T(8,128)} %param.3) | copy-start | bytes 4718596
  0.7 37.6 %copy-start.12 = (s32[4]{0:T(128)S(1)}, s32[4]{0:T(128)}, u32[]{:S(2)}) copy-start(s32[4]{0:T(128)} %param.5) | copy-start | bytes 52
  3.6 4.2 %collective-permute-start.2 = (f32[8,128]{1,0:T(8,128)S(1)}, f32[8,128]{1,0:T(8,128)S(1)}, u32[]{:S(2)}, u32[]{:S(2)}) collective-permute-start(f32[8,128]{1,0:T(8,128)S(1)} %broadcast_in_dim.7), channel_id=1, source_target_pairs={{0,1},{1,0},{2,3},{3,2},{4,5},{5,4},{6,7},{7,6},{8,9},{9,8},{10,11... | collective-permute-start | bytes 12296 | tf_op jit(solution)/shard_map/ppermute | solution.py:106
  8.4 2.5 %collective-permute-start.3 = (f32[8,128]{1,0:T(8,128)S(1)}, f32[8,128]{1,0:T(8,128)S(1)}, u32[]{:S(2)}, u32[]{:S(2)}) collective-permute-start(f32[8,128]{1,0:T(8,128)S(1)} %broadcast_maximum_fusion.1), channel_id=1, source_target_pairs={{0,2},{1,3},{2,0},{3,1},{4,6},{5,7},{6,4},{7,5},{8,10},{9,11},{10,... | collective-permute-start | bytes 12296 | tf_op jit(solution)/shard_map/ppermute | solution.py:106
  11.6 2.5 %collective-permute-start.4 = (f32[8,128]{1,0:T(8,128)S(1)}, f32[8,128]{1,0:T(8,128)S(1)}, u32[]{:S(2)}, u32[]{:S(2)}) collective-permute-start(f32[8,128]{1,0:T(8,128)S(1)} %fusion.58), channel_id=1, source_target_pairs={{0,4},{1,5},{2,6},{3,7},{4,0},{5,1},{6,2},{7,3},{8,12},{9,13},{10,... | collective-permute-start | bytes 12296 | tf_op jit(solution)/shard_map/ppermute | solution.py:106
  14.1 3.4 %collective-permute-start.5 = (f32[8,128]{1,0:T(8,128)S(1)}, f32[8,128]{1,0:T(8,128)S(1)}, u32[]{:S(2)}, u32[]{:S(2)}) collective-permute-start(f32[8,128]{1,0:T(8,128)S(1)} %max.62), channel_id=1, source_target_pairs={{0,8},{1,9},{2,10},{3,11},{4,12},{5,13},{6,14},{7,15},{8,0},{9,1},... | collective-permute-start | bytes 12296 | tf_op jit(solution)/shard_map/ppermute | solution.py:106
  17.5 6.4 %collective-permute-start.6 = (f32[8,128]{1,0:T(8,128)S(1)}, f32[8,128]{1,0:T(8,128)S(1)}, u32[]{:S(2)}, u32[]{:S(2)}) collective-permute-start(f32[8,128]{1,0:T(8,128)S(1)} %max.63), channel_id=1, source_target_pairs={{0,16},{1,17},{2,18},{3,19},{4,20},{5,21},{6,22},{7,23},{8,24},{9,... | collective-permute-start | bytes 12296 | tf_op jit(solution)/shard_map/ppermute | solution.py:106
  23.8 2.8 %collective-permute-start.7 = (f32[8,128]{1,0:T(8,128)S(1)}, f32[8,128]{1,0:T(8,128)S(1)}, u32[]{:S(2)}, u32[]{:S(2)}) collective-permute-start(f32[8,128]{1,0:T(8,128)S(1)} %max.64), channel_id=1, source_target_pairs={{0,32},{32,0},{64,96},{96,64},{128,160},{160,128},{192,224},{224,1... | collective-permute-start | bytes 12296 | tf_op jit(solution)/shard_map/ppermute | solution.py:106
  26.6 8.9 %collective-permute-start.8 = (f32[8,128]{1,0:T(8,128)S(1)}, f32[8,128]{1,0:T(8,128)S(1)}, u32[]{:S(2)}, u32[]{:S(2)}) collective-permute-start(f32[8,128]{1,0:T(8,128)S(1)} %max.65), channel_id=1, source_target_pairs={{0,64},{32,96},{64,0},{96,32},{128,192},{160,224},{192,128},{224,1... | collective-permute-start | bytes 12296 | tf_op jit(solution)/shard_map/ppermute | solution.py:106
  30.4 11.4 %collective-permute-start = (f32[3,5,2,1024]{3,2,1,0:T(2,128)S(1)}, f32[3,5,2,1024]{3,2,1,0:T(2,128)S(1)}, u32[]{:S(2)}, u32[]{:S(2)}) collective-permute-start(f32[3,5,2,1024]{3,2,1,0:T(2,128)S(1)} %get-tuple-element.18), channel_id=1, source_target_pairs={{0,32},{32,64},{64,96},{96,128},{128,160},{160,192},{192,224},{224... | collective-permute-start | bytes 368648 | tf_op jit(solution)/shard_map/ppermute | solution.py:22
  30.8 11.0 %collective-permute-start.1 = (f32[3,5,2,1024]{3,2,1,0:T(2,128)S(1)}, f32[3,5,2,1024]{3,2,1,0:T(2,128)S(1)}, u32[]{:S(2)}, u32[]{:S(2)}) collective-permute-start(f32[3,5,2,1024]{3,2,1,0:T(2,128)S(1)} %get-tuple-element.19), channel_id=1, source_target_pairs={{32,0},{64,32},{96,64},{128,96},{160,128},{192,160},{224,192},{0,2... | collective-permute-start | bytes 368648 | tf_op jit(solution)/shard_map/ppermute | solution.py:25
  35.5 5.0 %collective-permute-start.9 = (f32[8,128]{1,0:T(8,128)S(1)}, f32[8,128]{1,0:T(8,128)S(1)}, u32[]{:S(2)}, u32[]{:S(2)}) collective-permute-start(f32[8,128]{1,0:T(8,128)S(1)} %max.66), channel_id=1, source_target_pairs={{0,128},{32,160},{64,192},{96,224},{128,0},{160,32},{192,64},{224,... | collective-permute-start | bytes 12296 | tf_op jit(solution)/shard_map/ppermute | solution.py:106
  41.8 0.7 copy-start.10
  41.8 0.7 copy-start.11
  42.5 3.2 %copy-start.2 = (f32[5,36,1024]{2,1,0:T(8,128)}, f32[5,36,1024]{2,1,0:T(8,128)S(1)}, u32[]{:S(2)}) copy-start(f32[5,36,1024]{2,1,0:T(8,128)S(1)} %get-tuple-element.14) | copy-start | bytes 2211844
  46.9 0.7 copy-start.3
  48.4 8.6 %collective-permute-start.10 = (f32[48,1024]{1,0:T(8,128)}, f32[48,1024]{1,0:T(8,128)}, u32[]{:S(2)}, u32[]{:S(2)}) collective-permute-start(f32[48,1024]{1,0:T(8,128)} %slice_select_fusion.1), channel_id=1, source_target_pairs={{0,1},{1,0},{2,3},{3,2},{4,5},{5,4},{6,7},{7,6},{8,9},{9,8},{10,11... | collective-permute-start | bytes 589832 | tf_op jit(solution)/shard_map/ppermute | solution.py:126
  58.2 0.7 copy-start.8
  58.9 4.2 %collective-permute-start.11 = (f32[24,1024]{1,0:T(8,128)S(1)}, f32[24,1024]{1,0:T(8,128)}, u32[]{:S(2)}, u32[]{:S(2)}) collective-permute-start(f32[24,1024]{1,0:T(8,128)S(1)} %slice_select_fusion.3), channel_id=1, source_target_pairs={{0,2},{1,3},{2,0},{3,1},{4,6},{5,7},{6,4},{7,5},{8,10},{9,11},{10,... | collective-permute-start | bytes 294920 | tf_op jit(solution)/shard_map/ppermute | solution.py:126
  64.7 3.4 %collective-permute-start.12 = (f32[12,1024]{1,0:T(8,128)}, f32[12,1024]{1,0:T(8,128)}, u32[]{:S(2)}, u32[]{:S(2)}) collective-permute-start(f32[12,1024]{1,0:T(8,128)} %slice_select_fusion.5), channel_id=1, source_target_pairs={{0,4},{1,5},{2,6},{3,7},{4,0},{5,1},{6,2},{7,3},{8,12},{9,13},{10,... | collective-permute-start | bytes 147464 | tf_op jit(solution)/shard_map/ppermute | solution.py:126
  69.0 0.6 copy-start.9
  69.6 3.7 %collective-permute-start.13 = (f32[12,512]{1,0:T(8,128)S(1)}, f32[12,512]{1,0:T(8,128)S(1)}, u32[]{:S(2)}, u32[]{:S(2)}) collective-permute-start(f32[12,512]{1,0:T(8,128)S(1)} %slice_select_fusion.7), channel_id=1, source_target_pairs={{0,8},{1,9},{2,10},{3,11},{4,12},{5,13},{6,14},{7,15},{8,0},{9,1},... | collective-permute-start | bytes 73736 | tf_op jit(solution)/shard_map/ppermute | solution.py:126
  74.1 7.0 %collective-permute-start.14 = (f32[12,256]{1,0:T(8,128)S(1)}, f32[12,256]{1,0:T(8,128)S(1)}, u32[]{:S(2)}, u32[]{:S(2)}) collective-permute-start(f32[12,256]{1,0:T(8,128)S(1)} %slice_select_fusion.9), channel_id=1, source_target_pairs={{0,16},{1,17},{2,18},{3,19},{4,20},{5,21},{6,22},{7,23},{8,24},{9,... | collective-permute-start | bytes 36872 | tf_op jit(solution)/shard_map/ppermute | solution.py:126
  81.2 6.5 %collective-permute-start.15 = (f32[12,256]{1,0:T(8,128)S(1)}, f32[12,256]{1,0:T(8,128)S(1)}, u32[]{:S(2)}, u32[]{:S(2)}) collective-permute-start(f32[12,256]{1,0:T(8,128)S(1)} %select_add_fusion.9), channel_id=1, source_target_pairs={{0,16},{1,17},{2,18},{3,19},{4,20},{5,21},{6,22},{7,23},{8,24},{9,... | collective-permute-start | bytes 36872 | tf_op jit(solution)/shard_map/ppermute | solution.py:130
  87.7 4.0 %collective-permute-start.16 = (f32[12,512]{1,0:T(8,128)S(1)}, f32[12,512]{1,0:T(8,128)S(1)}, u32[]{:S(2)}, u32[]{:S(2)}) collective-permute-start(f32[12,512]{1,0:T(8,128)S(1)} %maximum_select_fusion.8), channel_id=1, source_target_pairs={{0,8},{1,9},{2,10},{3,11},{4,12},{5,13},{6,14},{7,15},{8,0},{9,1},... | collective-permute-start | bytes 73736 | tf_op jit(solution)/shard_map/ppermute | solution.py:130
  91.6 3.4 %collective-permute-start.17 = (f32[12,1024]{1,0:T(8,128)S(1)}, f32[12,1024]{1,0:T(8,128)S(1)}, u32[]{:S(2)}, u32[]{:S(2)}) collective-permute-start(f32[12,1024]{1,0:T(8,128)S(1)} %maximum_select_fusion.6), channel_id=1, source_target_pairs={{0,4},{1,5},{2,6},{3,7},{4,0},{5,1},{6,2},{7,3},{8,12},{9,13},{10,... | collective-permute-start | bytes 147464 | tf_op jit(solution)/shard_map/ppermute | solution.py:130
  93.3 15.2 %copy-start.4 = (f32[4,32,1024]{2,1,0:T(8,128)S(1)}, f32[4,32,1024]{2,1,0:T(8,128)}, u32[]{:S(2)}) copy-start(f32[4,32,1024]{2,1,0:T(8,128)} %get-tuple-element.44) | copy-start | bytes 1572868
  93.3 15.2 %copy-start.5 = (f32[4,32,1024]{2,1,0:T(8,128)S(1)}, f32[4,32,1024]{2,1,0:T(8,128)}, u32[]{:S(2)}) copy-start(f32[4,32,1024]{2,1,0:T(8,128)} %get-tuple-element.46) | copy-start | bytes 1572868
  93.3 15.2 %copy-start.6 = (f32[1,4,32,1024]{3,2,1,0:T(8,128)S(1)}, f32[1,4,32,1024]{3,2,1,0:T(8,128)}, u32[]{:S(2)}) copy-start(f32[1,4,32,1024]{3,2,1,0:T(8,128)} %get-tuple-element.26) | copy-start | bytes 1572868
  93.3 15.2 %copy-start.7 = (f32[1,4,32,1024]{3,2,1,0:T(8,128)S(1)}, f32[1,4,32,1024]{3,2,1,0:T(8,128)}, u32[]{:S(2)}) copy-start(f32[1,4,32,1024]{3,2,1,0:T(8,128)} %get-tuple-element.27) | copy-start | bytes 1572868
  95.0 3.6 %collective-permute-start.18 = (f32[24,1024]{1,0:T(8,128)S(1)}, f32[24,1024]{1,0:T(8,128)S(1)}, u32[]{:S(2)}, u32[]{:S(2)}) collective-permute-start(f32[24,1024]{1,0:T(8,128)S(1)} %maximum_select_fusion.4), channel_id=1, source_target_pairs={{0,2},{1,3},{2,0},{3,1},{4,6},{5,7},{6,4},{7,5},{8,10},{9,11},{10,... | collective-permute-start | bytes 294920 | tf_op jit(solution)/shard_map/ppermute | solution.py:130
  98.6 9.7 %collective-permute-start.19 = (f32[48,1024]{1,0:T(8,128)S(1)}, f32[48,1024]{1,0:T(8,128)S(1)}, u32[]{:S(2)}, u32[]{:S(2)}) collective-permute-start(f32[48,1024]{1,0:T(8,128)S(1)} %maximum_select_fusion.2), channel_id=1, source_target_pairs={{0,1},{1,0},{2,3},{3,2},{4,5},{5,4},{6,7},{7,6},{8,9},{9,8},{10,11... | collective-permute-start | bytes 589832 | tf_op jit(solution)/shard_map/ppermute | solution.py:130
  110.3 1.3 collective-permute-start.22
  112.2 5.8 %collective-permute-start.23 = (f32[8,128]{1,0:T(8,128)S(1)}, f32[8,128]{1,0:T(8,128)S(1)}, u32[]{:S(2)}, u32[]{:S(2)}) collective-permute-start(f32[8,128]{1,0:T(8,128)S(1)} %broadcast_maximum_fusion), channel_id=1, source_target_pairs={{0,2},{1,3},{2,0},{3,1},{4,6},{5,7},{6,4},{7,5},{8,10},{9,11},{10,... | collective-permute-start | bytes 12296 | tf_op jit(solution)/shard_map/ppermute | solution.py:106
  112.8 30.6 %collective-permute-start.20 = (f32[3,5,2,1024]{3,2,1,0:T(2,128)S(1)}, f32[3,5,2,1024]{3,2,1,0:T(2,128)S(1)}, u32[]{:S(2)}, u32[]{:S(2)}) collective-permute-start(f32[3,5,2,1024]{3,2,1,0:T(2,128)S(1)} %get-tuple-element.16), channel_id=1, source_target_pairs={{0,32},{32,64},{64,96},{96,128},{128,160},{160,192},{192,224},{224... | collective-permute-start | bytes 368648 | tf_op jit(solution)/shard_map/ppermute | solution.py:22
  112.9 30.5 %collective-permute-start.21 = (f32[3,5,2,1024]{3,2,1,0:T(2,128)S(1)}, f32[3,5,2,1024]{3,2,1,0:T(2,128)S(1)}, u32[]{:S(2)}, u32[]{:S(2)}) collective-permute-start(f32[3,5,2,1024]{3,2,1,0:T(2,128)S(1)} %get-tuple-element.17), channel_id=1, source_target_pairs={{32,0},{64,32},{96,64},{128,96},{160,128},{192,160},{224,192},{0,2... | collective-permute-start | bytes 368648 | tf_op jit(solution)/shard_map/ppermute | solution.py:25
  118.6 2.8 %collective-permute-start.24 = (f32[8,128]{1,0:T(8,128)S(1)}, f32[8,128]{1,0:T(8,128)S(1)}, u32[]{:S(2)}, u32[]{:S(2)}) collective-permute-start(f32[8,128]{1,0:T(8,128)S(1)} %fusion.57), channel_id=1, source_target_pairs={{0,4},{1,5},{2,6},{3,7},{4,0},{5,1},{6,2},{7,3},{8,12},{9,13},{10,... | collective-permute-start | bytes 12296 | tf_op jit(solution)/shard_map/ppermute | solution.py:106
  121.5 3.4 %collective-permute-start.25 = (f32[8,128]{1,0:T(8,128)S(1)}, f32[8,128]{1,0:T(8,128)S(1)}, u32[]{:S(2)}, u32[]{:S(2)}) collective-permute-start(f32[8,128]{1,0:T(8,128)S(1)} %max.72), channel_id=1, source_target_pairs={{0,8},{1,9},{2,10},{3,11},{4,12},{5,13},{6,14},{7,15},{8,0},{9,1},... | collective-permute-start | bytes 12296 | tf_op jit(solution)/shard_map/ppermute | solution.py:106
  124.8 6.7 %collective-permute-start.26 = (f32[8,128]{1,0:T(8,128)S(1)}, f32[8,128]{1,0:T(8,128)S(1)}, u32[]{:S(2)}, u32[]{:S(2)}) collective-permute-start(f32[8,128]{1,0:T(8,128)S(1)} %max.73), channel_id=1, source_target_pairs={{0,16},{1,17},{2,18},{3,19},{4,20},{5,21},{6,22},{7,23},{8,24},{9,... | collective-permute-start | bytes 12296 | tf_op jit(solution)/shard_map/ppermute | solution.py:106
  131.5 2.8 %collective-permute-start.27 = (f32[8,128]{1,0:T(8,128)S(1)}, f32[8,128]{1,0:T(8,128)S(1)}, u32[]{:S(2)}, u32[]{:S(2)}) collective-permute-start(f32[8,128]{1,0:T(8,128)S(1)} %max.74), channel_id=1, source_target_pairs={{0,32},{32,0},{64,96},{96,64},{128,160},{160,128},{192,224},{224,1... | collective-permute-start | bytes 12296 | tf_op jit(solution)/shard_map/ppermute | solution.py:106
  134.3 4.0 %collective-permute-start.28 = (f32[8,128]{1,0:T(8,128)S(1)}, f32[8,128]{1,0:T(8,128)S(1)}, u32[]{:S(2)}, u32[]{:S(2)}) collective-permute-start(f32[8,128]{1,0:T(8,128)S(1)} %max.75), channel_id=1, source_target_pairs={{0,64},{32,96},{64,0},{96,32},{128,192},{160,224},{192,128},{224,1... | collective-permute-start | bytes 12296 | tf_op jit(solution)/shard_map/ppermute | solution.py:106
  138.2 4.0 %collective-permute-start.29 = (f32[8,128]{1,0:T(8,128)S(1)}, f32[8,128]{1,0:T(8,128)S(1)}, u32[]{:S(2)}, u32[]{:S(2)}) collective-permute-start(f32[8,128]{1,0:T(8,128)S(1)} %max.76), channel_id=1, source_target_pairs={{0,128},{32,160},{64,192},{96,224},{128,0},{160,32},{192,64},{224,... | collective-permute-start | bytes 12296 | tf_op jit(solution)/shard_map/ppermute | solution.py:106
  146.7 8.3 %collective-permute-start.30 = (f32[48,1024]{1,0:T(8,128)S(1)}, f32[48,1024]{1,0:T(8,128)S(1)}, u32[]{:S(2)}, u32[]{:S(2)}) collective-permute-start(f32[48,1024]{1,0:T(8,128)S(1)} %slice_select_fusion), channel_id=1, source_target_pairs={{0,1},{1,0},{2,3},{3,2},{4,5},{5,4},{6,7},{7,6},{8,9},{9,8},{10,11... | collective-permute-start | bytes 589832 | tf_op jit(solution)/shard_map/ppermute | solution.py:126
  155.1 4.1 %collective-permute-start.31 = (f32[24,1024]{1,0:T(8,128)S(1)}, f32[24,1024]{1,0:T(8,128)S(1)}, u32[]{:S(2)}, u32[]{:S(2)}) collective-permute-start(f32[24,1024]{1,0:T(8,128)S(1)} %slice_select_fusion.2), channel_id=1, source_target_pairs={{0,2},{1,3},{2,0},{3,1},{4,6},{5,7},{6,4},{7,5},{8,10},{9,11},{10,... | collective-permute-start | bytes 294920 | tf_op jit(solution)/shard_map/ppermute | solution.py:126
  159.2 3.2 %collective-permute-start.32 = (f32[12,1024]{1,0:T(8,128)S(1)}, f32[12,1024]{1,0:T(8,128)S(1)}, u32[]{:S(2)}, u32[]{:S(2)}) collective-permute-start(f32[12,1024]{1,0:T(8,128)S(1)} %slice_select_fusion.4), channel_id=1, source_target_pairs={{0,4},{1,5},{2,6},{3,7},{4,0},{5,1},{6,2},{7,3},{8,12},{9,13},{10,... | collective-permute-start | bytes 147464 | tf_op jit(solution)/shard_map/ppermute | solution.py:126
  162.4 3.8 %collective-permute-start.33 = (f32[12,512]{1,0:T(8,128)S(1)}, f32[12,512]{1,0:T(8,128)S(1)}, u32[]{:S(2)}, u32[]{:S(2)}) collective-permute-start(f32[12,512]{1,0:T(8,128)S(1)} %slice_select_fusion.6), channel_id=1, source_target_pairs={{0,8},{1,9},{2,10},{3,11},{4,12},{5,13},{6,14},{7,15},{8,0},{9,1},... | collective-permute-start | bytes 73736 | tf_op jit(solution)/shard_map/ppermute | solution.py:126
  166.2 7.0 %collective-permute-start.34 = (f32[12,256]{1,0:T(8,128)S(1)}, f32[12,256]{1,0:T(8,128)S(1)}, u32[]{:S(2)}, u32[]{:S(2)}) collective-permute-start(f32[12,256]{1,0:T(8,128)S(1)} %slice_select_fusion.8), channel_id=1, source_target_pairs={{0,16},{1,17},{2,18},{3,19},{4,20},{5,21},{6,22},{7,23},{8,24},{9,... | collective-permute-start | bytes 36872 | tf_op jit(solution)/shard_map/ppermute | solution.py:126
  173.2 6.5 %collective-permute-start.35 = (f32[12,256]{1,0:T(8,128)S(1)}, f32[12,256]{1,0:T(8,128)S(1)}, u32[]{:S(2)}, u32[]{:S(2)}) collective-permute-start(f32[12,256]{1,0:T(8,128)S(1)} %select_add_fusion.8), channel_id=1, source_target_pairs={{0,16},{1,17},{2,18},{3,19},{4,20},{5,21},{6,22},{7,23},{8,24},{9,... | collective-permute-start | bytes 36872 | tf_op jit(solution)/shard_map/ppermute | solution.py:130
  179.7 4.0 %collective-permute-start.36 = (f32[12,512]{1,0:T(8,128)S(1)}, f32[12,512]{1,0:T(8,128)S(1)}, u32[]{:S(2)}, u32[]{:S(2)}) collective-permute-start(f32[12,512]{1,0:T(8,128)S(1)} %maximum_select_fusion.9), channel_id=1, source_target_pairs={{0,8},{1,9},{2,10},{3,11},{4,12},{5,13},{6,14},{7,15},{8,0},{9,1},... | collective-permute-start | bytes 73736 | tf_op jit(solution)/shard_map/ppermute | solution.py:130
  183.7 3.2 %collective-permute-start.37 = (f32[12,1024]{1,0:T(8,128)S(1)}, f32[12,1024]{1,0:T(8,128)S(1)}, u32[]{:S(2)}, u32[]{:S(2)}) collective-permute-start(f32[12,1024]{1,0:T(8,128)S(1)} %maximum_select_fusion.7), channel_id=1, source_target_pairs={{0,4},{1,5},{2,6},{3,7},{4,0},{5,1},{6,2},{7,3},{8,12},{9,13},{10,... | collective-permute-start | bytes 147464 | tf_op jit(solution)/shard_map/ppermute | solution.py:130
  186.9 3.6 %collective-permute-start.38 = (f32[24,1024]{1,0:T(8,128)S(1)}, f32[24,1024]{1,0:T(8,128)S(1)}, u32[]{:S(2)}, u32[]{:S(2)}) collective-permute-start(f32[24,1024]{1,0:T(8,128)S(1)} %maximum_select_fusion.5), channel_id=1, source_target_pairs={{0,2},{1,3},{2,0},{3,1},{4,6},{5,7},{6,4},{7,5},{8,10},{9,11},{10,... | collective-permute-start | bytes 294920 | tf_op jit(solution)/shard_map/ppermute | solution.py:130
  190.5 9.7 %collective-permute-start.39 = (f32[48,1024]{1,0:T(8,128)S(1)}, f32[48,1024]{1,0:T(8,128)S(1)}, u32[]{:S(2)}, u32[]{:S(2)}) collective-permute-start(f32[48,1024]{1,0:T(8,128)S(1)} %maximum_select_fusion.3), channel_id=1, source_target_pairs={{0,1},{1,0},{2,3},{3,2},{4,5},{5,4},{6,7},{7,6},{8,9},{9,8},{10,11... | collective-permute-start | bytes 589832 | tf_op jit(solution)/shard_map/ppermute | solution.py:130

commit v2 on v0

--- a/solution.py
+++ b/solution.py
@@ -94,14 +94,77 @@
     return jnp.stack([new_density, radial, azimuth])
 
 
+def xor_pairs(count, bit):
+    return [(i, i ^ bit) for i in range(count)]
+
+
+def mirror_pairs(count, block):
+    blocks = count // block
+    return [(i, (blocks - 1 - i // block) * block + i % block) for i in range(count)]
+
+
+def global_max(value, axes):
+    count = 1
+    for axis in axes:
+        count *= lax.axis_size(axis)
+    spread = jnp.broadcast_to(value, (count, 128))
+    return jnp.max(lax.all_to_all(spread, axes, 0, 0, tiled=True))
+
+
+def split_rounds(part, axis, rounds):
+    index = lax.axis_index(axis)
+    done = []
+    for bit in rounds:
+        dim = 0 if part.shape[0] % 2 == 0 and part.shape[0] >= 16 else 1
+        half = part.shape[dim] // 2
+        low = lax.slice_in_dim(part, 0, half, axis=dim)
+        high = lax.slice_in_dim(part, half, None, axis=dim)
+        upper = (index // bit) % 2 == 1
+        keep = jnp.where(upper, high, low)
+        send = jnp.where(upper, low, high)
+        part = keep + lax.ppermute(send, axis, xor_pairs(lax.axis_size(axis), bit))
+        done.append((bit, dim))
+    return part, done
+
+
+def join_rounds(part, axis, done):
+    index = lax.axis_index(axis)
+    for bit, dim in reversed(done):
+        other = lax.ppermute(part, axis, xor_pairs(lax.axis_size(axis), bit))
+        upper = (index // bit) % 2 == 1
+        part = jnp.where(
+            upper,
+            jnp.concatenate([other, part], axis=dim),
+            jnp.concatenate([part, other], axis=dim),
+        )
+    return part
+
+
+def species_sum(block, axis):
+    count = lax.axis_size(axis)
+    index = lax.axis_index(axis)
+    low_bits = [bit for bit in (1, 2) if bit < count]
+    part, done = split_rounds(block, axis, low_bits)
+    block_size = 2 * low_bits[-1] if low_bits else 1
+    bit = block_size
+    while bit < count:
+        pairs = mirror_pairs(count, block_size) if 2 * bit >= count else xor_pairs(count, bit)
+        other = lax.ppermute(part, axis, pairs)
+        upper = (index // bit) % 2 == 1 if 2 * bit < count else index >= count // 2
+        part = jnp.where(upper, other + part, part + other)
+        bit *= 2
+    return join_rounds(part, axis, done)
+
+
 def advance(wide, margin, tile_rows, stop_times, total_species):
     interior = lax.slice_in_dim(wide, margin, margin + tile_rows, axis=2)
     local_top = jnp.max(jnp.abs(interior[1]) + jnp.abs(interior[2]))
-    fastest = lax.pmax(local_top, ("space", "species"))
+    fastest = global_max(local_top, ("space", "species"))
     step_time = courant / (sound_speed + fastest)
     new_density, gas_velocity, dust_velocity = moved(wide, step_time)
     rate, terms = drag_terms(new_density, dust_velocity, stop_times, step_time, total_species)
-    totals = lax.psum(terms, "species")
+    shape = terms.shape
+    totals = species_sum(terms.reshape(-1, shape[-1]), "species").reshape(shape)
     gas_next = coupled_gas(gas_velocity, totals)
     return assemble(new_density, dust_velocity, gas_next, rate)
 

time: 627 us -> 142 us (0.23)
  waiting for transfers between devices: 412 us -> 59 us
  blocking collectives: 156 us -> 0 us
  starting transfers between devices: 11.5 us -> 49.3 us
  between operations: 15.8 us -> 2.62 us
    psum x2 -> x0, waiting for transfers between devices: 412 us -> none  [advance(): totals = lax.psum(terms, 'species')]
    pmax x2 -> x0, blocking collectives: 156 us -> none  [advance(): fastest = lax.pmax(local_top, ('space', 'species'))]
    ppermute x0 -> x14, waiting for transfers between devices: none -> 42.4 us  [the longest x6 24.8 us: species_sum(): other = lax.ppermute(part, axis, pairs)]
    all_to_all x0 -> x2, starting transfers between devices: none -> 22.5 us  [global_max(): return jnp.max(lax.all_to_all(spread, axes, 0, 0, tiled=True))]
    ppermute x0 -> x14, starting transfers between devices: none -> 18.9 us  [the longest x4 12.1 us: join_rounds(): other = lax.ppermute(part, axis, xor_pairs(lax.axis_size(axis), bit))]
    all_to_all x0 -> x2, waiting for transfers between devices: none -> 16.6 us  [global_max(): return jnp.max(lax.all_to_all(spread, axes, 0, 0, tiled=True))]
  transfers between devices with their start and end apart: 6 -> 20, of which waited for: 2 -> 15; matrix products, arithmetic and copies ran while one was open for 1% -> 10% of each run, Pallas kernels for 0% -> 0%
where the time goes in v2:
time: 142 us
  waiting for transfers between devices  59 us (42%)
  starting transfers between devices  49.3 us (35%)
  other arithmetic  25.8 us (18%)
  local copies, waits for them, and re-layouts  5.34 us (4%)
  between operations  2.62 us (2%)
    ppermute x6, waiting for transfers between devices, species_sum(): other = lax.ppermute(part, axis, pairs)  24.8 us
    all_to_all x2, starting transfers between devices, global_max(): return jnp.max(lax.all_to_all(spread, axes, 0, 0, tiled=True))  22.5 us
    all_to_all x2, waiting for transfers between devices, global_max(): return jnp.max(lax.all_to_all(spread, axes, 0, 0, tiled=True))  16.6 us
    ppermute x4, starting transfers between devices, join_rounds(): other = lax.ppermute(part, axis, xor_pairs(lax.axis_size(axis), bit))  12.1 us
    ppermute x4, waiting for transfers between devices, split_rounds(): part = keep + lax.ppermute(send, axis, xor_pairs(lax.axis_size(axis), bit))  9.92 us
    ppermute x4, waiting for transfers between devices, join_rounds(): other = lax.ppermute(part, axis, xor_pairs(lax.axis_size(axis), bit))  7.73 us
    add x4, other arithmetic, face_divergence(): jnp.maximum(face_speed, 0.0) * (1.5 * here - 0.5 * back_two)  6.44 us
    ppermute x2, starting transfers between devices, padded(): lax.ppermute(lax.slice_in_dim(block, 0, width, axis=dim), axis, backward)  5.22 us
  transfers between devices with their start and end apart: 20, of which 15 were waited for; matrix products, arithmetic and copies ran while one was open for 10% of the time, Pallas kernels for 0%

profile of v2, /device:TPU:1, one launch (start us, length us, event | category | flops | bytes accessed | tf_op | source)
XLA Modules:
  0.0 142.1 jit_solution(15518125865426904149)
XLA Ops:
  0.7 1.4 %pad_maximum_fusion.26 = (f32[3,5,2,1024]{3,2,1,0:T(2,128)S(1)}, f32[3,5,2,1024]{3,2,1,0:T(2,128)S(1)}) fusion(f32[3,1,32,1024]{3,2,1,0:T(8,128)} %bitcast.97, f32[3,4,32,1024]{3,2,1,0:T(8,128)} %param.3), kind=kLoop, calls=%fused_computation.144 | loop fusion | flops 61440 | bytes 2211840 | tf_op jit(solution)/shard_map/slice | solution.py:23
  2.1 2.2 %collective-permute-start = (f32[3,5,2,1024]{3,2,1,0:T(2,128)S(1)}, f32[3,5,2,1024]{3,2,1,0:T(2,128)S(1)}, u32[]{:S(2)}, u32[]{:S(2)}) collective-permute-start(f32[3,5,2,1024]{3,2,1,0:T(2,128)S(1)} %get-tuple-element.22), channel_id=1, source_target_pairs={{0,32},{32,64},{64,96},{96,128},{128,160},{160,192},{192,224},{224... | collective-permute-start | bytes 368648 | tf_op jit(solution)/shard_map/ppermute | solution.py:22
  4.3 4.0 %collective-permute-start.1 = (f32[3,5,2,1024]{3,2,1,0:T(2,128)S(1)}, f32[3,5,2,1024]{3,2,1,0:T(2,128)S(1)}, u32[]{:S(2)}, u32[]{:S(2)}) collective-permute-start(f32[3,5,2,1024]{3,2,1,0:T(2,128)S(1)} %get-tuple-element.23), channel_id=1, source_target_pairs={{32,0},{64,32},{96,64},{128,96},{160,128},{192,160},{224,192},{0,2... | collective-permute-start | bytes 368648 | tf_op jit(solution)/shard_map/ppermute | solution.py:25
  8.3 0.8 fusion.22
  9.1 1.4 broadcast_in_dim.7
  10.4 13.6 %all-to-all-start = ((f32[256,1,128]{2,1,0:T(1,128)}), f32[256,1,128]{2,1,0:T(1,128)}, u32[]{:S(2)}, u32[]{:S(2)}) async-start(f32[256,1,128]{2,1,0:T(1,128)} %broadcast_in_dim.7), calls=%async_computation | async-start | bytes 262144 | tf_op jit(solution)/shard_map/all_to_all | solution.py:111
  24.1 0.4 pad_maximum_fusion
  24.5 0.2 slice_bitcast_fusion.4
  24.8 1.5 %fusion.10 = f32[5,33,1024]{2,1,0:T(8,128)} fusion(f32[5,36,1024]{2,1,0:T(8,128)S(1)} %get-tuple-element.19, f32[5,36,1024]{2,1,0:T(8,128)S(1)} %get-tuple-element.17), kind=kLoop, calls=%fused_computation.25 | loop fusion | flops 2196480 | bytes 4730880 | tf_op jit(solution)/shard_map/add | solution.py:41
  26.4 1.7 %multiply_add_fusion.1 = f32[5,32,1025]{2,1,0:T(8,128)} fusion(f32[5,32,1024]{2,1,0:T(8,128)S(1)} %slice.438, f32[5,32,1024]{2,1,0:T(8,128)S(1)} %slice.449), kind=kLoop, calls=%fused_computation.36 | loop fusion | flops 2132000 | bytes 1966720 | tf_op jit(solution)/shard_map/add | solution.py:41
  28.1 7.8 %all-to-all-done = f32[256,1,128]{2,1,0:T(1,128)} async-done(((f32[256,1,128]{2,1,0:T(1,128)}), f32[256,1,128]{2,1,0:T(1,128)}, u32[]{:S(2)}, u32[]{:S(2)}) %all-to-all-start) | async-done | bytes 131104 | tf_op jit(solution)/shard_map/all_to_all | solution.py:111
  35.9 1.5 %reduce_max.37 = f32[]{:T(128)} reduce(f32[256,1,128]{2,0,1:T(8,128)} %bitcast.2, f32[]{:T(128)} %constant.110.clone.1), dimensions={0,1,2}, to_apply=%region_1.0 | reduce | flops 32767 | bytes 131080 | tf_op jit(solution)/shard_map/reduce_max | solution.py:111
  38.2 2.2 %fusion.19 = f32[5,32,1024]{2,1,0:T(8,128)S(1)} fusion(f32[5,32,1025]{2,1,0:T(8,128)} %multiply_add_fusion.1, f32[5,33,1024]{2,1,0:T(8,128)} %fusion.10, f32[]{:T(128)S(6)} %div.163, f32[5,36,1024]{2,1,0:T(8,128)S(1)} %get-tuple-element.19), kind=kLoop, calls=%fused_computation.45 | loop fusion | flops 819200 | bytes 3932164 | tf_op jit(solution)/shard_map/sub | solution.py:58
  40.4 1.0 broadcast_divide_fusion.1
  41.4 1.2 fusion.52
  42.7 0.7 slice_select_fusion.1
  43.4 1.2 collective-permute-start.2
  44.6 1.4 collective-permute-done.2
  46.0 1.0 select_add_fusion.1
  47.0 0.4 collective-permute-start.3
  47.4 3.7 %collective-permute-done.3 = f32[24,1024]{1,0:T(8,128)S(1)} collective-permute-done((f32[24,1024]{1,0:T(8,128)S(1)}, f32[24,1024]{1,0:T(8,128)S(1)}, u32[]{:S(2)}, u32[]{:S(2)}) %collective-permute-start.3) | collective-permute-done | bytes 98336 | tf_op jit(solution)/shard_map/ppermute | solution.py:125
  51.1 0.6 collective-permute-start.4
  51.7 2.9 %collective-permute-done.4 = f32[24,1024]{1,0:T(8,128)S(1)} collective-permute-done((f32[24,1024]{1,0:T(8,128)S(1)}, f32[24,1024]{1,0:T(8,128)S(1)}, u32[]{:S(2)}, u32[]{:S(2)}) %collective-permute-start.4) | collective-permute-done | bytes 98336 | tf_op jit(solution)/shard_map/ppermute | solution.py:152
  54.7 0.9 collective-permute-start.5
  55.6 4.6 %collective-permute-done.5 = f32[24,1024]{1,0:T(8,128)S(1)} collective-permute-done((f32[24,1024]{1,0:T(8,128)S(1)}, f32[24,1024]{1,0:T(8,128)S(1)}, u32[]{:S(2)}, u32[]{:S(2)}) %collective-permute-start.5) | collective-permute-done | bytes 98336 | tf_op jit(solution)/shard_map/ppermute | solution.py:152
  60.2 0.5 collective-permute-start.6
  60.6 1.0 slice_bitcast_fusion.17
  61.7 4.3 %collective-permute-done.6 = f32[24,1024]{1,0:T(8,128)S(1)} collective-permute-done((f32[24,1024]{1,0:T(8,128)S(1)}, f32[24,1024]{1,0:T(8,128)S(1)}, u32[]{:S(2)}, u32[]{:S(2)}) %collective-permute-start.6) | collective-permute-done | bytes 98336 | tf_op jit(solution)/shard_map/ppermute | solution.py:152
  66.0 0.4 collective-permute-start.7
  66.5 3.4 %collective-permute-done.7 = f32[24,1024]{1,0:T(8,128)S(1)} collective-permute-done((f32[24,1024]{1,0:T(8,128)S(1)}, f32[24,1024]{1,0:T(8,128)S(1)}, u32[]{:S(2)}, u32[]{:S(2)}) %collective-permute-start.7) | collective-permute-done | bytes 98336 | tf_op jit(solution)/shard_map/ppermute | solution.py:133
  69.9 5.7 %collective-permute-start.8 = (f32[48,1024]{1,0:T(8,128)S(1)}, f32[48,1024]{1,0:T(8,128)S(1)}, u32[]{:S(2)}, u32[]{:S(2)}) collective-permute-start(f32[48,1024]{1,0:T(8,128)S(1)} %maximum_select_fusion.2), channel_id=1, source_target_pairs={{0,1},{1,0},{2,3},{3,2},{4,5},{5,4},{6,7},{7,6},{8,9},{9,8},{10,11... | collective-permute-start | bytes 589832 | tf_op jit(solution)/shard_map/ppermute | solution.py:133
  75.6 1.1 fusion.50
  76.8 0.3 fusion
  77.2 0.9 add_reduce_fusion
  78.2 1.2 collective-permute-start.10
  79.4 0.5 collective-permute-start.9
  79.9 1.4 broadcast_in_dim.8
  81.3 8.9 %all-to-all-start.1 = ((f32[256,1,128]{2,1,0:T(1,128)}), f32[256,1,128]{2,1,0:T(1,128)S(1)}, u32[]{:S(2)}, u32[]{:S(2)}) async-start(f32[256,1,128]{2,1,0:T(1,128)} %broadcast_in_dim.8), calls=%async_computation.1 | async-start | bytes 262144 | tf_op jit(solution)/shard_map/all_to_all | solution.py:111
  90.2 0.4 pad_maximum_fusion.1
  90.6 0.2 slice_bitcast_fusion.1
  90.8 1.5 %fusion.4 = f32[5,33,1024]{2,1,0:T(8,128)} fusion(f32[5,36,1024]{2,1,0:T(8,128)S(1)} %get-tuple-element.16, f32[5,36,1024]{2,1,0:T(8,128)S(1)} %get-tuple-element.14), kind=kLoop, calls=%fused_computation.11 | loop fusion | flops 2196480 | bytes 4730880 | tf_op jit(solution)/shard_map/add | solution.py:41
  92.5 1.7 %multiply_add_fusion = f32[5,32,1025]{2,1,0:T(8,128)} fusion(f32[5,32,1024]{2,1,0:T(8,128)S(1)} %slice.471, f32[5,32,1024]{2,1,0:T(8,128)S(1)} %slice.482), kind=kLoop, calls=%fused_computation.35 | loop fusion | flops 2132000 | bytes 1966720 | tf_op jit(solution)/shard_map/add | solution.py:41
  94.2 8.7 %all-to-all-done.1 = f32[256,1,128]{2,1,0:T(1,128)S(1)} async-done(((f32[256,1,128]{2,1,0:T(1,128)}), f32[256,1,128]{2,1,0:T(1,128)S(1)}, u32[]{:S(2)}, u32[]{:S(2)}) %all-to-all-start.1) | async-done | bytes 131104 | tf_op jit(solution)/shard_map/all_to_all | solution.py:111
  102.9 0.6 reduce_max.39
  104.3 2.3 %fusion.16 = f32[5,32,1024]{2,1,0:T(8,128)S(1)} fusion(f32[5,32,1025]{2,1,0:T(8,128)} %multiply_add_fusion, f32[5,33,1024]{2,1,0:T(8,128)} %fusion.4, f32[]{:T(128)S(6)} %div.184, f32[5,36,1024]{2,1,0:T(8,128)S(1)} %get-tuple-element.16), kind=kLoop, calls=%fused_computation.40 | loop fusion | flops 819200 | bytes 3932164 | tf_op jit(solution)/shard_map/sub | solution.py:58
  106.6 0.2 broadcast_divide_fusion
  106.9 0.2 fusion.51
  107.2 1.1 collective-permute-start.11
  108.3 1.1 collective-permute-done.11
  109.4 0.4 collective-permute-start.12
  109.8 3.7 %collective-permute-done.12 = f32[24,1024]{1,0:T(8,128)S(1)} collective-permute-done((f32[24,1024]{1,0:T(8,128)S(1)}, f32[24,1024]{1,0:T(8,128)S(1)}, u32[]{:S(2)}, u32[]{:S(2)}) %collective-permute-start.12) | collective-permute-done | bytes 98336 | tf_op jit(solution)/shard_map/ppermute | solution.py:125
  113.5 0.9 collective-permute-start.13
  114.5 2.6 %collective-permute-done.13 = f32[24,1024]{1,0:T(8,128)S(1)} collective-permute-done((f32[24,1024]{1,0:T(8,128)S(1)}, f32[24,1024]{1,0:T(8,128)S(1)}, u32[]{:S(2)}, u32[]{:S(2)}) %collective-permute-start.13) | collective-permute-done | bytes 98336 | tf_op jit(solution)/shard_map/ppermute | solution.py:152
  117.1 0.7 collective-permute-start.14
  117.8 4.8 %collective-permute-done.14 = f32[24,1024]{1,0:T(8,128)S(1)} collective-permute-done((f32[24,1024]{1,0:T(8,128)S(1)}, f32[24,1024]{1,0:T(8,128)S(1)}, u32[]{:S(2)}, u32[]{:S(2)}) %collective-permute-start.14) | collective-permute-done | bytes 98336 | tf_op jit(solution)/shard_map/ppermute | solution.py:152
  122.6 0.2 collective-permute-start.15
  122.9 5.5 %collective-permute-done.15 = f32[24,1024]{1,0:T(8,128)S(1)} collective-permute-done((f32[24,1024]{1,0:T(8,128)S(1)}, f32[24,1024]{1,0:T(8,128)S(1)}, u32[]{:S(2)}, u32[]{:S(2)}) %collective-permute-start.15) | collective-permute-done | bytes 98336 | tf_op jit(solution)/shard_map/ppermute | solution.py:152
  128.5 0.4 collective-permute-start.16
  129.0 3.3 %collective-permute-done.16 = f32[24,1024]{1,0:T(8,128)S(1)} collective-permute-done((f32[24,1024]{1,0:T(8,128)S(1)}, f32[24,1024]{1,0:T(8,128)S(1)}, u32[]{:S(2)}, u32[]{:S(2)}) %collective-permute-start.16) | collective-permute-done | bytes 98336 | tf_op jit(solution)/shard_map/ppermute | solution.py:133
  132.3 5.6 %collective-permute-start.17 = (f32[48,1024]{1,0:T(8,128)S(1)}, f32[48,1024]{1,0:T(8,128)S(1)}, u32[]{:S(2)}, u32[]{:S(2)}) collective-permute-start(f32[48,1024]{1,0:T(8,128)S(1)} %maximum_select_fusion.3), channel_id=1, source_target_pairs={{0,1},{1,0},{2,3},{3,2},{4,5},{5,4},{6,7},{7,6},{8,9},{9,8},{10,11... | collective-permute-start | bytes 589832 | tf_op jit(solution)/shard_map/ppermute | solution.py:133
  138.0 1.0 collective-permute-done.17
  139.2 0.3 fusion.1
  139.7 0.8 maximum_bitcast_fusion.2
  140.8 1.3 copy.15
  (81 shorter events, 2.0 us)
Async XLA Ops:
  0.6 7.7 %copy-start.5 = (f32[3,32,1024]{2,1,0:T(8,128)S(1)}, f32[3,32,1024]{2,1,0:T(8,128)}, u32[]{:S(2)}) copy-start(f32[3,32,1024]{2,1,0:T(8,128)} %param.4) | copy-start | bytes 1179652
  0.6 7.7 %copy-start = (f32[3,4,32,1024]{3,2,1,0:T(8,128)S(1)}, f32[3,4,32,1024]{3,2,1,0:T(8,128)}, u32[]{:S(2)}) copy-start(f32[3,4,32,1024]{3,2,1,0:T(8,128)} %param.3) | copy-start | bytes 4718596
  0.7 23.4 %copy-start.15 = (s32[4]{0:T(128)S(1)}, s32[4]{0:T(128)}, u32[]{:S(2)}) copy-start(s32[4]{0:T(128)} %param.5) | copy-start | bytes 52
  2.1 21.9 %collective-permute-start = (f32[3,5,2,1024]{3,2,1,0:T(2,128)S(1)}, f32[3,5,2,1024]{3,2,1,0:T(2,128)S(1)}, u32[]{:S(2)}, u32[]{:S(2)}) collective-permute-start(f32[3,5,2,1024]{3,2,1,0:T(2,128)S(1)} %get-tuple-element.22), channel_id=1, source_target_pairs={{0,32},{32,64},{64,96},{96,128},{128,160},{160,192},{192,224},{224... | collective-permute-start | bytes 368648 | tf_op jit(solution)/shard_map/ppermute | solution.py:22
  4.3 19.8 %collective-permute-start.1 = (f32[3,5,2,1024]{3,2,1,0:T(2,128)S(1)}, f32[3,5,2,1024]{3,2,1,0:T(2,128)S(1)}, u32[]{:S(2)}, u32[]{:S(2)}) collective-permute-start(f32[3,5,2,1024]{3,2,1,0:T(2,128)S(1)} %get-tuple-element.23), channel_id=1, source_target_pairs={{32,0},{64,32},{96,64},{128,96},{160,128},{192,160},{224,192},{0,2... | collective-permute-start | bytes 368648 | tf_op jit(solution)/shard_map/ppermute | solution.py:25
  10.4 25.5 %all-to-all-start = ((f32[256,1,128]{2,1,0:T(1,128)}), f32[256,1,128]{2,1,0:T(1,128)}, u32[]{:S(2)}, u32[]{:S(2)}) async-start(f32[256,1,128]{2,1,0:T(1,128)} %broadcast_in_dim.7), calls=%async_computation | async-start | bytes 262144 | tf_op jit(solution)/shard_map/all_to_all | solution.py:111
  24.0 0.7 copy-start.13
  24.1 0.7 copy-start.14
  24.7 1.5 %copy-start.1 = (f32[5,36,1024]{2,1,0:T(8,128)}, f32[5,36,1024]{2,1,0:T(8,128)S(1)}, u32[]{:S(2)}) copy-start(f32[5,36,1024]{2,1,0:T(8,128)S(1)} %get-tuple-element.17) | copy-start | bytes 2211844
  24.7 1.6 %copy-start.6 = (f32[5,36,1024]{2,1,0:T(8,128)}, f32[5,36,1024]{2,1,0:T(8,128)S(1)}, u32[]{:S(2)}) copy-start(f32[5,36,1024]{2,1,0:T(8,128)S(1)} %get-tuple-element.18) | copy-start | bytes 2211844
  38.2 3.3 %copy-start.2 = (f32[5,36,1024]{2,1,0:T(8,128)S(1)}, f32[5,36,1024]{2,1,0:T(8,128)}, u32[]{:S(2)}) copy-start(f32[5,36,1024]{2,1,0:T(8,128)} %copy-done.1) | copy-start | bytes 2211844
  38.2 3.2 %copy-start.7 = (f32[5,36,1024]{2,1,0:T(8,128)S(1)}, f32[5,36,1024]{2,1,0:T(8,128)}, u32[]{:S(2)}) copy-start(f32[5,36,1024]{2,1,0:T(8,128)} %copy-done.6) | copy-start | bytes 2211844
  43.4 2.6 %collective-permute-start.2 = (f32[48,1024]{1,0:T(8,128)}, f32[48,1024]{1,0:T(8,128)}, u32[]{:S(2)}, u32[]{:S(2)}) collective-permute-start(f32[48,1024]{1,0:T(8,128)} %slice_select_fusion.1), channel_id=1, source_target_pairs={{0,1},{1,0},{2,3},{3,2},{4,5},{5,4},{6,7},{7,6},{8,9},{9,8},{10,11... | collective-permute-start | bytes 589832 | tf_op jit(solution)/shard_map/ppermute | solution.py:125
  47.0 4.1 %collective-permute-start.3 = (f32[24,1024]{1,0:T(8,128)S(1)}, f32[24,1024]{1,0:T(8,128)S(1)}, u32[]{:S(2)}, u32[]{:S(2)}) collective-permute-start(f32[24,1024]{1,0:T(8,128)S(1)} %slice_select_fusion.3), channel_id=1, source_target_pairs={{0,2},{1,3},{2,0},{3,1},{4,6},{5,7},{6,4},{7,5},{8,10},{9,11},{10,... | collective-permute-start | bytes 294920 | tf_op jit(solution)/shard_map/ppermute | solution.py:125
  51.1 3.6 %collective-permute-start.4 = (f32[24,1024]{1,0:T(8,128)S(1)}, f32[24,1024]{1,0:T(8,128)S(1)}, u32[]{:S(2)}, u32[]{:S(2)}) collective-permute-start(f32[24,1024]{1,0:T(8,128)S(1)} %select_add_fusion.3), channel_id=1, source_target_pairs={{0,4},{1,5},{2,6},{3,7},{4,0},{5,1},{6,2},{7,3},{8,12},{9,13},{10,... | collective-permute-start | bytes 294920 | tf_op jit(solution)/shard_map/ppermute | solution.py:152
  54.7 5.5 %collective-permute-start.5 = (f32[24,1024]{1,0:T(8,128)S(1)}, f32[24,1024]{1,0:T(8,128)S(1)}, u32[]{:S(2)}, u32[]{:S(2)}) collective-permute-start(f32[24,1024]{1,0:T(8,128)S(1)} %add.168), channel_id=1, source_target_pairs={{0,8},{1,9},{2,10},{3,11},{4,12},{5,13},{6,14},{7,15},{8,0},{9,1},... | collective-permute-start | bytes 294920 | tf_op jit(solution)/shard_map/ppermute | solution.py:152
  60.2 5.8 %collective-permute-start.6 = (f32[24,1024]{1,0:T(8,128)S(1)}, f32[24,1024]{1,0:T(8,128)S(1)}, u32[]{:S(2)}, u32[]{:S(2)}) collective-permute-start(f32[24,1024]{1,0:T(8,128)S(1)} %add.169), channel_id=1, source_target_pairs={{0,28},{1,29},{2,30},{3,31},{4,24},{5,25},{6,26},{7,27},{8,20},{9,... | collective-permute-start | bytes 294920 | tf_op jit(solution)/shard_map/ppermute | solution.py:152
  61.6 15.2 %copy-start.10 = (f32[4,32,1024]{2,1,0:T(8,128)S(1)}, f32[4,32,1024]{2,1,0:T(8,128)}, u32[]{:S(2)}) copy-start(f32[4,32,1024]{2,1,0:T(8,128)} %get-tuple-element.50) | copy-start | bytes 1572868
  61.7 15.2 %copy-start.11 = (f32[1,4,32,1024]{3,2,1,0:T(8,128)S(1)}, f32[1,4,32,1024]{3,2,1,0:T(8,128)}, u32[]{:S(2)}) copy-start(f32[1,4,32,1024]{3,2,1,0:T(8,128)} %get-tuple-element.30) | copy-start | bytes 1572868
  61.7 15.2 %copy-start.12 = (f32[1,4,32,1024]{3,2,1,0:T(8,128)S(1)}, f32[1,4,32,1024]{3,2,1,0:T(8,128)}, u32[]{:S(2)}) copy-start(f32[1,4,32,1024]{3,2,1,0:T(8,128)} %get-tuple-element.31) | copy-start | bytes 1572868
  66.0 3.8 %collective-permute-start.7 = (f32[24,1024]{1,0:T(8,128)S(1)}, f32[24,1024]{1,0:T(8,128)S(1)}, u32[]{:S(2)}, u32[]{:S(2)}) collective-permute-start(f32[24,1024]{1,0:T(8,128)S(1)} %add.170), channel_id=1, source_target_pairs={{0,2},{1,3},{2,0},{3,1},{4,6},{5,7},{6,4},{7,5},{8,10},{9,11},{10,... | collective-permute-start | bytes 294920 | tf_op jit(solution)/shard_map/ppermute | solution.py:133
  69.9 6.8 %collective-permute-start.8 = (f32[48,1024]{1,0:T(8,128)S(1)}, f32[48,1024]{1,0:T(8,128)S(1)}, u32[]{:S(2)}, u32[]{:S(2)}) collective-permute-start(f32[48,1024]{1,0:T(8,128)S(1)} %maximum_select_fusion.2), channel_id=1, source_target_pairs={{0,1},{1,0},{2,3},{3,2},{4,5},{5,4},{6,7},{7,6},{8,9},{9,8},{10,11... | collective-permute-start | bytes 589832 | tf_op jit(solution)/shard_map/ppermute | solution.py:133
  78.1 12.1 %copy-start.3 = (f32[1,5,32,1024]{3,2,1,0:T(8,128)}, f32[1,5,32,1024]{3,2,1,0:T(8,128)S(1)}, u32[]{:S(2)}) copy-start(f32[1,5,32,1024]{3,2,1,0:T(8,128)S(1)} %get-tuple-element.36) | copy-start | bytes 1966084
  78.2 12.0 %collective-permute-start.10 = (f32[3,5,2,1024]{3,2,1,0:T(2,128)S(1)}, f32[3,5,2,1024]{3,2,1,0:T(2,128)S(1)}, u32[]{:S(2)}, u32[]{:S(2)}) collective-permute-start(f32[3,5,2,1024]{3,2,1,0:T(2,128)S(1)} %get-tuple-element.21), channel_id=1, source_target_pairs={{32,0},{64,32},{96,64},{128,96},{160,128},{192,160},{224,192},{0,2... | collective-permute-start | bytes 368648 | tf_op jit(solution)/shard_map/ppermute | solution.py:25
  79.4 10.8 %collective-permute-start.9 = (f32[3,5,2,1024]{3,2,1,0:T(2,128)S(1)}, f32[3,5,2,1024]{3,2,1,0:T(2,128)S(1)}, u32[]{:S(2)}, u32[]{:S(2)}) collective-permute-start(f32[3,5,2,1024]{3,2,1,0:T(2,128)S(1)} %get-tuple-element.20), channel_id=1, source_target_pairs={{0,32},{32,64},{64,96},{96,128},{128,160},{160,192},{192,224},{224... | collective-permute-start | bytes 368648 | tf_op jit(solution)/shard_map/ppermute | solution.py:22
  81.3 21.7 %all-to-all-start.1 = ((f32[256,1,128]{2,1,0:T(1,128)}), f32[256,1,128]{2,1,0:T(1,128)S(1)}, u32[]{:S(2)}, u32[]{:S(2)}) async-start(f32[256,1,128]{2,1,0:T(1,128)} %broadcast_in_dim.8), calls=%async_computation.1 | async-start | bytes 262144 | tf_op jit(solution)/shard_map/all_to_all | solution.py:111
  90.8 1.6 %copy-start.8 = (f32[5,36,1024]{2,1,0:T(8,128)}, f32[5,36,1024]{2,1,0:T(8,128)S(1)}, u32[]{:S(2)}) copy-start(f32[5,36,1024]{2,1,0:T(8,128)S(1)} %get-tuple-element.15) | copy-start | bytes 2211844
  104.3 2.6 %copy-start.9 = (f32[5,36,1024]{2,1,0:T(8,128)S(1)}, f32[5,36,1024]{2,1,0:T(8,128)}, u32[]{:S(2)}) copy-start(f32[5,36,1024]{2,1,0:T(8,128)} %copy-done.8) | copy-start | bytes 2211844
  107.1 30.8 %copy-start.4 = (f32[1,5,32,1024]{3,2,1,0:T(8,128)S(1)}, f32[1,5,32,1024]{3,2,1,0:T(8,128)}, u32[]{:S(2)}) copy-start(f32[1,5,32,1024]{3,2,1,0:T(8,128)} %copy-done.3) | copy-start | bytes 1966084
  107.2 2.1 %collective-permute-start.11 = (f32[48,1024]{1,0:T(8,128)S(1)}, f32[48,1024]{1,0:T(8,128)S(1)}, u32[]{:S(2)}, u32[]{:S(2)}) collective-permute-start(f32[48,1024]{1,0:T(8,128)S(1)} %slice_select_fusion), channel_id=1, source_target_pairs={{0,1},{1,0},{2,3},{3,2},{4,5},{5,4},{6,7},{7,6},{8,9},{9,8},{10,11... | collective-permute-start | bytes 589832 | tf_op jit(solution)/shard_map/ppermute | solution.py:125
  109.4 4.1 %collective-permute-start.12 = (f32[24,1024]{1,0:T(8,128)S(1)}, f32[24,1024]{1,0:T(8,128)S(1)}, u32[]{:S(2)}, u32[]{:S(2)}) collective-permute-start(f32[24,1024]{1,0:T(8,128)S(1)} %slice_select_fusion.2), channel_id=1, source_target_pairs={{0,2},{1,3},{2,0},{3,1},{4,6},{5,7},{6,4},{7,5},{8,10},{9,11},{10,... | collective-permute-start | bytes 294920 | tf_op jit(solution)/shard_map/ppermute | solution.py:125
  113.5 3.6 %collective-permute-start.13 = (f32[24,1024]{1,0:T(8,128)S(1)}, f32[24,1024]{1,0:T(8,128)S(1)}, u32[]{:S(2)}, u32[]{:S(2)}) collective-permute-start(f32[24,1024]{1,0:T(8,128)S(1)} %select_add_fusion.2), channel_id=1, source_target_pairs={{0,4},{1,5},{2,6},{3,7},{4,0},{5,1},{6,2},{7,3},{8,12},{9,13},{10,... | collective-permute-start | bytes 294920 | tf_op jit(solution)/shard_map/ppermute | solution.py:152
  117.1 5.5 %collective-permute-start.14 = (f32[24,1024]{1,0:T(8,128)S(1)}, f32[24,1024]{1,0:T(8,128)S(1)}, u32[]{:S(2)}, u32[]{:S(2)}) collective-permute-start(f32[24,1024]{1,0:T(8,128)S(1)} %add.184), channel_id=1, source_target_pairs={{0,8},{1,9},{2,10},{3,11},{4,12},{5,13},{6,14},{7,15},{8,0},{9,1},... | collective-permute-start | bytes 294920 | tf_op jit(solution)/shard_map/ppermute | solution.py:152
  122.6 5.8 %collective-permute-start.15 = (f32[24,1024]{1,0:T(8,128)S(1)}, f32[24,1024]{1,0:T(8,128)S(1)}, u32[]{:S(2)}, u32[]{:S(2)}) collective-permute-start(f32[24,1024]{1,0:T(8,128)S(1)} %add.185), channel_id=1, source_target_pairs={{0,28},{1,29},{2,30},{3,31},{4,24},{5,25},{6,26},{7,27},{8,20},{9,... | collective-permute-start | bytes 294920 | tf_op jit(solution)/shard_map/ppermute | solution.py:152
  128.5 3.8 %collective-permute-start.16 = (f32[24,1024]{1,0:T(8,128)S(1)}, f32[24,1024]{1,0:T(8,128)S(1)}, u32[]{:S(2)}, u32[]{:S(2)}) collective-permute-start(f32[24,1024]{1,0:T(8,128)S(1)} %add.186), channel_id=1, source_target_pairs={{0,2},{1,3},{2,0},{3,1},{4,6},{5,7},{6,4},{7,5},{8,10},{9,11},{10,... | collective-permute-start | bytes 294920 | tf_op jit(solution)/shard_map/ppermute | solution.py:133
  132.3 6.7 %collective-permute-start.17 = (f32[48,1024]{1,0:T(8,128)S(1)}, f32[48,1024]{1,0:T(8,128)S(1)}, u32[]{:S(2)}, u32[]{:S(2)}) collective-permute-start(f32[48,1024]{1,0:T(8,128)S(1)} %maximum_select_fusion.3), channel_id=1, source_target_pairs={{0,1},{1,0},{2,3},{3,2},{4,5},{5,4},{6,7},{7,6},{8,9},{9,8},{10,11... | collective-permute-start | bytes 589832 | tf_op jit(solution)/shard_map/ppermute | solution.py:133

commit v3 on v2

--- a/solution.py
+++ b/solution.py
@@ -89,9 +89,9 @@
 
 def assemble(new_density, dust_velocity, gas_next, rate):
     dust_next = (dust_velocity + rate[None] * gas_next[:, None]) / (1.0 + rate[None])
-    radial = jnp.concatenate([dust_next[0], gas_next[0][None]], axis=0)
-    azimuth = jnp.concatenate([dust_next[1], gas_next[1][None]], axis=0)
-    return jnp.stack([new_density, radial, azimuth])
+    dust = jnp.concatenate([new_density[None, :-1], dust_next], axis=0)
+    gas = jnp.concatenate([new_density[None, -1], gas_next], axis=0)
+    return dust, gas
 
 
 def xor_pairs(count, bit):
@@ -107,7 +107,7 @@
     count = 1
     for axis in axes:
         count *= lax.axis_size(axis)
-    spread = jnp.broadcast_to(value, (count, 128))
+    spread = jnp.broadcast_to(value, (count,))
     return jnp.max(lax.all_to_all(spread, axes, 0, 0, tiled=True))
 
 
@@ -179,8 +179,9 @@
     )
     for iteration in range(STEPS):
         wide = padded(fluid, (("space", 2),), 2)
-        fluid = advance(wide, 2, tile_rows, stop_times, total_species)
-    return (fluid[:, :local_species], fluid[:, local_species])
+        dust, gas = advance(wide, 2, tile_rows, stop_times, total_species)
+        fluid = jnp.concatenate([dust, gas[:, None]], axis=1)
+    return (dust, gas)
 
 
 def solution(mesh):

time: 142 us -> 142 us (level)
  blocking collectives: 0 us -> 21.3 us
  starting transfers between devices: 49.3 us -> 39 us
  other arithmetic: 25.8 us -> 20.8 us
  waiting for transfers between devices: 59 us -> 54.6 us
  local copies, waits for them, and re-layouts: 5.34 us -> 3.91 us
    all_to_all x0 -> x1, blocking collectives: none -> 21.3 us  [global_max(): return jnp.max(lax.all_to_all(spread, axes, 0, 0, tiled=True))]
    all_to_all x2 -> x1, starting transfers between devices: 22.5 us -> 12.6 us  [global_max(): return jnp.max(lax.all_to_all(spread, axes, 0, 0, tiled=True))]
    all_to_all x2 -> x1, waiting for transfers between devices: 16.6 us -> 12.7 us  [global_max(): return jnp.max(lax.all_to_all(spread, axes, 0, 0, tiled=True))]
    sub x2, other arithmetic: 4.52 us -> 0.73 us  [moved(): new_density = inner_density - step_time * (div_azimuth + div_radial)]
    add x4, other arithmetic: 6.44 us -> 2.84 us  [face_divergence(): jnp.maximum(face_speed, 0.0) * (1.5 * here - 0.5 * back_two)]
    concatenate x0 -> x2, other arithmetic: none -> 2.03 us  [the longest x1 1.25 us: assemble(): dust = jnp.concatenate([new_density[None, :-1], dust_next], axis=0)]
    broadcast_in_dim x0 -> x3, other arithmetic: none -> 1.47 us  [the longest x2 1.45 us: assemble(): dust = jnp.concatenate([new_density[None, :-1], dust_next], axis=0)]
  transfers between devices with their start and end apart: 20 -> 19, of which waited for: 15 -> 14; matrix products, arithmetic and copies ran while one was open for 10% -> 6% of each run, Pallas kernels for 0% -> 0%
where the time goes in v3:
time: 142 us
  waiting for transfers between devices  54.6 us (38%)
  starting transfers between devices  39 us (27%)
  blocking collectives  21.3 us (15%)
  other arithmetic  20.8 us (15%)
  local copies, waits for them, and re-layouts  3.91 us (3%)
  between operations  2.56 us (2%)
    ppermute x6, waiting for transfers between devices, species_sum(): other = lax.ppermute(part, axis, pairs)  25.2 us
    all_to_all x1, blocking collectives, global_max(): return jnp.max(lax.all_to_all(spread, axes, 0, 0, tiled=True))  21.3 us
    all_to_all x1, waiting for transfers between devices, global_max(): return jnp.max(lax.all_to_all(spread, axes, 0, 0, tiled=True))  12.7 us
    all_to_all x1, starting transfers between devices, global_max(): return jnp.max(lax.all_to_all(spread, axes, 0, 0, tiled=True))  12.6 us
    ppermute x4, starting transfers between devices, join_rounds(): other = lax.ppermute(part, axis, xor_pairs(lax.axis_size(axis), bit))  12 us
    ppermute x4, waiting for transfers between devices, split_rounds(): part = keep + lax.ppermute(send, axis, xor_pairs(lax.axis_size(axis), bit))  9.94 us
    ppermute x4, waiting for transfers between devices, join_rounds(): other = lax.ppermute(part, axis, xor_pairs(lax.axis_size(axis), bit))  6.85 us
    ppermute x2, starting transfers between devices, padded(): lax.ppermute(lax.slice_in_dim(block, 0, width, axis=dim), axis, backward)  5.41 us
  transfers between devices with their start and end apart: 19, of which 14 were waited for; matrix products, arithmetic and copies ran while one was open for 6% of the time, Pallas kernels for 0%

profile of v3, /device:TPU:1, one launch (start us, length us, event | category | flops | bytes accessed | tf_op | source)
XLA Modules:
  0.0 142.2 jit_solution(11204098610612914214)
XLA Ops:
  0.7 1.4 %pad_maximum_fusion.26 = (f32[3,5,2,1024]{3,2,1,0:T(2,128)S(1)}, f32[3,5,2,1024]{3,2,1,0:T(2,128)S(1)}) fusion(f32[3,1,32,1024]{3,2,1,0:T(8,128)} %bitcast.75, f32[3,4,32,1024]{3,2,1,0:T(8,128)} %param.3), kind=kLoop, calls=%fused_computation.136 | loop fusion | flops 61440 | bytes 2211840 | tf_op jit(solution)/shard_map/slice | solution.py:23
  2.1 2.2 %collective-permute-start = (f32[3,5,2,1024]{3,2,1,0:T(2,128)S(1)}, f32[3,5,2,1024]{3,2,1,0:T(2,128)S(1)}, u32[]{:S(2)}, u32[]{:S(2)}) collective-permute-start(f32[3,5,2,1024]{3,2,1,0:T(2,128)S(1)} %get-tuple-element.16), channel_id=1, source_target_pairs={{0,32},{32,64},{64,96},{96,128},{128,160},{160,192},{192,224},{224... | collective-permute-start | bytes 368648 | tf_op jit(solution)/shard_map/ppermute | solution.py:22
  4.3 4.0 %collective-permute-start.1 = (f32[3,5,2,1024]{3,2,1,0:T(2,128)S(1)}, f32[3,5,2,1024]{3,2,1,0:T(2,128)S(1)}, u32[]{:S(2)}, u32[]{:S(2)}) collective-permute-start(f32[3,5,2,1024]{3,2,1,0:T(2,128)S(1)} %get-tuple-element.17), channel_id=1, source_target_pairs={{32,0},{64,32},{96,64},{128,96},{160,128},{192,160},{224,192},{0,2... | collective-permute-start | bytes 368648 | tf_op jit(solution)/shard_map/ppermute | solution.py:25
  8.3 0.8 fusion.25
  9.1 1.4 broadcast_in_dim.13
  10.4 12.6 %all-to-all-start = ((f32[256,1,1]{2,1,0:T(1,128)}), f32[256,1,1]{2,1,0:T(1,128)S(1)}, u32[]{:S(2)}, u32[]{:S(2)}) async-start(f32[256,1,1]{2,1,0:T(1,128)} %broadcast_in_dim.13), calls=%async_computation | async-start | bytes 262144 | tf_op jit(solution)/shard_map/all_to_all | solution.py:111
  23.0 12.7 %all-to-all-done = f32[256,1,1]{2,1,0:T(1,128)S(1)} async-done(((f32[256,1,1]{2,1,0:T(1,128)}), f32[256,1,1]{2,1,0:T(1,128)S(1)}, u32[]{:S(2)}, u32[]{:S(2)}) %all-to-all-start) | async-done | bytes 1056 | tf_op jit(solution)/shard_map/all_to_all | solution.py:111
  35.7 0.9 reduce_max.37
  37.3 0.4 pad_maximum_fusion
  37.7 0.2 slice_bitcast_fusion.4
  38.1 0.6 fusion.10
  38.8 0.8 multiply_add_fusion.1
  39.6 0.4 fusion.22
  40.0 0.8 slice_bitcast_fusion.15
  40.7 1.2 slice_bitcast_fusion.11
  42.0 1.2 fusion.49
  43.2 0.7 copy-done.3
  44.0 0.7 slice_select_fusion.1
  44.7 1.0 collective-permute-start.2
  45.7 1.4 collective-permute-done.2
  47.1 1.1 select_add_fusion.1
  48.3 0.4 collective-permute-start.3
  48.6 3.7 %collective-permute-done.3 = f32[24,1024]{1,0:T(8,128)S(1)} collective-permute-done((f32[24,1024]{1,0:T(8,128)S(1)}, f32[24,1024]{1,0:T(8,128)S(1)}, u32[]{:S(2)}, u32[]{:S(2)}) %collective-permute-start.3) | collective-permute-done | bytes 98336 | tf_op jit(solution)/shard_map/ppermute | solution.py:125
  52.4 0.9 collective-permute-start.4
  53.3 2.6 %collective-permute-done.4 = f32[24,1024]{1,0:T(8,128)S(1)} collective-permute-done((f32[24,1024]{1,0:T(8,128)S(1)}, f32[24,1024]{1,0:T(8,128)S(1)}, u32[]{:S(2)}, u32[]{:S(2)}) %collective-permute-start.4) | collective-permute-done | bytes 98336 | tf_op jit(solution)/shard_map/ppermute | solution.py:152
  55.9 0.7 collective-permute-start.5
  56.6 4.8 %collective-permute-done.5 = f32[24,1024]{1,0:T(8,128)S(1)} collective-permute-done((f32[24,1024]{1,0:T(8,128)S(1)}, f32[24,1024]{1,0:T(8,128)S(1)}, u32[]{:S(2)}, u32[]{:S(2)}) %collective-permute-start.5) | collective-permute-done | bytes 98336 | tf_op jit(solution)/shard_map/ppermute | solution.py:152
  61.5 0.2 collective-permute-start.6
  61.7 0.8 slice_bitcast_fusion.14
  62.5 4.7 %collective-permute-done.6 = f32[24,1024]{1,0:T(8,128)S(1)} collective-permute-done((f32[24,1024]{1,0:T(8,128)S(1)}, f32[24,1024]{1,0:T(8,128)S(1)}, u32[]{:S(2)}, u32[]{:S(2)}) %collective-permute-start.6) | collective-permute-done | bytes 98336 | tf_op jit(solution)/shard_map/ppermute | solution.py:152
  67.3 0.4 collective-permute-start.7
  67.7 3.4 %collective-permute-done.7 = f32[24,1024]{1,0:T(8,128)S(1)} collective-permute-done((f32[24,1024]{1,0:T(8,128)S(1)}, f32[24,1024]{1,0:T(8,128)S(1)}, u32[]{:S(2)}, u32[]{:S(2)}) %collective-permute-start.7) | collective-permute-done | bytes 98336 | tf_op jit(solution)/shard_map/ppermute | solution.py:133
  71.2 5.6 %collective-permute-start.8 = (f32[48,1024]{1,0:T(8,128)S(1)}, f32[48,1024]{1,0:T(8,128)S(1)}, u32[]{:S(2)}, u32[]{:S(2)}) collective-permute-start(f32[48,1024]{1,0:T(8,128)S(1)} %maximum_select_fusion.2), channel_id=1, source_target_pairs={{0,1},{1,0},{2,3},{3,2},{4,5},{5,4},{6,7},{7,6},{8,9},{9,8},{10,11... | collective-permute-start | bytes 589832 | tf_op jit(solution)/shard_map/ppermute | solution.py:133
  76.8 1.1 fusion.47
  78.1 0.3 fusion
  78.5 1.4 %collective-permute-start.10 = (f32[3,5,2,1024]{3,2,1,0:T(2,128)S(1)}, f32[3,5,2,1024]{3,2,1,0:T(2,128)S(1)}, u32[]{:S(2)}, u32[]{:S(2)}) collective-permute-start(f32[3,5,2,1024]{3,2,1,0:T(2,128)S(1)} %get-tuple-element.15), channel_id=1, source_target_pairs={{32,0},{64,32},{96,64},{128,96},{160,128},{192,160},{224,192},{0,2... | collective-permute-start | bytes 368648 | tf_op jit(solution)/shard_map/ppermute | solution.py:25
  79.9 0.3 collective-permute-start.9
  80.2 0.8 fusion.19
  81.0 0.7 broadcast_in_dim.32
  81.7 21.3 %all_to_all.12 = f32[256,1,1]{2,1,0:T(1,128)S(1)} all-to-all(f32[256,1,1]{2,1,0:T(1,128)S(1)} %broadcast_in_dim.32), channel_id=1, replica_groups=mesh['space'=8,'species'=32] {'space','species'}, dimensions={0} | all-to-all | bytes 2048 | tf_op jit(solution)/shard_map/all_to_all | solution.py:111
  103.0 0.9 reduce_max.39
  104.6 0.4 pad_maximum_fusion.1
  105.0 0.3 slice_bitcast_fusion.2
  105.4 0.6 fusion.4
  106.1 0.8 multiply_add_fusion
  106.9 0.4 fusion.16
  107.5 0.3 fusion.48
  107.9 1.1 collective-permute-start.11
  108.9 1.1 collective-permute-done.11
  110.1 0.4 collective-permute-start.12
  110.4 3.7 %collective-permute-done.12 = f32[24,1024]{1,0:T(8,128)S(1)} collective-permute-done((f32[24,1024]{1,0:T(8,128)S(1)}, f32[24,1024]{1,0:T(8,128)S(1)}, u32[]{:S(2)}, u32[]{:S(2)}) %collective-permute-start.12) | collective-permute-done | bytes 98336 | tf_op jit(solution)/shard_map/ppermute | solution.py:125
  114.2 0.9 collective-permute-start.13
  115.1 2.6 %collective-permute-done.13 = f32[24,1024]{1,0:T(8,128)S(1)} collective-permute-done((f32[24,1024]{1,0:T(8,128)S(1)}, f32[24,1024]{1,0:T(8,128)S(1)}, u32[]{:S(2)}, u32[]{:S(2)}) %collective-permute-start.13) | collective-permute-done | bytes 98336 | tf_op jit(solution)/shard_map/ppermute | solution.py:152
  117.8 0.7 collective-permute-start.14
  118.4 4.8 %collective-permute-done.14 = f32[24,1024]{1,0:T(8,128)S(1)} collective-permute-done((f32[24,1024]{1,0:T(8,128)S(1)}, f32[24,1024]{1,0:T(8,128)S(1)}, u32[]{:S(2)}, u32[]{:S(2)}) %collective-permute-start.14) | collective-permute-done | bytes 98336 | tf_op jit(solution)/shard_map/ppermute | solution.py:152
  123.3 0.2 collective-permute-start.15
  123.6 5.5 %collective-permute-done.15 = f32[24,1024]{1,0:T(8,128)S(1)} collective-permute-done((f32[24,1024]{1,0:T(8,128)S(1)}, f32[24,1024]{1,0:T(8,128)S(1)}, u32[]{:S(2)}, u32[]{:S(2)}) %collective-permute-start.15) | collective-permute-done | bytes 98336 | tf_op jit(solution)/shard_map/ppermute | solution.py:152
  129.1 0.4 collective-permute-start.16
  129.6 3.3 %collective-permute-done.16 = f32[24,1024]{1,0:T(8,128)S(1)} collective-permute-done((f32[24,1024]{1,0:T(8,128)S(1)}, f32[24,1024]{1,0:T(8,128)S(1)}, u32[]{:S(2)}, u32[]{:S(2)}) %collective-permute-start.16) | collective-permute-done | bytes 98336 | tf_op jit(solution)/shard_map/ppermute | solution.py:133
  133.0 5.6 %collective-permute-start.17 = (f32[48,1024]{1,0:T(8,128)S(1)}, f32[48,1024]{1,0:T(8,128)S(1)}, u32[]{:S(2)}, u32[]{:S(2)}) collective-permute-start(f32[48,1024]{1,0:T(8,128)S(1)} %maximum_select_fusion.3), channel_id=1, source_target_pairs={{0,1},{1,0},{2,3},{3,2},{4,5},{5,4},{6,7},{7,6},{8,9},{9,8},{10,11... | collective-permute-start | bytes 589832 | tf_op jit(solution)/shard_map/ppermute | solution.py:133
  138.6 1.0 fusion.32
  139.8 0.8 pad_maximum_fusion.8
  140.6 0.3 fusion.1
  140.9 1.2 pad_maximum_fusion.2
  (67 shorter events, 1.7 us)
Async XLA Ops:
  0.6 7.7 %copy-start.1 = (f32[3,32,1024]{2,1,0:T(8,128)S(1)}, f32[3,32,1024]{2,1,0:T(8,128)}, u32[]{:S(2)}) copy-start(f32[3,32,1024]{2,1,0:T(8,128)} %param.4) | copy-start | bytes 1179652
  0.6 7.7 %copy-start = (f32[3,4,32,1024]{3,2,1,0:T(8,128)S(1)}, f32[3,4,32,1024]{3,2,1,0:T(8,128)}, u32[]{:S(2)}) copy-start(f32[3,4,32,1024]{3,2,1,0:T(8,128)} %param.3) | copy-start | bytes 4718596
  0.7 22.4 %copy-start.12 = (s32[4]{0:T(128)S(1)}, s32[4]{0:T(128)}, u32[]{:S(2)}) copy-start(s32[4]{0:T(128)} %param.5) | copy-start | bytes 52
  2.1 35.2 %collective-permute-start = (f32[3,5,2,1024]{3,2,1,0:T(2,128)S(1)}, f32[3,5,2,1024]{3,2,1,0:T(2,128)S(1)}, u32[]{:S(2)}, u32[]{:S(2)}) collective-permute-start(f32[3,5,2,1024]{3,2,1,0:T(2,128)S(1)} %get-tuple-element.16), channel_id=1, source_target_pairs={{0,32},{32,64},{64,96},{96,128},{128,160},{160,192},{192,224},{224... | collective-permute-start | bytes 368648 | tf_op jit(solution)/shard_map/ppermute | solution.py:22
  4.3 33.0 %collective-permute-start.1 = (f32[3,5,2,1024]{3,2,1,0:T(2,128)S(1)}, f32[3,5,2,1024]{3,2,1,0:T(2,128)S(1)}, u32[]{:S(2)}, u32[]{:S(2)}) collective-permute-start(f32[3,5,2,1024]{3,2,1,0:T(2,128)S(1)} %get-tuple-element.17), channel_id=1, source_target_pairs={{32,0},{64,32},{96,64},{128,96},{160,128},{192,160},{224,192},{0,2... | collective-permute-start | bytes 368648 | tf_op jit(solution)/shard_map/ppermute | solution.py:25
  10.4 25.3 %all-to-all-start = ((f32[256,1,1]{2,1,0:T(1,128)}), f32[256,1,1]{2,1,0:T(1,128)S(1)}, u32[]{:S(2)}, u32[]{:S(2)}) async-start(f32[256,1,1]{2,1,0:T(1,128)} %broadcast_in_dim.13), calls=%async_computation | async-start | bytes 262144 | tf_op jit(solution)/shard_map/all_to_all | solution.py:111
  37.3 0.7 copy-start.10
  37.3 0.7 copy-start.11
  38.0 4.0 %copy-start.2 = (f32[5,36,1024]{2,1,0:T(8,128)}, f32[5,36,1024]{2,1,0:T(8,128)S(1)}, u32[]{:S(2)}) copy-start(f32[5,36,1024]{2,1,0:T(8,128)S(1)} %get-tuple-element.12) | copy-start | bytes 2211844
  40.0 3.2 %copy-start.4 = (f32[5,32,1024]{2,1,0:T(8,128)}, f32[5,32,1024]{2,1,0:T(8,128)S(1)}, u32[]{:S(2)}) copy-start(f32[5,32,1024]{2,1,0:T(8,128)S(1)} %fusion.22) | copy-start | bytes 1966084
  43.2 0.7 copy-start.3
  44.7 2.4 %collective-permute-start.2 = (f32[48,1024]{1,0:T(8,128)}, f32[48,1024]{1,0:T(8,128)}, u32[]{:S(2)}, u32[]{:S(2)}) collective-permute-start(f32[48,1024]{1,0:T(8,128)} %slice_select_fusion.1), channel_id=1, source_target_pairs={{0,1},{1,0},{2,3},{3,2},{4,5},{5,4},{6,7},{7,6},{8,9},{9,8},{10,11... | collective-permute-start | bytes 589832 | tf_op jit(solution)/shard_map/ppermute | solution.py:125
  48.3 4.1 %collective-permute-start.3 = (f32[24,1024]{1,0:T(8,128)S(1)}, f32[24,1024]{1,0:T(8,128)S(1)}, u32[]{:S(2)}, u32[]{:S(2)}) collective-permute-start(f32[24,1024]{1,0:T(8,128)S(1)} %slice_select_fusion.3), channel_id=1, source_target_pairs={{0,2},{1,3},{2,0},{3,1},{4,6},{5,7},{6,4},{7,5},{8,10},{9,11},{10,... | collective-permute-start | bytes 294920 | tf_op jit(solution)/shard_map/ppermute | solution.py:125
  52.4 3.6 %collective-permute-start.4 = (f32[24,1024]{1,0:T(8,128)S(1)}, f32[24,1024]{1,0:T(8,128)S(1)}, u32[]{:S(2)}, u32[]{:S(2)}) collective-permute-start(f32[24,1024]{1,0:T(8,128)S(1)} %select_add_fusion.3), channel_id=1, source_target_pairs={{0,4},{1,5},{2,6},{3,7},{4,0},{5,1},{6,2},{7,3},{8,12},{9,13},{10,... | collective-permute-start | bytes 294920 | tf_op jit(solution)/shard_map/ppermute | solution.py:152
  55.9 5.5 %collective-permute-start.5 = (f32[24,1024]{1,0:T(8,128)S(1)}, f32[24,1024]{1,0:T(8,128)S(1)}, u32[]{:S(2)}, u32[]{:S(2)}) collective-permute-start(f32[24,1024]{1,0:T(8,128)S(1)} %add.169), channel_id=1, source_target_pairs={{0,8},{1,9},{2,10},{3,11},{4,12},{5,13},{6,14},{7,15},{8,0},{9,1},... | collective-permute-start | bytes 294920 | tf_op jit(solution)/shard_map/ppermute | solution.py:152
  61.5 5.8 %collective-permute-start.6 = (f32[24,1024]{1,0:T(8,128)S(1)}, f32[24,1024]{1,0:T(8,128)S(1)}, u32[]{:S(2)}, u32[]{:S(2)}) collective-permute-start(f32[24,1024]{1,0:T(8,128)S(1)} %add.170), channel_id=1, source_target_pairs={{0,28},{1,29},{2,30},{3,31},{4,24},{5,25},{6,26},{7,27},{8,20},{9,... | collective-permute-start | bytes 294920 | tf_op jit(solution)/shard_map/ppermute | solution.py:152
  62.5 15.5 %copy-start.9 = (f32[1,32,1024]{2,1,0:T(8,128)S(1)}, f32[1,32,1024]{2,1,0:T(8,128)}, u32[]{:S(2)}) copy-start(f32[1,32,1024]{2,1,0:T(8,128)} %get-tuple-element.30) | copy-start | bytes 393220
  62.5 15.6 %copy-start.5 = (f32[4,32,1024]{2,1,0:T(8,128)S(1)}, f32[4,32,1024]{2,1,0:T(8,128)}, u32[]{:S(2)}) copy-start(f32[4,32,1024]{2,1,0:T(8,128)} %get-tuple-element.35) | copy-start | bytes 1572868
  62.5 15.6 %copy-start.6 = (f32[4,32,1024]{2,1,0:T(8,128)S(1)}, f32[4,32,1024]{2,1,0:T(8,128)}, u32[]{:S(2)}) copy-start(f32[4,32,1024]{2,1,0:T(8,128)} %get-tuple-element.36) | copy-start | bytes 1572868
  62.5 15.6 %copy-start.7 = (f32[1,4,32,1024]{3,2,1,0:T(8,128)S(1)}, f32[1,4,32,1024]{3,2,1,0:T(8,128)}, u32[]{:S(2)}) copy-start(f32[1,4,32,1024]{3,2,1,0:T(8,128)} %get-tuple-element.20) | copy-start | bytes 1572868
  62.5 15.6 %copy-start.8 = (f32[1,4,32,1024]{3,2,1,0:T(8,128)S(1)}, f32[1,4,32,1024]{3,2,1,0:T(8,128)}, u32[]{:S(2)}) copy-start(f32[1,4,32,1024]{3,2,1,0:T(8,128)} %get-tuple-element.21) | copy-start | bytes 1572868
  67.3 3.8 %collective-permute-start.7 = (f32[24,1024]{1,0:T(8,128)S(1)}, f32[24,1024]{1,0:T(8,128)S(1)}, u32[]{:S(2)}, u32[]{:S(2)}) collective-permute-start(f32[24,1024]{1,0:T(8,128)S(1)} %add.171), channel_id=1, source_target_pairs={{0,2},{1,3},{2,0},{3,1},{4,6},{5,7},{6,4},{7,5},{8,10},{9,11},{10,... | collective-permute-start | bytes 294920 | tf_op jit(solution)/shard_map/ppermute | solution.py:133
  71.2 6.7 %collective-permute-start.8 = (f32[48,1024]{1,0:T(8,128)S(1)}, f32[48,1024]{1,0:T(8,128)S(1)}, u32[]{:S(2)}, u32[]{:S(2)}) collective-permute-start(f32[48,1024]{1,0:T(8,128)S(1)} %maximum_select_fusion.2), channel_id=1, source_target_pairs={{0,1},{1,0},{2,3},{3,2},{4,5},{5,4},{6,7},{7,6},{8,9},{9,8},{10,11... | collective-permute-start | bytes 589832 | tf_op jit(solution)/shard_map/ppermute | solution.py:133
  78.5 26.1 %collective-permute-start.10 = (f32[3,5,2,1024]{3,2,1,0:T(2,128)S(1)}, f32[3,5,2,1024]{3,2,1,0:T(2,128)S(1)}, u32[]{:S(2)}, u32[]{:S(2)}) collective-permute-start(f32[3,5,2,1024]{3,2,1,0:T(2,128)S(1)} %get-tuple-element.15), channel_id=1, source_target_pairs={{32,0},{64,32},{96,64},{128,96},{160,128},{192,160},{224,192},{0,2... | collective-permute-start | bytes 368648 | tf_op jit(solution)/shard_map/ppermute | solution.py:25
  79.9 24.7 %collective-permute-start.9 = (f32[3,5,2,1024]{3,2,1,0:T(2,128)S(1)}, f32[3,5,2,1024]{3,2,1,0:T(2,128)S(1)}, u32[]{:S(2)}, u32[]{:S(2)}) collective-permute-start(f32[3,5,2,1024]{3,2,1,0:T(2,128)S(1)} %get-tuple-element.14), channel_id=1, source_target_pairs={{0,32},{32,64},{64,96},{96,128},{128,160},{160,192},{192,224},{224... | collective-permute-start | bytes 368648 | tf_op jit(solution)/shard_map/ppermute | solution.py:22
  107.9 2.1 %collective-permute-start.11 = (f32[48,1024]{1,0:T(8,128)S(1)}, f32[48,1024]{1,0:T(8,128)S(1)}, u32[]{:S(2)}, u32[]{:S(2)}) collective-permute-start(f32[48,1024]{1,0:T(8,128)S(1)} %slice_select_fusion), channel_id=1, source_target_pairs={{0,1},{1,0},{2,3},{3,2},{4,5},{5,4},{6,7},{7,6},{8,9},{9,8},{10,11... | collective-permute-start | bytes 589832 | tf_op jit(solution)/shard_map/ppermute | solution.py:125
  110.1 4.1 %collective-permute-start.12 = (f32[24,1024]{1,0:T(8,128)S(1)}, f32[24,1024]{1,0:T(8,128)S(1)}, u32[]{:S(2)}, u32[]{:S(2)}) collective-permute-start(f32[24,1024]{1,0:T(8,128)S(1)} %slice_select_fusion.2), channel_id=1, source_target_pairs={{0,2},{1,3},{2,0},{3,1},{4,6},{5,7},{6,4},{7,5},{8,10},{9,11},{10,... | collective-permute-start | bytes 294920 | tf_op jit(solution)/shard_map/ppermute | solution.py:125
  114.2 3.6 %collective-permute-start.13 = (f32[24,1024]{1,0:T(8,128)S(1)}, f32[24,1024]{1,0:T(8,128)S(1)}, u32[]{:S(2)}, u32[]{:S(2)}) collective-permute-start(f32[24,1024]{1,0:T(8,128)S(1)} %select_add_fusion.2), channel_id=1, source_target_pairs={{0,4},{1,5},{2,6},{3,7},{4,0},{5,1},{6,2},{7,3},{8,12},{9,13},{10,... | collective-permute-start | bytes 294920 | tf_op jit(solution)/shard_map/ppermute | solution.py:152
  117.8 5.5 %collective-permute-start.14 = (f32[24,1024]{1,0:T(8,128)S(1)}, f32[24,1024]{1,0:T(8,128)S(1)}, u32[]{:S(2)}, u32[]{:S(2)}) collective-permute-start(f32[24,1024]{1,0:T(8,128)S(1)} %add.185), channel_id=1, source_target_pairs={{0,8},{1,9},{2,10},{3,11},{4,12},{5,13},{6,14},{7,15},{8,0},{9,1},... | collective-permute-start | bytes 294920 | tf_op jit(solution)/shard_map/ppermute | solution.py:152
  123.3 5.8 %collective-permute-start.15 = (f32[24,1024]{1,0:T(8,128)S(1)}, f32[24,1024]{1,0:T(8,128)S(1)}, u32[]{:S(2)}, u32[]{:S(2)}) collective-permute-start(f32[24,1024]{1,0:T(8,128)S(1)} %add.186), channel_id=1, source_target_pairs={{0,28},{1,29},{2,30},{3,31},{4,24},{5,25},{6,26},{7,27},{8,20},{9,... | collective-permute-start | bytes 294920 | tf_op jit(solution)/shard_map/ppermute | solution.py:152
  129.1 3.8 %collective-permute-start.16 = (f32[24,1024]{1,0:T(8,128)S(1)}, f32[24,1024]{1,0:T(8,128)S(1)}, u32[]{:S(2)}, u32[]{:S(2)}) collective-permute-start(f32[24,1024]{1,0:T(8,128)S(1)} %add.187), channel_id=1, source_target_pairs={{0,2},{1,3},{2,0},{3,1},{4,6},{5,7},{6,4},{7,5},{8,10},{9,11},{10,... | collective-permute-start | bytes 294920 | tf_op jit(solution)/shard_map/ppermute | solution.py:133
  133.0 6.7 %collective-permute-start.17 = (f32[48,1024]{1,0:T(8,128)S(1)}, f32[48,1024]{1,0:T(8,128)S(1)}, u32[]{:S(2)}, u32[]{:S(2)}) collective-permute-start(f32[48,1024]{1,0:T(8,128)S(1)} %maximum_select_fusion.3), channel_id=1, source_target_pairs={{0,1},{1,0},{2,3},{3,2},{4,5},{5,4},{6,7},{7,6},{8,9},{9,8},{10,11... | collective-permute-start | bytes 589832 | tf_op jit(solution)/shard_map/ppermute | solution.py:133

commit v4 on v3

--- a/solution.py
+++ b/solution.py
@@ -1,6 +1,8 @@
 import jax
 import jax.numpy as jnp
 from jax import lax
+from jax.experimental import pallas as pl
+from jax.experimental.pallas import tpu as pltpu
 from jax.sharding import PartitionSpec as P
 
 STEPS = 2
@@ -140,11 +142,13 @@
     return part
 
 
-def species_sum(block, axis):
+def species_sum(block, axis, first_done=()):
     count = lax.axis_size(axis)
     index = lax.axis_index(axis)
     low_bits = [bit for bit in (1, 2) if bit < count]
-    part, done = split_rounds(block, axis, low_bits)
+    taken = [bit for bit, dim in first_done]
+    part, done = split_rounds(block, axis, [bit for bit in low_bits if bit not in taken])
+    done = list(first_done) + done
     block_size = 2 * low_bits[-1] if low_bits else 1
     bit = block_size
     while bit < count:
@@ -156,31 +160,148 @@
     return join_rounds(part, axis, done)
 
 
-def advance(wide, margin, tile_rows, stop_times, total_species):
-    interior = lax.slice_in_dim(wide, margin, margin + tile_rows, axis=2)
-    local_top = jnp.max(jnp.abs(interior[1]) + jnp.abs(interior[2]))
+def drag_kernel(scalars, stop_times, flag, dust, gas, divergence, density_out, keep, send):
+    step_time = scalars[0]
+    total_species = scalars[1]
+    local_species = dust.shape[1]
+    gas_new = gas[0] - step_time * divergence[local_species]
+    density_out[local_species] = gas_new
+    scale = total_species * gas_new
+    sums = [None, None, None]
+    for k in range(local_species):
+        fresh = dust[0, k] - step_time * divergence[k]
+        density_out[k] = fresh
+        rate = step_time * gas_new / stop_times[k]
+        weight = fresh / scale * rate / (1.0 + rate)
+        parts = (weight, weight * dust[1, k], weight * dust[2, k])
+        sums = [p if s is None else s + p for s, p in zip(sums, parts)]
+    rows = gas_new.shape[0]
+    half = rows // 2
+    total_zero, total_radial, total_azimuth = sums
+
+    @pl.when(flag[0] == 0)
+    def _():
+        keep[0:rows] = total_zero
+        keep[rows : rows + half] = total_radial[0:half]
+        send[0:half] = total_radial[half:rows]
+        send[half : half + rows] = total_azimuth
+
+    @pl.when(flag[0] != 0)
+    def _():
+        send[0:rows] = total_zero
+        send[rows : rows + half] = total_radial[0:half]
+        keep[0:half] = total_radial[half:rows]
+        keep[half : half + rows] = total_azimuth
+
+
+def update_kernel(scalars, stop_times, totals, gas_star, density, dust, dust_out, gas_out, top):
+    step_time = scalars[0]
+    local_species = dust.shape[1]
+    rows = gas_star.shape[1]
+    gas_new = density[local_species]
+    relief = 1.0 + totals[0:rows]
+    gas_radial = (gas_star[0] + totals[rows : 2 * rows]) / relief
+    gas_azimuth = (gas_star[1] + totals[2 * rows : 3 * rows]) / relief
+    gas_out[0] = gas_new
+    gas_out[1] = gas_radial
+    gas_out[2] = gas_azimuth
+    fastest = jnp.abs(gas_radial) + jnp.abs(gas_azimuth)
+    for k in range(local_species):
+        rate = step_time * gas_new / stop_times[k]
+        radial = (dust[1, k] + rate * gas_radial) / (1.0 + rate)
+        azimuth = (dust[2, k] + rate * gas_azimuth) / (1.0 + rate)
+        dust_out[0, k] = density[k]
+        dust_out[1, k] = radial
+        dust_out[2, k] = azimuth
+        fastest = jnp.maximum(fastest, jnp.abs(radial) + jnp.abs(azimuth))
+    top[...] = jnp.broadcast_to(jnp.max(fastest, axis=0, keepdims=True), top.shape)
+
+
+def smem():
+    return pl.BlockSpec(memory_space=pltpu.SMEM)
+
+
+def vmem():
+    return pl.BlockSpec(memory_space=pltpu.VMEM)
+
+
+def drag_call(scalars, stop_times, flag, dust, gas, divergence):
+    rows, lanes = gas.shape[1:]
+    f32 = jnp.float32
+    return pl.pallas_call(
+        drag_kernel,
+        out_shape=(
+            jax.ShapeDtypeStruct(divergence.shape, f32),
+            jax.ShapeDtypeStruct((3 * rows // 2, lanes), f32),
+            jax.ShapeDtypeStruct((3 * rows // 2, lanes), f32),
+        ),
+        in_specs=[smem(), smem(), smem(), vmem(), vmem(), vmem()],
+        out_specs=(vmem(), vmem(), vmem()),
+    )(scalars, stop_times, flag, dust, gas, divergence)
+
+
+def update_call(scalars, stop_times, totals, gas_star, density, dust):
+    f32 = jnp.float32
+    return pl.pallas_call(
+        update_kernel,
+        out_shape=(
+            jax.ShapeDtypeStruct(dust.shape, f32),
+            jax.ShapeDtypeStruct((3,) + gas_star.shape[1:], f32),
+            jax.ShapeDtypeStruct((8, gas_star.shape[2]), f32),
+        ),
+        in_specs=[smem(), smem(), vmem(), vmem(), vmem(), vmem()],
+        out_specs=(vmem(), vmem(), vmem()),
+    )(scalars, stop_times, totals, gas_star, density, dust)
+
+
+def transport(wide):
+    density = wide[0]
+    radial = wide[1]
+    azimuth = wide[2]
+    div_azimuth = face_divergence(density, azimuth, 1)
+    inner_density = density[:, 2:-2]
+    inner_radial = radial[:, 2:-2]
+    zero_pad = ((0, 0), (0, 0), (2, 2))
+    div_radial = face_divergence(
+        jnp.pad(inner_density, zero_pad), jnp.pad(inner_radial, zero_pad), 2
+    )
+    gas_density = density[-1]
+    inner_gas = gas_density[2:-2]
+    grad_azimuth = 0.5 * (gas_density[3:-1] - gas_density[1:-3])
+    edge_gas = jnp.pad(inner_gas, ((0, 0), (1, 1)), mode="edge")
+    grad_radial = 0.5 * (edge_gas[:, 2:] - edge_gas[:, :-2])
+    return div_azimuth + div_radial, inner_gas, grad_radial, grad_azimuth
+
+
+def advance(wide, dust, gas, local_top, stop_times, total_species):
+    divergence, inner_gas, grad_radial, grad_azimuth = transport(wide)
     fastest = global_max(local_top, ("space", "species"))
     step_time = courant / (sound_speed + fastest)
-    new_density, gas_velocity, dust_velocity = moved(wide, step_time)
-    rate, terms = drag_terms(new_density, dust_velocity, stop_times, step_time, total_species)
-    shape = terms.shape
-    totals = species_sum(terms.reshape(-1, shape[-1]), "species").reshape(shape)
-    gas_next = coupled_gas(gas_velocity, totals)
-    return assemble(new_density, dust_velocity, gas_next, rate)
+    scalars = jnp.stack([step_time, jnp.float32(total_species)])
+    flag = (lax.axis_index("species") % 2).astype(jnp.int32).reshape(1)
+    density, keep, send = drag_call(scalars, stop_times, flag, dust, gas, divergence)
+    push = step_time * sound_sq / inner_gas
+    gas_star = jnp.stack([gas[1] - push * grad_radial, gas[2] - push * grad_azimuth])
+    part = keep + lax.ppermute(send, "species", xor_pairs(lax.axis_size("species"), 1))
+    totals = species_sum(part, "species", first_done=[(1, 0)])
+    return update_call(scalars, stop_times, totals, gas_star, density, dust)
 
 
 def local(dust_state, gas_state, species_bin):
     local_species = dust_state.shape[1]
     total_species = local_species * lax.axis_size("species")
-    tile_rows = dust_state.shape[2]
-    fluid = jnp.concatenate([dust_state, gas_state[:, None]], axis=1)
     stop_times = stop_floor * jnp.exp(
         stop_span * species_bin.astype(jnp.float32) / (total_species - 1)
     )
+    dust, gas = dust_state, gas_state
+    local_top = jnp.maximum(
+        jnp.max(jnp.abs(dust[1]) + jnp.abs(dust[2])), jnp.max(jnp.abs(gas[1]) + jnp.abs(gas[2]))
+    )
     for iteration in range(STEPS):
+        fluid = jnp.concatenate([dust, gas[:, None]], axis=1)
         wide = padded(fluid, (("space", 2),), 2)
-        dust, gas = advance(wide, 2, tile_rows, stop_times, total_species)
-        fluid = jnp.concatenate([dust, gas[:, None]], axis=1)
+        dust, gas, top = advance(wide, dust, gas, local_top, stop_times, total_species)
+        local_top = jnp.max(top)
     return (dust, gas)
 
 

time: 142 us -> 156 us (1.099)
  Pallas kernels: 0 us -> 12.8 us
  waiting for transfers between devices: 54.6 us -> 43.5 us
  starting transfers between devices: 39 us -> 47.3 us
  blocking collectives: 21.3 us -> 23.9 us
    pallas_call x0 -> x4, Pallas kernels: none -> 12.8 us  [the longest x2 6.68 us: update_call(): pl.pallas_call(update_kernel, out_shape=(jax.ShapeDtypeStruct(dust.shape,...]
    ppermute x6, starting transfers between devices: 3.7 us -> 10.6 us  [species_sum(): other = lax.ppermute(part, axis, pairs)]
    all_to_all x1, waiting for transfers between devices: 12.7 us -> 5.96 us  [global_max(): return jnp.max(lax.all_to_all(spread, axes, 0, 0, tiled=True))]
    ppermute x6, waiting for transfers between devices: 25.2 us -> 20.3 us  [species_sum(): other = lax.ppermute(part, axis, pairs)]
    add x2 -> x4, other arithmetic: 0.02 us -> 4.06 us  [the longest x2 2.15 us: transport(): return (div_azimuth + div_radial, inner_gas, grad_radial, grad_azimuth)]
    reduce_max x2 -> x3, other arithmetic: 1.54 us -> 5.06 us  [the longest x1 2.08 us: local(): jnp.max(jnp.abs(dust[1]) + jnp.abs(dust[2]))]
    all_to_all x1, starting transfers between devices: 12.6 us -> 15.7 us  [global_max(): return jnp.max(lax.all_to_all(spread, axes, 0, 0, tiled=True))]
    all_to_all x1, blocking collectives: 21.3 us -> 23.9 us  [global_max(): return jnp.max(lax.all_to_all(spread, axes, 0, 0, tiled=True))]
  transfers between devices with their start and end apart: 19 -> 19, of which waited for: 14 -> 15; matrix products, arithmetic and copies ran while one was open for 6% -> 6% of each run, Pallas kernels for 0% -> 0%
where the time goes in v4:
time: 156 us
  starting transfers between devices  47.3 us (30%)
  waiting for transfers between devices  43.5 us (28%)
  blocking collectives  23.9 us (15%)
  other arithmetic  22.3 us (14%)
  Pallas kernels  12.8 us (8%)
  between operations  3.57 us (2%)
  local copies, waits for them, and re-layouts  2.4 us (2%)
    all_to_all x1, blocking collectives, global_max(): return jnp.max(lax.all_to_all(spread, axes, 0, 0, tiled=True))  23.9 us
    ppermute x6, waiting for transfers between devices, species_sum(): other = lax.ppermute(part, axis, pairs)  20.3 us
    all_to_all x1, starting transfers between devices, global_max(): return jnp.max(lax.all_to_all(spread, axes, 0, 0, tiled=True))  15.7 us
    ppermute x4, starting transfers between devices, join_rounds(): other = lax.ppermute(part, axis, xor_pairs(lax.axis_size(axis), bit))  11.7 us
    ppermute x6, starting transfers between devices, species_sum(): other = lax.ppermute(part, axis, pairs)  10.6 us
    ppermute x2, waiting for transfers between devices, split_rounds(): part = keep + lax.ppermute(send, axis, xor_pairs(lax.axis_size(axis), bit))  7.46 us
    ppermute x4, waiting for transfers between devices, join_rounds(): other = lax.ppermute(part, axis, xor_pairs(lax.axis_size(axis), bit))  7.2 us
    pallas_call x2, Pallas kernels, update_call(): pl.pallas_call(update_kernel, out_shape=(jax.ShapeDtypeStruct(dust.shape,...  6.68 us
  transfers between devices with their start and end apart: 19, of which 15 were waited for; matrix products, arithmetic and copies ran while one was open for 6% of the time, Pallas kernels for 0%

profile of v4, /device:TPU:1, one launch (start us, length us, event | category | flops | bytes accessed | tf_op | source)
XLA Modules:
  0.0 155.8 jit_solution(1941011339655779925)
XLA Ops:
  0.7 2.1 %add_reduce_fusion = f32[]{:T(128)} fusion(f32[3,4,32,1024]{3,2,1,0:T(8,128)} %dust.3), kind=kLoop, calls=%fused_computation.38 | loop fusion | flops 524287 | bytes 1048580 | tf_op jit(solution)/shard_map/reduce_max | solution.py:298
  2.7 1.6 %fusion.34 = f32[]{:T(128)} fusion(f32[3,32,1024]{2,1,0:T(8,128)} %gas.1), kind=kLoop, calls=%fused_computation.78 | loop fusion | flops 131071 | bytes 262148 | tf_op jit(solution)/shard_map/reduce_max | solution.py:298
  5.7 0.7 broadcast_in_dim.12
  6.4 15.7 %all-to-all-start = ((f32[256,1,1]{2,1,0:T(1,128)}), f32[256,1,1]{2,1,0:T(1,128)S(1)}, u32[]{:S(2)}, u32[]{:S(2)}) async-start(f32[256,1,1]{2,1,0:T(1,128)} %broadcast_in_dim.12), calls=%async_computation | async-start | bytes 262144 | tf_op jit(solution)/shard_map/all_to_all | solution.py:113
  22.1 1.0 pad_maximum_fusion.19
  23.1 5.2 %collective-permute-start.1 = (f32[3,5,2,1024]{3,2,1,0:T(2,128)S(1)}, f32[3,5,2,1024]{3,2,1,0:T(2,128)S(1)}, u32[]{:S(2)}, u32[]{:S(2)}) collective-permute-start(f32[3,5,2,1024]{3,2,1,0:T(2,128)S(1)} %get-tuple-element.33), channel_id=1, source_target_pairs={{32,0},{64,32},{96,64},{128,96},{160,128},{192,160},{224,192},{0,2... | collective-permute-start | bytes 368648 | tf_op jit(solution)/shard_map/ppermute | solution.py:27
  28.3 0.5 exponential_multiply_fusion.stop_times
  28.8 6.0 %all-to-all-done = f32[256,1,1]{2,1,0:T(1,128)S(1)} async-done(((f32[256,1,1]{2,1,0:T(1,128)}), f32[256,1,1]{2,1,0:T(1,128)S(1)}, u32[]{:S(2)}, u32[]{:S(2)}) %all-to-all-start) | async-done | bytes 1056 | tf_op jit(solution)/shard_map/all_to_all | solution.py:113
  34.8 0.9 reduce_max.47
  36.3 0.6 pad_maximum_fusion.21.scalars
  36.9 0.4 pad_maximum_fusion
  37.3 0.3 slice_bitcast_fusion.5
  37.7 0.6 fusion.8
  38.4 0.8 multiply_add_fusion.1
  39.2 1.1 fusion.13.divergence
  40.2 3.1 %shard_map.50 = (f32[5,32,1024]{2,1,0:T(8,128)}, f32[48,1024]{1,0:T(8,128)}, f32[48,1024]{1,0:T(8,128)}) custom-call(f32[2]{0:T(128)} %pad_maximum_fusion.21.scalars, f32[4]{0:T(128)} %exponential_multiply_fusion.stop_times, s32[1]{0:T(128)} %bitcast.3.flag, f32[3,4,32,1024]{3,2,1,0:T(8,128)} %dust.3, f32[3,32,1024]{2,1,0:T(8,128)} %gas.1, ...), custom_call_target="tpu_custom_call" | custom-call | tf_op jit(solution)/shard_map/pallas_call | solution.py:231
  43.3 1.0 collective-permute-start.2
  44.3 1.3 collective-permute-done.2
  45.6 0.9 add.118
  46.5 0.4 collective-permute-start.3
  46.9 3.7 %collective-permute-done.3 = f32[24,1024]{1,0:T(8,128)S(1)} collective-permute-done((f32[24,1024]{1,0:T(8,128)S(1)}, f32[24,1024]{1,0:T(8,128)S(1)}, u32[]{:S(2)}, u32[]{:S(2)}) %collective-permute-start.3) | collective-permute-done | bytes 98336 | tf_op jit(solution)/shard_map/ppermute | solution.py:127
  50.7 1.2 collective-permute-start.4
  51.9 2.3 %collective-permute-done.4 = f32[24,1024]{1,0:T(8,128)S(1)} collective-permute-done((f32[24,1024]{1,0:T(8,128)S(1)}, f32[24,1024]{1,0:T(8,128)S(1)}, u32[]{:S(2)}, u32[]{:S(2)}) %collective-permute-start.4) | collective-permute-done | bytes 98336 | tf_op jit(solution)/shard_map/ppermute | solution.py:156
  54.2 2.4 %collective-permute-start.5 = (f32[24,1024]{1,0:T(8,128)S(1)}, f32[24,1024]{1,0:T(8,128)S(1)}, u32[]{:S(2)}, u32[]{:S(2)}) collective-permute-start(f32[24,1024]{1,0:T(8,128)S(1)} %add.120), channel_id=1, source_target_pairs={{0,8},{1,9},{2,10},{3,11},{4,12},{5,13},{6,14},{7,15},{8,0},{9,1},... | collective-permute-start | bytes 294920 | tf_op jit(solution)/shard_map/ppermute | solution.py:156
  56.6 2.1 %collective-permute-done.5 = f32[24,1024]{1,0:T(8,128)S(1)} collective-permute-done((f32[24,1024]{1,0:T(8,128)S(1)}, f32[24,1024]{1,0:T(8,128)S(1)}, u32[]{:S(2)}, u32[]{:S(2)}) %collective-permute-start.5) | collective-permute-done | bytes 98336 | tf_op jit(solution)/shard_map/ppermute | solution.py:156
  58.7 5.1 %collective-permute-start.6 = (f32[24,1024]{1,0:T(8,128)S(1)}, f32[24,1024]{1,0:T(8,128)S(1)}, u32[]{:S(2)}, u32[]{:S(2)}) collective-permute-start(f32[24,1024]{1,0:T(8,128)S(1)} %add.121), channel_id=1, source_target_pairs={{0,28},{1,29},{2,30},{3,31},{4,24},{5,25},{6,26},{7,27},{8,20},{9,... | collective-permute-start | bytes 294920 | tf_op jit(solution)/shard_map/ppermute | solution.py:156
  63.9 3.0 %collective-permute-done.6 = f32[24,1024]{1,0:T(8,128)S(1)} collective-permute-done((f32[24,1024]{1,0:T(8,128)S(1)}, f32[24,1024]{1,0:T(8,128)S(1)}, u32[]{:S(2)}, u32[]{:S(2)}) %collective-permute-start.6) | collective-permute-done | bytes 98336 | tf_op jit(solution)/shard_map/ppermute | solution.py:156
  66.9 0.4 collective-permute-start.7
  67.3 3.4 %collective-permute-done.7 = f32[24,1024]{1,0:T(8,128)S(1)} collective-permute-done((f32[24,1024]{1,0:T(8,128)S(1)}, f32[24,1024]{1,0:T(8,128)S(1)}, u32[]{:S(2)}, u32[]{:S(2)}) %collective-permute-start.7) | collective-permute-done | bytes 98336 | tf_op jit(solution)/shard_map/ppermute | solution.py:135
  70.8 5.3 %collective-permute-start.8 = (f32[48,1024]{1,0:T(8,128)S(1)}, f32[48,1024]{1,0:T(8,128)S(1)}, u32[]{:S(2)}, u32[]{:S(2)}) collective-permute-start(f32[48,1024]{1,0:T(8,128)S(1)} %maximum_select_fusion.2), channel_id=1, source_target_pairs={{0,1},{1,0},{2,3},{3,2},{4,5},{5,4},{6,7},{7,6},{8,9},{9,8},{10,11... | collective-permute-start | bytes 589832 | tf_op jit(solution)/shard_map/ppermute | solution.py:135
  76.2 0.7 pad_maximum_fusion.2.gas_star
  77.1 0.8 maximum_select_fusion.totals
  77.9 3.4 %shard_map.51 = (f32[3,4,32,1024]{3,2,1,0:T(8,128)}, f32[3,32,1024]{2,1,0:T(8,128)}, f32[8,1024]{1,0:T(8,128)}) custom-call(f32[2]{0:T(128)} %pad_maximum_fusion.21.scalars, f32[4]{0:T(128)} %exponential_multiply_fusion.stop_times, f32[96,1024]{1,0:T(8,128)} %maximum_select_fusion.totals, f32[2,32,1024]{2,1,0:T(8,128)} %pad_maximum_fusion.2.gas_star, ...), custom_call_target="tpu_custom_call" | custom-call | tf_op jit(solution)/shard_map/pallas_call | solution.py:245
  81.3 1.4 pad_maximum_fusion.17
  82.7 0.3 collective-permute-start.10
  83.0 1.3 collective-permute-start.9
  84.3 1.4 reduce_max.48
  85.6 0.7 broadcast_in_dim.14
  86.4 23.9 %all_to_all.12 = f32[256,1,1]{2,1,0:T(1,128)S(1)} all-to-all(f32[256,1,1]{2,1,0:T(1,128)S(1)} %broadcast_in_dim.14), channel_id=1, replica_groups=mesh['space'=8,'species'=32] {'space','species'}, dimensions={0} | all-to-all | bytes 2048 | tf_op jit(solution)/shard_map/all_to_all | solution.py:113
  110.3 0.9 reduce_max.49
  111.8 0.6 pad_maximum_fusion.20.scalars
  112.5 0.4 pad_maximum_fusion.1
  112.8 0.3 slice_bitcast_fusion.2
  113.2 0.6 fusion.2
  113.9 0.8 multiply_add_fusion
  114.7 1.1 fusion.12.divergence
  115.8 3.1 %shard_map.52 = (f32[5,32,1024]{2,1,0:T(8,128)}, f32[48,1024]{1,0:T(8,128)}, f32[48,1024]{1,0:T(8,128)}) custom-call(f32[2]{0:T(128)} %pad_maximum_fusion.20.scalars, f32[4]{0:T(128)} %exponential_multiply_fusion.stop_times, s32[1]{0:T(128)} %bitcast.3.flag, f32[3,4,32,1024]{3,2,1,0:T(8,128)} %get-tuple-element.17.dust, ...), custom_call_target="tpu_custom_call" | custom-call | tf_op jit(solution)/shard_map/pallas_call | solution.py:231
  118.8 1.0 collective-permute-start.11
  119.8 1.3 collective-permute-done.11
  121.1 1.0 add.129
  122.1 0.4 collective-permute-start.12
  122.4 3.7 %collective-permute-done.12 = f32[24,1024]{1,0:T(8,128)S(1)} collective-permute-done((f32[24,1024]{1,0:T(8,128)S(1)}, f32[24,1024]{1,0:T(8,128)S(1)}, u32[]{:S(2)}, u32[]{:S(2)}) %collective-permute-start.12) | collective-permute-done | bytes 98336 | tf_op jit(solution)/shard_map/ppermute | solution.py:127
  126.2 0.9 collective-permute-start.13
  127.1 2.6 %collective-permute-done.13 = f32[24,1024]{1,0:T(8,128)S(1)} collective-permute-done((f32[24,1024]{1,0:T(8,128)S(1)}, f32[24,1024]{1,0:T(8,128)S(1)}, u32[]{:S(2)}, u32[]{:S(2)}) %collective-permute-start.13) | collective-permute-done | bytes 98336 | tf_op jit(solution)/shard_map/ppermute | solution.py:156
  129.8 0.7 collective-permute-start.14
  130.4 4.8 %collective-permute-done.14 = f32[24,1024]{1,0:T(8,128)S(1)} collective-permute-done((f32[24,1024]{1,0:T(8,128)S(1)}, f32[24,1024]{1,0:T(8,128)S(1)}, u32[]{:S(2)}, u32[]{:S(2)}) %collective-permute-start.14) | collective-permute-done | bytes 98336 | tf_op jit(solution)/shard_map/ppermute | solution.py:156
  135.3 0.2 collective-permute-start.15
  135.6 5.5 %collective-permute-done.15 = f32[24,1024]{1,0:T(8,128)S(1)} collective-permute-done((f32[24,1024]{1,0:T(8,128)S(1)}, f32[24,1024]{1,0:T(8,128)S(1)}, u32[]{:S(2)}, u32[]{:S(2)}) %collective-permute-start.15) | collective-permute-done | bytes 98336 | tf_op jit(solution)/shard_map/ppermute | solution.py:156
  141.1 0.4 collective-permute-start.16
  141.6 3.4 %collective-permute-done.16 = f32[24,1024]{1,0:T(8,128)S(1)} collective-permute-done((f32[24,1024]{1,0:T(8,128)S(1)}, f32[24,1024]{1,0:T(8,128)S(1)}, u32[]{:S(2)}, u32[]{:S(2)}) %collective-permute-start.16) | collective-permute-done | bytes 98336 | tf_op jit(solution)/shard_map/ppermute | solution.py:135
  145.0 5.6 %collective-permute-start.17 = (f32[48,1024]{1,0:T(8,128)S(1)}, f32[48,1024]{1,0:T(8,128)S(1)}, u32[]{:S(2)}, u32[]{:S(2)}) collective-permute-start(f32[48,1024]{1,0:T(8,128)S(1)} %maximum_select_fusion.3), channel_id=1, source_target_pairs={{0,1},{1,0},{2,3},{3,2},{4,5},{5,4},{6,7},{7,6},{8,9},{9,8},{10,11... | collective-permute-start | bytes 589832 | tf_op jit(solution)/shard_map/ppermute | solution.py:135
  150.8 0.7 pad_maximum_fusion.3.gas_star
  151.7 0.8 maximum_select_fusion.1.totals
  152.5 3.3 %shard_map.53 = (f32[3,4,32,1024]{3,2,1,0:T(8,128)}, f32[3,32,1024]{2,1,0:T(8,128)}, f32[8,1024]{1,0:T(8,128)}) custom-call(f32[2]{0:T(128)} %pad_maximum_fusion.20.scalars, f32[4]{0:T(128)} %exponential_multiply_fusion.stop_times, f32[96,1024]{1,0:T(8,128)} %maximum_select_fusion.1.totals, f32[2,32,1024]{2,1,0:T(8,128)} %pad_maximum_fusion.3.gas_star, ...), custom_call_target="tpu_custom_call" | custom-call | tf_op jit(solution)/shard_map/pallas_call | solution.py:245
  (47 shorter events, 1.4 us)
Async XLA Ops:
  0.6 21.4 %copy-start = (f32[3,4,32,1024]{3,2,1,0:T(8,128)S(1)}, f32[3,4,32,1024]{3,2,1,0:T(8,128)}, u32[]{:S(2)}) copy-start(f32[3,4,32,1024]{3,2,1,0:T(8,128)} %dust.3) | copy-start | bytes 4718596
  0.6 36.3 %copy-start.4 = (f32[3,32,1024]{2,1,0:T(8,128)S(1)}, f32[3,32,1024]{2,1,0:T(8,128)}, u32[]{:S(2)}) copy-start(f32[3,32,1024]{2,1,0:T(8,128)} %gas.1) | copy-start | bytes 1179652
  0.7 27.6 %copy-start.8 = (s32[4]{0:T(128)S(1)}, s32[4]{0:T(128)}, u32[]{:S(2)}) copy-start(s32[4]{0:T(128)} %param.5) | copy-start | bytes 52
  6.4 28.4 %all-to-all-start = ((f32[256,1,1]{2,1,0:T(1,128)}), f32[256,1,1]{2,1,0:T(1,128)S(1)}, u32[]{:S(2)}, u32[]{:S(2)}) async-start(f32[256,1,1]{2,1,0:T(1,128)} %broadcast_in_dim.12), calls=%async_computation | async-start | bytes 262144 | tf_op jit(solution)/shard_map/all_to_all | solution.py:113
  23.1 13.8 %collective-permute-start.1 = (f32[3,5,2,1024]{3,2,1,0:T(2,128)S(1)}, f32[3,5,2,1024]{3,2,1,0:T(2,128)S(1)}, u32[]{:S(2)}, u32[]{:S(2)}) collective-permute-start(f32[3,5,2,1024]{3,2,1,0:T(2,128)S(1)} %get-tuple-element.33), channel_id=1, source_target_pairs={{32,0},{64,32},{96,64},{128,96},{160,128},{192,160},{224,192},{0,2... | collective-permute-start | bytes 368648 | tf_op jit(solution)/shard_map/ppermute | solution.py:27
  28.3 8.7 %collective-permute-start = (f32[3,5,2,1024]{3,2,1,0:T(2,128)S(1)}, f32[3,5,2,1024]{3,2,1,0:T(2,128)S(1)}, u32[]{:S(2)}, u32[]{:S(2)}) collective-permute-start(f32[3,5,2,1024]{3,2,1,0:T(2,128)S(1)} %get-tuple-element.32), channel_id=1, source_target_pairs={{0,32},{32,64},{64,96},{96,128},{128,160},{160,192},{192,224},{224... | collective-permute-start | bytes 368648 | tf_op jit(solution)/shard_map/ppermute | solution.py:24
  40.2 23.6 %copy-start.1 = (f32[3,4,32,1024]{3,2,1,0:T(8,128)S(1)}, f32[3,4,32,1024]{3,2,1,0:T(8,128)}, u32[]{:S(2)}) copy-start(f32[3,4,32,1024]{3,2,1,0:T(8,128)} %dust.3) | copy-start | bytes 4718596
  40.2 23.6 %copy-start.5 = (f32[3,32,1024]{2,1,0:T(8,128)S(1)}, f32[3,32,1024]{2,1,0:T(8,128)}, u32[]{:S(2)}) copy-start(f32[3,32,1024]{2,1,0:T(8,128)} %gas.1) | copy-start | bytes 1179652
  43.3 2.3 %collective-permute-start.2 = (f32[48,1024]{1,0:T(8,128)}, f32[48,1024]{1,0:T(8,128)S(1)}, u32[]{:S(2)}, u32[]{:S(2)}) collective-permute-start(f32[48,1024]{1,0:T(8,128)} %get-tuple-element.14), channel_id=1, source_target_pairs={{0,1},{1,0},{2,3},{3,2},{4,5},{5,4},{6,7},{7,6},{8,9},{9,8},{10,11... | collective-permute-start | bytes 589832 | tf_op jit(solution)/shard_map/ppermute | solution.py:285
  46.5 4.1 %collective-permute-start.3 = (f32[24,1024]{1,0:T(8,128)S(1)}, f32[24,1024]{1,0:T(8,128)S(1)}, u32[]{:S(2)}, u32[]{:S(2)}) collective-permute-start(f32[24,1024]{1,0:T(8,128)S(1)} %slice_select_fusion.1), channel_id=1, source_target_pairs={{0,2},{1,3},{2,0},{3,1},{4,6},{5,7},{6,4},{7,5},{8,10},{9,11},{10,... | collective-permute-start | bytes 294920 | tf_op jit(solution)/shard_map/ppermute | solution.py:127
  50.7 3.6 %collective-permute-start.4 = (f32[24,1024]{1,0:T(8,128)S(1)}, f32[24,1024]{1,0:T(8,128)S(1)}, u32[]{:S(2)}, u32[]{:S(2)}) collective-permute-start(f32[24,1024]{1,0:T(8,128)S(1)} %select_add_fusion.1), channel_id=1, source_target_pairs={{0,4},{1,5},{2,6},{3,7},{4,0},{5,1},{6,2},{7,3},{8,12},{9,13},{10,... | collective-permute-start | bytes 294920 | tf_op jit(solution)/shard_map/ppermute | solution.py:156
  54.2 4.5 %collective-permute-start.5 = (f32[24,1024]{1,0:T(8,128)S(1)}, f32[24,1024]{1,0:T(8,128)S(1)}, u32[]{:S(2)}, u32[]{:S(2)}) collective-permute-start(f32[24,1024]{1,0:T(8,128)S(1)} %add.120), channel_id=1, source_target_pairs={{0,8},{1,9},{2,10},{3,11},{4,12},{5,13},{6,14},{7,15},{8,0},{9,1},... | collective-permute-start | bytes 294920 | tf_op jit(solution)/shard_map/ppermute | solution.py:156
  58.7 8.2 %collective-permute-start.6 = (f32[24,1024]{1,0:T(8,128)S(1)}, f32[24,1024]{1,0:T(8,128)S(1)}, u32[]{:S(2)}, u32[]{:S(2)}) collective-permute-start(f32[24,1024]{1,0:T(8,128)S(1)} %add.121), channel_id=1, source_target_pairs={{0,28},{1,29},{2,30},{3,31},{4,24},{5,25},{6,26},{7,27},{8,20},{9,... | collective-permute-start | bytes 294920 | tf_op jit(solution)/shard_map/ppermute | solution.py:156
  66.9 3.8 %collective-permute-start.7 = (f32[24,1024]{1,0:T(8,128)S(1)}, f32[24,1024]{1,0:T(8,128)S(1)}, u32[]{:S(2)}, u32[]{:S(2)}) collective-permute-start(f32[24,1024]{1,0:T(8,128)S(1)} %add.122), channel_id=1, source_target_pairs={{0,2},{1,3},{2,0},{3,1},{4,6},{5,7},{6,4},{7,5},{8,10},{9,11},{10,... | collective-permute-start | bytes 294920 | tf_op jit(solution)/shard_map/ppermute | solution.py:135
  70.8 6.4 %collective-permute-start.8 = (f32[48,1024]{1,0:T(8,128)S(1)}, f32[48,1024]{1,0:T(8,128)S(1)}, u32[]{:S(2)}, u32[]{:S(2)}) collective-permute-start(f32[48,1024]{1,0:T(8,128)S(1)} %maximum_select_fusion.2), channel_id=1, source_target_pairs={{0,1},{1,0},{2,3},{3,2},{4,5},{5,4},{6,7},{7,6},{8,9},{9,8},{10,11... | collective-permute-start | bytes 589832 | tf_op jit(solution)/shard_map/ppermute | solution.py:135
  81.3 31.2 %copy-start.2 = (f32[3,4,32,1024]{3,2,1,0:T(8,128)S(1)}, f32[3,4,32,1024]{3,2,1,0:T(8,128)}, u32[]{:S(2)}) copy-start(f32[3,4,32,1024]{3,2,1,0:T(8,128)} %get-tuple-element.17.dust) | copy-start | bytes 4718596
  81.3 31.2 %copy-start.6 = (f32[3,32,1024]{2,1,0:T(8,128)S(1)}, f32[3,32,1024]{2,1,0:T(8,128)}, u32[]{:S(2)}) copy-start(f32[3,32,1024]{2,1,0:T(8,128)} %get-tuple-element.18.gas) | copy-start | bytes 1179652
  82.7 29.7 %collective-permute-start.10 = (f32[3,5,2,1024]{3,2,1,0:T(2,128)S(1)}, f32[3,5,2,1024]{3,2,1,0:T(2,128)S(1)}, u32[]{:S(2)}, u32[]{:S(2)}) collective-permute-start(f32[3,5,2,1024]{3,2,1,0:T(2,128)S(1)} %get-tuple-element.31), channel_id=1, source_target_pairs={{32,0},{64,32},{96,64},{128,96},{160,128},{192,160},{224,192},{0,2... | collective-permute-start | bytes 368648 | tf_op jit(solution)/shard_map/ppermute | solution.py:27
  83.0 29.4 %collective-permute-start.9 = (f32[3,5,2,1024]{3,2,1,0:T(2,128)S(1)}, f32[3,5,2,1024]{3,2,1,0:T(2,128)S(1)}, u32[]{:S(2)}, u32[]{:S(2)}) collective-permute-start(f32[3,5,2,1024]{3,2,1,0:T(2,128)S(1)} %get-tuple-element.30), channel_id=1, source_target_pairs={{0,32},{32,64},{64,96},{96,128},{128,160},{160,192},{192,224},{224... | collective-permute-start | bytes 368648 | tf_op jit(solution)/shard_map/ppermute | solution.py:24
  115.8 19.8 %copy-start.3 = (f32[3,4,32,1024]{3,2,1,0:T(8,128)S(1)}, f32[3,4,32,1024]{3,2,1,0:T(8,128)}, u32[]{:S(2)}) copy-start(f32[3,4,32,1024]{3,2,1,0:T(8,128)} %get-tuple-element.17.dust) | copy-start | bytes 4718596
  115.8 19.8 %copy-start.7 = (f32[3,32,1024]{2,1,0:T(8,128)S(1)}, f32[3,32,1024]{2,1,0:T(8,128)}, u32[]{:S(2)}) copy-start(f32[3,32,1024]{2,1,0:T(8,128)} %get-tuple-element.18.gas) | copy-start | bytes 1179652
  118.8 2.3 %collective-permute-start.11 = (f32[48,1024]{1,0:T(8,128)}, f32[48,1024]{1,0:T(8,128)S(1)}, u32[]{:S(2)}, u32[]{:S(2)}) collective-permute-start(f32[48,1024]{1,0:T(8,128)} %get-tuple-element.20), channel_id=1, source_target_pairs={{0,1},{1,0},{2,3},{3,2},{4,5},{5,4},{6,7},{7,6},{8,9},{9,8},{10,11... | collective-permute-start | bytes 589832 | tf_op jit(solution)/shard_map/ppermute | solution.py:285
  122.1 4.1 %collective-permute-start.12 = (f32[24,1024]{1,0:T(8,128)S(1)}, f32[24,1024]{1,0:T(8,128)S(1)}, u32[]{:S(2)}, u32[]{:S(2)}) collective-permute-start(f32[24,1024]{1,0:T(8,128)S(1)} %slice_select_fusion), channel_id=1, source_target_pairs={{0,2},{1,3},{2,0},{3,1},{4,6},{5,7},{6,4},{7,5},{8,10},{9,11},{10,... | collective-permute-start | bytes 294920 | tf_op jit(solution)/shard_map/ppermute | solution.py:127
  126.2 3.6 %collective-permute-start.13 = (f32[24,1024]{1,0:T(8,128)S(1)}, f32[24,1024]{1,0:T(8,128)S(1)}, u32[]{:S(2)}, u32[]{:S(2)}) collective-permute-start(f32[24,1024]{1,0:T(8,128)S(1)} %select_add_fusion), channel_id=1, source_target_pairs={{0,4},{1,5},{2,6},{3,7},{4,0},{5,1},{6,2},{7,3},{8,12},{9,13},{10,... | collective-permute-start | bytes 294920 | tf_op jit(solution)/shard_map/ppermute | solution.py:156
  129.8 5.5 %collective-permute-start.14 = (f32[24,1024]{1,0:T(8,128)S(1)}, f32[24,1024]{1,0:T(8,128)S(1)}, u32[]{:S(2)}, u32[]{:S(2)}) collective-permute-start(f32[24,1024]{1,0:T(8,128)S(1)} %add.131), channel_id=1, source_target_pairs={{0,8},{1,9},{2,10},{3,11},{4,12},{5,13},{6,14},{7,15},{8,0},{9,1},... | collective-permute-start | bytes 294920 | tf_op jit(solution)/shard_map/ppermute | solution.py:156
  135.3 5.8 %collective-permute-start.15 = (f32[24,1024]{1,0:T(8,128)S(1)}, f32[24,1024]{1,0:T(8,128)S(1)}, u32[]{:S(2)}, u32[]{:S(2)}) collective-permute-start(f32[24,1024]{1,0:T(8,128)S(1)} %add.132), channel_id=1, source_target_pairs={{0,28},{1,29},{2,30},{3,31},{4,24},{5,25},{6,26},{7,27},{8,20},{9,... | collective-permute-start | bytes 294920 | tf_op jit(solution)/shard_map/ppermute | solution.py:156
  141.1 3.8 %collective-permute-start.16 = (f32[24,1024]{1,0:T(8,128)S(1)}, f32[24,1024]{1,0:T(8,128)S(1)}, u32[]{:S(2)}, u32[]{:S(2)}) collective-permute-start(f32[24,1024]{1,0:T(8,128)S(1)} %add.133), channel_id=1, source_target_pairs={{0,2},{1,3},{2,0},{3,1},{4,6},{5,7},{6,4},{7,5},{8,10},{9,11},{10,... | collective-permute-start | bytes 294920 | tf_op jit(solution)/shard_map/ppermute | solution.py:135
  145.0 6.7 %collective-permute-start.17 = (f32[48,1024]{1,0:T(8,128)S(1)}, f32[48,1024]{1,0:T(8,128)S(1)}, u32[]{:S(2)}, u32[]{:S(2)}) collective-permute-start(f32[48,1024]{1,0:T(8,128)S(1)} %maximum_select_fusion.3), channel_id=1, source_target_pairs={{0,1},{1,0},{2,3},{3,2},{4,5},{5,4},{6,7},{7,6},{8,9},{9,8},{10,11... | collective-permute-start | bytes 589832 | tf_op jit(solution)/shard_map/ppermute | solution.py:135

commit v5 on v3

--- a/solution.py
+++ b/solution.py
@@ -140,11 +140,13 @@
     return part
 
 
-def species_sum(block, axis):
+def species_sum(block, axis, first_done=()):
     count = lax.axis_size(axis)
     index = lax.axis_index(axis)
     low_bits = [bit for bit in (1, 2) if bit < count]
-    part, done = split_rounds(block, axis, low_bits)
+    taken = [bit for bit, dim in first_done]
+    part, done = split_rounds(block, axis, [bit for bit in low_bits if bit not in taken])
+    done = list(first_done) + done
     block_size = 2 * low_bits[-1] if low_bits else 1
     bit = block_size
     while bit < count:
@@ -156,31 +158,88 @@
     return join_rounds(part, axis, done)
 
 
-def advance(wide, margin, tile_rows, stop_times, total_species):
-    interior = lax.slice_in_dim(wide, margin, margin + tile_rows, axis=2)
-    local_top = jnp.max(jnp.abs(interior[1]) + jnp.abs(interior[2]))
+def drag_sums(step_time, stop_times, upper, dust, gas, divergence, total_species):
+    local_species = dust.shape[1]
+    gas_new = gas[0] - step_time * divergence[local_species]
+    fresh = dust[0] - step_time * divergence[:local_species]
+    rate = step_time * gas_new[None] / stop_times[:, None, None]
+    weight = fresh / (total_species * gas_new[None]) * rate / (1.0 + rate)
+    totals = jnp.concatenate(
+        [jnp.sum(weight, 0), jnp.sum(weight * dust[1], 0), jnp.sum(weight * dust[2], 0)], axis=0
+    )
+    half = totals.shape[0] // 2
+    low, high = totals[:half], totals[half:]
+    keep = jnp.where(upper, high, low)
+    send = jnp.where(upper, low, high)
+    density = jnp.concatenate([fresh, gas_new[None]], axis=0)
+    return density, keep, send
+
+
+def updated(step_time, stop_times, totals, gas_star, density, dust):
+    local_species = dust.shape[1]
+    rows = gas_star.shape[1]
+    gas_new = density[local_species]
+    relief = 1.0 + totals[0:rows]
+    gas_velocity = jnp.stack(
+        [(gas_star[0] + totals[rows : 2 * rows]) / relief, (gas_star[1] + totals[2 * rows :]) / relief]
+    )
+    rate = step_time * gas_new[None] / stop_times[:, None, None]
+    dust_velocity = (dust[1:] + rate[None] * gas_velocity[:, None]) / (1.0 + rate[None])
+    dust_next = jnp.concatenate([density[None, :local_species], dust_velocity], axis=0)
+    gas_next = jnp.concatenate([gas_new[None], gas_velocity], axis=0)
+    speed = jnp.maximum(
+        jnp.max(jnp.abs(dust_velocity[0]) + jnp.abs(dust_velocity[1])),
+        jnp.max(jnp.abs(gas_velocity[0]) + jnp.abs(gas_velocity[1])),
+    )
+    return dust_next, gas_next, speed
+
+
+def transport(wide):
+    density = wide[0]
+    radial = wide[1]
+    azimuth = wide[2]
+    div_azimuth = face_divergence(density, azimuth, 1)
+    inner_density = density[:, 2:-2]
+    inner_radial = radial[:, 2:-2]
+    zero_pad = ((0, 0), (0, 0), (2, 2))
+    div_radial = face_divergence(
+        jnp.pad(inner_density, zero_pad), jnp.pad(inner_radial, zero_pad), 2
+    )
+    gas_density = density[-1]
+    inner_gas = gas_density[2:-2]
+    grad_azimuth = 0.5 * (gas_density[3:-1] - gas_density[1:-3])
+    edge_gas = jnp.pad(inner_gas, ((0, 0), (1, 1)), mode="edge")
+    grad_radial = 0.5 * (edge_gas[:, 2:] - edge_gas[:, :-2])
+    return div_azimuth + div_radial, inner_gas, grad_radial, grad_azimuth
+
+
+def advance(wide, dust, gas, local_top, stop_times, total_species):
+    divergence, inner_gas, grad_radial, grad_azimuth = transport(wide)
     fastest = global_max(local_top, ("space", "species"))
     step_time = courant / (sound_speed + fastest)
-    new_density, gas_velocity, dust_velocity = moved(wide, step_time)
-    rate, terms = drag_terms(new_density, dust_velocity, stop_times, step_time, total_species)
-    shape = terms.shape
-    totals = species_sum(terms.reshape(-1, shape[-1]), "species").reshape(shape)
-    gas_next = coupled_gas(gas_velocity, totals)
-    return assemble(new_density, dust_velocity, gas_next, rate)
+    upper = lax.axis_index("species") % 2 == 1
+    density, keep, send = drag_sums(step_time, stop_times, upper, dust, gas, divergence, total_species)
+    push = step_time * sound_sq / inner_gas
+    gas_star = jnp.stack([gas[1] - push * grad_radial, gas[2] - push * grad_azimuth])
+    part = keep + lax.ppermute(send, "species", xor_pairs(lax.axis_size("species"), 1))
+    totals = species_sum(part, "species", first_done=[(1, 0)])
+    return updated(step_time, stop_times, totals, gas_star, density, dust)
 
 
 def local(dust_state, gas_state, species_bin):
     local_species = dust_state.shape[1]
     total_species = local_species * lax.axis_size("species")
-    tile_rows = dust_state.shape[2]
-    fluid = jnp.concatenate([dust_state, gas_state[:, None]], axis=1)
     stop_times = stop_floor * jnp.exp(
         stop_span * species_bin.astype(jnp.float32) / (total_species - 1)
     )
+    dust, gas = dust_state, gas_state
+    local_top = jnp.maximum(
+        jnp.max(jnp.abs(dust[1]) + jnp.abs(dust[2])), jnp.max(jnp.abs(gas[1]) + jnp.abs(gas[2]))
+    )
     for iteration in range(STEPS):
+        fluid = jnp.concatenate([dust, gas[:, None]], axis=1)
         wide = padded(fluid, (("space", 2),), 2)
-        dust, gas = advance(wide, 2, tile_rows, stop_times, total_species)
-        fluid = jnp.concatenate([dust, gas[:, None]], axis=1)
+        dust, gas, local_top = advance(wide, dust, gas, local_top, stop_times, total_species)
     return (dust, gas)
 
 

time: 142 us -> 147 us (1.035)
  between operations: 2.56 us -> 5.06 us
  waiting for transfers between devices: 54.6 us -> 56.7 us
    ppermute x4 -> x2, waiting for transfers between devices: 9.94 us -> 7.29 us  [split_rounds(): part = keep + lax.ppermute(send, axis, xor_pairs(lax.axis_size(axis), bit))]
    ppermute x0 -> x2, waiting for transfers between devices: none -> 2.48 us  [advance(): lax.ppermute(send, 'species', xor_pairs(lax.axis_size('species'), 1))]
    ppermute x0 -> x2, starting transfers between devices: none -> 2.25 us  [advance(): lax.ppermute(send, 'species', xor_pairs(lax.axis_size('species'), 1))]
    div x4 -> x7, other arithmetic: 0.65 us -> 2.6 us  [the longest x3 1.94 us: drag_sums(): weight = fresh / (total_species * gas_new[None]) * rate / (1.0 + rate)]
    ppermute x4, waiting for transfers between devices: 6.85 us -> 8.79 us  [join_rounds(): other = lax.ppermute(part, axis, xor_pairs(lax.axis_size(axis), bit))]
    ppermute x4 -> x2, starting transfers between devices: 2.78 us -> 0.9 us  [split_rounds(): part = keep + lax.ppermute(send, axis, xor_pairs(lax.axis_size(axis), bit))]
    sub x3 -> x0, other arithmetic: 1.7 us -> none  [the longest x1 0.97 us: moved(): azimuth[-1, 2:-2] - push * grad_azimuth]
    slice x3 -> x0, other arithmetic: 1.57 us -> none  [the longest x2 1.54 us: moved(): inner_gas = gas_density[2:-2]]
  transfers between devices with their start and end apart: 19 -> 19, of which waited for: 14 -> 15; matrix products, arithmetic and copies ran while one was open for 6% -> 4% of each run, Pallas kernels for 0% -> 0%
where the time goes in v5:
time: 147 us
  waiting for transfers between devices  56.7 us (39%)
  starting transfers between devices  39.9 us (27%)
  blocking collectives  21.3 us (14%)
  other arithmetic  21.1 us (14%)
  between operations  5.06 us (3%)
  local copies, waits for them, and re-layouts  2.48 us (2%)
    ppermute x6, waiting for transfers between devices, species_sum(): other = lax.ppermute(part, axis, pairs)  25.4 us
    all_to_all x1, blocking collectives, global_max(): return jnp.max(lax.all_to_all(spread, axes, 0, 0, tiled=True))  21.3 us
    all_to_all x1, waiting for transfers between devices, global_max(): return jnp.max(lax.all_to_all(spread, axes, 0, 0, tiled=True))  12.7 us
    all_to_all x1, starting transfers between devices, global_max(): return jnp.max(lax.all_to_all(spread, axes, 0, 0, tiled=True))  12.6 us
    ppermute x4, starting transfers between devices, join_rounds(): other = lax.ppermute(part, axis, xor_pairs(lax.axis_size(axis), bit))  12.2 us
    ppermute x4, waiting for transfers between devices, join_rounds(): other = lax.ppermute(part, axis, xor_pairs(lax.axis_size(axis), bit))  8.79 us
    ppermute x2, waiting for transfers between devices, split_rounds(): part = keep + lax.ppermute(send, axis, xor_pairs(lax.axis_size(axis), bit))  7.29 us
    ppermute x2, starting transfers between devices, padded(): lax.ppermute(lax.slice_in_dim(block, 0, width, axis=dim), axis, backward)  5.15 us
  transfers between devices with their start and end apart: 19, of which 15 were waited for; matrix products, arithmetic and copies ran while one was open for 4% of the time, Pallas kernels for 0%

profile of v5, /device:TPU:1, one launch (start us, length us, event | category | flops | bytes accessed | tf_op | source)
XLA Modules:
  0.0 146.6 jit_solution(16889925125285595374)
XLA Ops:
  0.7 1.4 pad_maximum_fusion.28
  2.1 2.2 %collective-permute-start = (f32[3,5,2,1024]{3,2,1,0:T(2,128)S(1)}, f32[3,5,2,1024]{3,2,1,0:T(2,128)S(1)}, u32[]{:S(2)}, u32[]{:S(2)}) collective-permute-start(f32[3,5,2,1024]{3,2,1,0:T(2,128)S(1)} %get-tuple-element.25), channel_id=1, source_target_pairs={{0,32},{32,64},{64,96},{96,128},{128,160},{160,192},{192,224},{224... | collective-permute-start | bytes 368648 | tf_op jit(solution)/shard_map/ppermute | solution.py:22
  4.3 4.0 %collective-permute-start.1 = (f32[3,5,2,1024]{3,2,1,0:T(2,128)S(1)}, f32[3,5,2,1024]{3,2,1,0:T(2,128)S(1)}, u32[]{:S(2)}, u32[]{:S(2)}) collective-permute-start(f32[3,5,2,1024]{3,2,1,0:T(2,128)S(1)} %get-tuple-element.26), channel_id=1, source_target_pairs={{32,0},{64,32},{96,64},{128,96},{160,128},{192,160},{224,192},{0,2... | collective-permute-start | bytes 368648 | tf_op jit(solution)/shard_map/ppermute | solution.py:25
  8.3 0.7 fusion.17
  9.0 0.6 fusion.48
  11.0 0.7 broadcast_in_dim.12
  11.7 12.6 %all-to-all-start = ((f32[256,1,1]{2,1,0:T(1,128)}), f32[256,1,1]{2,1,0:T(1,128)S(1)}, u32[]{:S(2)}, u32[]{:S(2)}) async-start(f32[256,1,1]{2,1,0:T(1,128)} %broadcast_in_dim.12), calls=%async_computation | async-start | bytes 262144 | tf_op jit(solution)/shard_map/all_to_all | solution.py:111
  24.3 12.7 %all-to-all-done = f32[256,1,1]{2,1,0:T(1,128)S(1)} async-done(((f32[256,1,1]{2,1,0:T(1,128)}), f32[256,1,1]{2,1,0:T(1,128)S(1)}, u32[]{:S(2)}, u32[]{:S(2)}) %all-to-all-start) | async-done | bytes 1056 | tf_op jit(solution)/shard_map/all_to_all | solution.py:111
  37.0 0.9 reduce_max.56
  38.6 0.4 pad_maximum_fusion
  39.0 0.3 slice_bitcast_fusion.5
  39.3 0.6 fusion.8
  40.0 0.8 multiply_add_fusion.1
  40.8 0.2 fusion.13
  41.1 0.7 multiply_bitcast_fusion.2
  41.8 1.2 multiply_divide_fusion.1
  43.2 0.7 fusion.49
  43.9 1.0 collective-permute-start.2
  44.9 1.4 collective-permute-done.2
  46.3 1.0 select_add_fusion.1
  47.3 0.4 collective-permute-start.3
  47.7 3.7 %collective-permute-done.3 = f32[24,1024]{1,0:T(8,128)S(1)} collective-permute-done((f32[24,1024]{1,0:T(8,128)S(1)}, f32[24,1024]{1,0:T(8,128)S(1)}, u32[]{:S(2)}, u32[]{:S(2)}) %collective-permute-start.3) | collective-permute-done | bytes 98336 | tf_op jit(solution)/shard_map/ppermute | solution.py:125
  51.4 0.9 collective-permute-start.4
  52.3 2.6 %collective-permute-done.4 = f32[24,1024]{1,0:T(8,128)S(1)} collective-permute-done((f32[24,1024]{1,0:T(8,128)S(1)}, f32[24,1024]{1,0:T(8,128)S(1)}, u32[]{:S(2)}, u32[]{:S(2)}) %collective-permute-start.4) | collective-permute-done | bytes 98336 | tf_op jit(solution)/shard_map/ppermute | solution.py:154
  55.0 0.7 collective-permute-start.5
  55.6 4.8 %collective-permute-done.5 = f32[24,1024]{1,0:T(8,128)S(1)} collective-permute-done((f32[24,1024]{1,0:T(8,128)S(1)}, f32[24,1024]{1,0:T(8,128)S(1)}, u32[]{:S(2)}, u32[]{:S(2)}) %collective-permute-start.5) | collective-permute-done | bytes 98336 | tf_op jit(solution)/shard_map/ppermute | solution.py:154
  60.7 5.6 %collective-permute-done.6 = f32[24,1024]{1,0:T(8,128)S(1)} collective-permute-done((f32[24,1024]{1,0:T(8,128)S(1)}, f32[24,1024]{1,0:T(8,128)S(1)}, u32[]{:S(2)}, u32[]{:S(2)}) %collective-permute-start.6) | collective-permute-done | bytes 98336 | tf_op jit(solution)/shard_map/ppermute | solution.py:154
  66.3 0.4 collective-permute-start.7
  66.7 3.5 %collective-permute-done.7 = f32[24,1024]{1,0:T(8,128)S(1)} collective-permute-done((f32[24,1024]{1,0:T(8,128)S(1)}, f32[24,1024]{1,0:T(8,128)S(1)}, u32[]{:S(2)}, u32[]{:S(2)}) %collective-permute-start.7) | collective-permute-done | bytes 98336 | tf_op jit(solution)/shard_map/ppermute | solution.py:133
  70.2 5.6 %collective-permute-start.8 = (f32[48,1024]{1,0:T(8,128)S(1)}, f32[48,1024]{1,0:T(8,128)S(1)}, u32[]{:S(2)}, u32[]{:S(2)}) collective-permute-start(f32[48,1024]{1,0:T(8,128)S(1)} %maximum_select_fusion.2), channel_id=1, source_target_pairs={{0,1},{1,0},{2,3},{3,2},{4,5},{5,4},{6,7},{7,6},{8,9},{9,8},{10,11... | collective-permute-start | bytes 589832 | tf_op jit(solution)/shard_map/ppermute | solution.py:133
  75.9 1.0 collective-permute-done.8
  77.0 0.7 add_reduce_fusion.1
  77.8 0.6 copy-done.10
  78.4 0.2 add_divide_fusion.1
  78.7 0.8 pad_maximum_fusion.26
  79.5 1.2 collective-permute-start.10
  80.6 0.3 collective-permute-start.9
  80.9 0.8 add_reduce_fusion
  83.1 21.3 %all_to_all.12 = f32[256,1,1]{2,1,0:T(1,128)} all-to-all(f32[256,1,1]{2,1,0:T(1,128)S(1)} %broadcast_in_dim.14), channel_id=1, replica_groups=mesh['space'=8,'species'=32] {'space','species'}, dimensions={0} | all-to-all | bytes 2048 | tf_op jit(solution)/shard_map/all_to_all | solution.py:111
  104.4 1.8 %reduce_max.59 = f32[]{:T(128)} reduce(f32[256,1,1]{2,1,0:T(1,128)} %all_to_all.12, f32[]{:T(128)} %constant.108.clone.1), dimensions={0,1,2}, to_apply=%region_8.9 | reduce | flops 255 | bytes 1032 | tf_op jit(solution)/shard_map/reduce_max | solution.py:111
  106.8 1.3 pad_maximum_fusion.1
  108.2 0.3 slice_bitcast_fusion.2
  108.6 0.6 fusion.2
  109.3 0.8 multiply_add_fusion
  110.1 0.2 fusion.12
  110.4 0.3 fusion.20
  110.9 1.3 collective-permute-start.11
  112.1 1.1 collective-permute-done.11
  113.3 0.5 collective-permute-start.12
  113.8 3.6 %collective-permute-done.12 = f32[24,1024]{1,0:T(8,128)S(1)} collective-permute-done((f32[24,1024]{1,0:T(8,128)S(1)}, f32[24,1024]{1,0:T(8,128)S(1)}, u32[]{:S(2)}, u32[]{:S(2)}) %collective-permute-start.12) | collective-permute-done | bytes 98336 | tf_op jit(solution)/shard_map/ppermute | solution.py:125
  117.4 0.8 collective-permute-start.13
  118.2 2.8 %collective-permute-done.13 = f32[24,1024]{1,0:T(8,128)S(1)} collective-permute-done((f32[24,1024]{1,0:T(8,128)S(1)}, f32[24,1024]{1,0:T(8,128)S(1)}, u32[]{:S(2)}, u32[]{:S(2)}) %collective-permute-start.13) | collective-permute-done | bytes 98336 | tf_op jit(solution)/shard_map/ppermute | solution.py:154
  121.0 1.1 collective-permute-start.14
  122.0 4.4 %collective-permute-done.14 = f32[24,1024]{1,0:T(8,128)S(1)} collective-permute-done((f32[24,1024]{1,0:T(8,128)S(1)}, f32[24,1024]{1,0:T(8,128)S(1)}, u32[]{:S(2)}, u32[]{:S(2)}) %collective-permute-start.14) | collective-permute-done | bytes 98336 | tf_op jit(solution)/shard_map/ppermute | solution.py:154
  126.5 0.6 collective-permute-start.15
  127.1 5.2 %collective-permute-done.15 = f32[24,1024]{1,0:T(8,128)S(1)} collective-permute-done((f32[24,1024]{1,0:T(8,128)S(1)}, f32[24,1024]{1,0:T(8,128)S(1)}, u32[]{:S(2)}, u32[]{:S(2)}) %collective-permute-start.15) | collective-permute-done | bytes 98336 | tf_op jit(solution)/shard_map/ppermute | solution.py:154
  132.3 0.5 collective-permute-start.16
  132.9 3.3 %collective-permute-done.16 = f32[24,1024]{1,0:T(8,128)S(1)} collective-permute-done((f32[24,1024]{1,0:T(8,128)S(1)}, f32[24,1024]{1,0:T(8,128)S(1)}, u32[]{:S(2)}, u32[]{:S(2)}) %collective-permute-start.16) | collective-permute-done | bytes 98336 | tf_op jit(solution)/shard_map/ppermute | solution.py:133
  136.2 5.7 %collective-permute-start.17 = (f32[48,1024]{1,0:T(8,128)S(1)}, f32[48,1024]{1,0:T(8,128)S(1)}, u32[]{:S(2)}, u32[]{:S(2)}) collective-permute-start(f32[48,1024]{1,0:T(8,128)S(1)} %maximum_select_fusion.3), channel_id=1, source_target_pairs={{0,1},{1,0},{2,3},{3,2},{4,5},{5,4},{6,7},{7,6},{8,9},{9,8},{10,11... | collective-permute-start | bytes 589832 | tf_op jit(solution)/shard_map/ppermute | solution.py:133
  142.0 1.0 collective-permute-done.17
  143.2 0.9 fusion.22
  144.1 0.8 pad_maximum_fusion.3
  144.9 0.4 add_divide_fusion
  145.3 1.2 pad_maximum_fusion.2
  (69 shorter events, 1.7 us)
Async XLA Ops:
  0.6 8.4 %copy-start.1 = (f32[3,32,1024]{2,1,0:T(8,128)S(1)}, f32[3,32,1024]{2,1,0:T(8,128)}, u32[]{:S(2)}) copy-start(f32[3,32,1024]{2,1,0:T(8,128)} %param.4) | copy-start | bytes 1179652
  0.6 7.7 %copy-start = (f32[3,4,32,1024]{3,2,1,0:T(8,128)S(1)}, f32[3,4,32,1024]{3,2,1,0:T(8,128)}, u32[]{:S(2)}) copy-start(f32[3,4,32,1024]{3,2,1,0:T(8,128)} %param.3) | copy-start | bytes 4718596
  0.7 23.6 %copy-start.15 = (s32[4]{0:T(128)S(1)}, s32[4]{0:T(128)}, u32[]{:S(2)}) copy-start(s32[4]{0:T(128)} %param.5) | copy-start | bytes 52
  2.1 36.4 %collective-permute-start = (f32[3,5,2,1024]{3,2,1,0:T(2,128)S(1)}, f32[3,5,2,1024]{3,2,1,0:T(2,128)S(1)}, u32[]{:S(2)}, u32[]{:S(2)}) collective-permute-start(f32[3,5,2,1024]{3,2,1,0:T(2,128)S(1)} %get-tuple-element.25), channel_id=1, source_target_pairs={{0,32},{32,64},{64,96},{96,128},{128,160},{160,192},{192,224},{224... | collective-permute-start | bytes 368648 | tf_op jit(solution)/shard_map/ppermute | solution.py:22
  4.3 34.3 %collective-permute-start.1 = (f32[3,5,2,1024]{3,2,1,0:T(2,128)S(1)}, f32[3,5,2,1024]{3,2,1,0:T(2,128)S(1)}, u32[]{:S(2)}, u32[]{:S(2)}) collective-permute-start(f32[3,5,2,1024]{3,2,1,0:T(2,128)S(1)} %get-tuple-element.26), channel_id=1, source_target_pairs={{32,0},{64,32},{96,64},{128,96},{160,128},{192,160},{224,192},{0,2... | collective-permute-start | bytes 368648 | tf_op jit(solution)/shard_map/ppermute | solution.py:25
  11.7 25.3 %all-to-all-start = ((f32[256,1,1]{2,1,0:T(1,128)}), f32[256,1,1]{2,1,0:T(1,128)S(1)}, u32[]{:S(2)}, u32[]{:S(2)}) async-start(f32[256,1,1]{2,1,0:T(1,128)} %broadcast_in_dim.12), calls=%async_computation | async-start | bytes 262144 | tf_op jit(solution)/shard_map/all_to_all | solution.py:111
  41.8 36.0 %copy-start.2 = (f32[1,32,1024]{2,1,0:T(8,128)}, f32[1,32,1024]{2,1,0:T(8,128)S(1)}, u32[]{:S(2)}) copy-start(f32[1,32,1024]{2,1,0:T(8,128)S(1)} %get-tuple-element.16) | copy-start | bytes 393220
  43.2 32.6 %copy-start.14 = (f32[32,1024]{1,0:T(8,128)S(1)}, f32[32,1024]{1,0:T(8,128)}, u32[]{:S(2)}) copy-start(f32[32,1024]{1,0:T(8,128)} %get-tuple-element.29) | copy-start | bytes 393220
  43.9 2.4 %collective-permute-start.2 = (f32[48,1024]{1,0:T(8,128)}, f32[48,1024]{1,0:T(8,128)}, u32[]{:S(2)}, u32[]{:S(2)}) collective-permute-start(f32[48,1024]{1,0:T(8,128)} %fusion.49), channel_id=1, source_target_pairs={{0,1},{1,0},{2,3},{3,2},{4,5},{5,4},{6,7},{7,6},{8,9},{9,8},{10,11... | collective-permute-start | bytes 589832 | tf_op jit(solution)/shard_map/ppermute | solution.py:224
  47.3 4.1 %collective-permute-start.3 = (f32[24,1024]{1,0:T(8,128)S(1)}, f32[24,1024]{1,0:T(8,128)S(1)}, u32[]{:S(2)}, u32[]{:S(2)}) collective-permute-start(f32[24,1024]{1,0:T(8,128)S(1)} %slice_select_fusion.1), channel_id=1, source_target_pairs={{0,2},{1,3},{2,0},{3,1},{4,6},{5,7},{6,4},{7,5},{8,10},{9,11},{10,... | collective-permute-start | bytes 294920 | tf_op jit(solution)/shard_map/ppermute | solution.py:125
  51.4 3.6 %collective-permute-start.4 = (f32[24,1024]{1,0:T(8,128)S(1)}, f32[24,1024]{1,0:T(8,128)S(1)}, u32[]{:S(2)}, u32[]{:S(2)}) collective-permute-start(f32[24,1024]{1,0:T(8,128)S(1)} %select_add_fusion.3), channel_id=1, source_target_pairs={{0,4},{1,5},{2,6},{3,7},{4,0},{5,1},{6,2},{7,3},{8,12},{9,13},{10,... | collective-permute-start | bytes 294920 | tf_op jit(solution)/shard_map/ppermute | solution.py:154
  55.0 5.5 %collective-permute-start.5 = (f32[24,1024]{1,0:T(8,128)S(1)}, f32[24,1024]{1,0:T(8,128)S(1)}, u32[]{:S(2)}, u32[]{:S(2)}) collective-permute-start(f32[24,1024]{1,0:T(8,128)S(1)} %add.168), channel_id=1, source_target_pairs={{0,8},{1,9},{2,10},{3,11},{4,12},{5,13},{6,14},{7,15},{8,0},{9,1},... | collective-permute-start | bytes 294920 | tf_op jit(solution)/shard_map/ppermute | solution.py:154
  60.5 5.8 %collective-permute-start.6 = (f32[24,1024]{1,0:T(8,128)S(1)}, f32[24,1024]{1,0:T(8,128)S(1)}, u32[]{:S(2)}, u32[]{:S(2)}) collective-permute-start(f32[24,1024]{1,0:T(8,128)S(1)} %add.169), channel_id=1, source_target_pairs={{0,28},{1,29},{2,30},{3,31},{4,24},{5,25},{6,26},{7,27},{8,20},{9,... | collective-permute-start | bytes 294920 | tf_op jit(solution)/shard_map/ppermute | solution.py:154
  66.3 3.8 %collective-permute-start.7 = (f32[24,1024]{1,0:T(8,128)S(1)}, f32[24,1024]{1,0:T(8,128)S(1)}, u32[]{:S(2)}, u32[]{:S(2)}) collective-permute-start(f32[24,1024]{1,0:T(8,128)S(1)} %add.170), channel_id=1, source_target_pairs={{0,2},{1,3},{2,0},{3,1},{4,6},{5,7},{6,4},{7,5},{8,10},{9,11},{10,... | collective-permute-start | bytes 294920 | tf_op jit(solution)/shard_map/ppermute | solution.py:133
  70.2 6.7 %collective-permute-start.8 = (f32[48,1024]{1,0:T(8,128)S(1)}, f32[48,1024]{1,0:T(8,128)S(1)}, u32[]{:S(2)}, u32[]{:S(2)}) collective-permute-start(f32[48,1024]{1,0:T(8,128)S(1)} %maximum_select_fusion.2), channel_id=1, source_target_pairs={{0,1},{1,0},{2,3},{3,2},{4,5},{5,4},{6,7},{7,6},{8,9},{9,8},{10,11... | collective-permute-start | bytes 589832 | tf_op jit(solution)/shard_map/ppermute | solution.py:133
  77.0 1.5 copy-start.4
  77.0 1.4 copy-start.6
  77.7 0.7 copy-start.10
  77.7 0.7 copy-start.12
  77.8 1.7 %copy-start.8 = (f32[2,32,1024]{2,1,0:T(8,128)}, f32[2,32,1024]{2,1,0:T(8,128)S(1)}, u32[]{:S(2)}) copy-start(f32[2,32,1024]{2,1,0:T(8,128)S(1)} %pad_maximum_fusion.4) | copy-start | bytes 786436
  79.5 27.4 %collective-permute-start.10 = (f32[3,5,2,1024]{3,2,1,0:T(2,128)}, f32[3,5,2,1024]{3,2,1,0:T(2,128)}, u32[]{:S(2)}, u32[]{:S(2)}) collective-permute-start(f32[3,5,2,1024]{3,2,1,0:T(2,128)} %get-tuple-element.24), channel_id=1, source_target_pairs={{32,0},{64,32},{96,64},{128,96},{160,128},{192,160},{224,192},{0,2... | collective-permute-start | bytes 368648 | tf_op jit(solution)/shard_map/ppermute | solution.py:25
  80.6 26.2 %collective-permute-start.9 = (f32[3,5,2,1024]{3,2,1,0:T(2,128)}, f32[3,5,2,1024]{3,2,1,0:T(2,128)}, u32[]{:S(2)}, u32[]{:S(2)}) collective-permute-start(f32[3,5,2,1024]{3,2,1,0:T(2,128)} %get-tuple-element.23), channel_id=1, source_target_pairs={{0,32},{32,64},{64,96},{96,128},{128,160},{160,192},{192,224},{224... | collective-permute-start | bytes 368648 | tf_op jit(solution)/shard_map/ppermute | solution.py:22
  109.3 1.1 copy-start.3
  110.8 32.2 %copy-start.13 = (f32[32,1024]{1,0:T(8,128)S(1)}, f32[32,1024]{1,0:T(8,128)}, u32[]{:S(2)}) copy-start(f32[32,1024]{1,0:T(8,128)} %copy-done.12) | copy-start | bytes 393220
  110.8 32.4 %copy-start.11 = (f32[32,1024]{1,0:T(8,128)S(1)}, f32[32,1024]{1,0:T(8,128)}, u32[]{:S(2)}) copy-start(f32[32,1024]{1,0:T(8,128)} %copy-done.10) | copy-start | bytes 393220
  110.9 2.3 %collective-permute-start.11 = (f32[48,1024]{1,0:T(8,128)S(1)}, f32[48,1024]{1,0:T(8,128)S(1)}, u32[]{:S(2)}, u32[]{:S(2)}) collective-permute-start(f32[48,1024]{1,0:T(8,128)S(1)} %fusion.50), channel_id=1, source_target_pairs={{0,1},{1,0},{2,3},{3,2},{4,5},{5,4},{6,7},{7,6},{8,9},{9,8},{10,11... | collective-permute-start | bytes 589832 | tf_op jit(solution)/shard_map/ppermute | solution.py:224
  113.3 4.1 %collective-permute-start.12 = (f32[24,1024]{1,0:T(8,128)S(1)}, f32[24,1024]{1,0:T(8,128)S(1)}, u32[]{:S(2)}, u32[]{:S(2)}) collective-permute-start(f32[24,1024]{1,0:T(8,128)S(1)} %slice_select_fusion), channel_id=1, source_target_pairs={{0,2},{1,3},{2,0},{3,1},{4,6},{5,7},{6,4},{7,5},{8,10},{9,11},{10,... | collective-permute-start | bytes 294920 | tf_op jit(solution)/shard_map/ppermute | solution.py:125
  117.4 3.6 %collective-permute-start.13 = (f32[24,1024]{1,0:T(8,128)S(1)}, f32[24,1024]{1,0:T(8,128)S(1)}, u32[]{:S(2)}, u32[]{:S(2)}) collective-permute-start(f32[24,1024]{1,0:T(8,128)S(1)} %select_add_fusion.2), channel_id=1, source_target_pairs={{0,4},{1,5},{2,6},{3,7},{4,0},{5,1},{6,2},{7,3},{8,12},{9,13},{10,... | collective-permute-start | bytes 294920 | tf_op jit(solution)/shard_map/ppermute | solution.py:154
  121.0 5.5 %collective-permute-start.14 = (f32[24,1024]{1,0:T(8,128)S(1)}, f32[24,1024]{1,0:T(8,128)S(1)}, u32[]{:S(2)}, u32[]{:S(2)}) collective-permute-start(f32[24,1024]{1,0:T(8,128)S(1)} %add.186), channel_id=1, source_target_pairs={{0,8},{1,9},{2,10},{3,11},{4,12},{5,13},{6,14},{7,15},{8,0},{9,1},... | collective-permute-start | bytes 294920 | tf_op jit(solution)/shard_map/ppermute | solution.py:154
  126.5 5.8 %collective-permute-start.15 = (f32[24,1024]{1,0:T(8,128)S(1)}, f32[24,1024]{1,0:T(8,128)S(1)}, u32[]{:S(2)}, u32[]{:S(2)}) collective-permute-start(f32[24,1024]{1,0:T(8,128)S(1)} %add.187), channel_id=1, source_target_pairs={{0,28},{1,29},{2,30},{3,31},{4,24},{5,25},{6,26},{7,27},{8,20},{9,... | collective-permute-start | bytes 294920 | tf_op jit(solution)/shard_map/ppermute | solution.py:154
  132.3 3.8 %collective-permute-start.16 = (f32[24,1024]{1,0:T(8,128)S(1)}, f32[24,1024]{1,0:T(8,128)S(1)}, u32[]{:S(2)}, u32[]{:S(2)}) collective-permute-start(f32[24,1024]{1,0:T(8,128)S(1)} %add.188), channel_id=1, source_target_pairs={{0,2},{1,3},{2,0},{3,1},{4,6},{5,7},{6,4},{7,5},{8,10},{9,11},{10,... | collective-permute-start | bytes 294920 | tf_op jit(solution)/shard_map/ppermute | solution.py:133
  136.2 6.8 %collective-permute-start.17 = (f32[48,1024]{1,0:T(8,128)S(1)}, f32[48,1024]{1,0:T(8,128)S(1)}, u32[]{:S(2)}, u32[]{:S(2)}) collective-permute-start(f32[48,1024]{1,0:T(8,128)S(1)} %maximum_select_fusion.3), channel_id=1, source_target_pairs={{0,1},{1,0},{2,3},{3,2},{4,5},{5,4},{6,7},{7,6},{8,9},{9,8},{10,11... | collective-permute-start | bytes 589832 | tf_op jit(solution)/shard_map/ppermute | solution.py:133
  143.0 1.9 %copy-start.5 = (f32[4,32,1024]{2,1,0:T(8,128)S(1)}, f32[4,32,1024]{2,1,0:T(8,128)}, u32[]{:S(2)}) copy-start(f32[4,32,1024]{2,1,0:T(8,128)} %get-tuple-element.32) | copy-start | bytes 1572868
  143.0 1.9 %copy-start.7 = (f32[4,32,1024]{2,1,0:T(8,128)S(1)}, f32[4,32,1024]{2,1,0:T(8,128)}, u32[]{:S(2)}) copy-start(f32[4,32,1024]{2,1,0:T(8,128)} %get-tuple-element.33) | copy-start | bytes 1572868
  143.0 1.9 %copy-start.9 = (f32[2,32,1024]{2,1,0:T(8,128)S(1)}, f32[2,32,1024]{2,1,0:T(8,128)}, u32[]{:S(2)}) copy-start(f32[2,32,1024]{2,1,0:T(8,128)} %copy-done.8) | copy-start | bytes 786436

commit v6 on v3

--- a/solution.py
+++ b/solution.py
@@ -140,11 +140,13 @@
     return part
 
 
-def species_sum(block, axis):
+def species_sum(block, axis, first_done=()):
     count = lax.axis_size(axis)
     index = lax.axis_index(axis)
     low_bits = [bit for bit in (1, 2) if bit < count]
-    part, done = split_rounds(block, axis, low_bits)
+    taken = [bit for bit, dim in first_done]
+    part, done = split_rounds(block, axis, [bit for bit in low_bits if bit not in taken])
+    done = list(first_done) + done
     block_size = 2 * low_bits[-1] if low_bits else 1
     bit = block_size
     while bit < count:
@@ -156,15 +158,57 @@
     return join_rounds(part, axis, done)
 
 
+def drag_sums(step_time, stop_times, upper, dust, gas_density, divergence, total_species):
+    local_species = dust.shape[1]
+    gas_new = gas_density - step_time * divergence[local_species]
+    fresh = dust[0] - step_time * divergence[:local_species]
+    rate = step_time * gas_new[None] / stop_times[:, None, None]
+    weight = fresh / (total_species * gas_new[None]) * rate / (1.0 + rate)
+    totals = jnp.concatenate(
+        [jnp.sum(weight, 0), jnp.sum(weight * dust[1], 0), jnp.sum(weight * dust[2], 0)], axis=0
+    )
+    half = totals.shape[0] // 2
+    low, high = totals[:half], totals[half:]
+    keep = jnp.where(upper, high, low)
+    send = jnp.where(upper, low, high)
+    density = jnp.concatenate([fresh, gas_new[None]], axis=0)
+    return density, rate, keep, send
+
+
 def advance(wide, margin, tile_rows, stop_times, total_species):
     interior = lax.slice_in_dim(wide, margin, margin + tile_rows, axis=2)
     local_top = jnp.max(jnp.abs(interior[1]) + jnp.abs(interior[2]))
     fastest = global_max(local_top, ("space", "species"))
     step_time = courant / (sound_speed + fastest)
-    new_density, gas_velocity, dust_velocity = moved(wide, step_time)
-    rate, terms = drag_terms(new_density, dust_velocity, stop_times, step_time, total_species)
-    shape = terms.shape
-    totals = species_sum(terms.reshape(-1, shape[-1]), "species").reshape(shape)
+    density = wide[0]
+    radial = wide[1]
+    azimuth = wide[2]
+    div_azimuth = face_divergence(density, azimuth, 1)
+    inner_density = density[:, 2:-2]
+    inner_radial = radial[:, 2:-2]
+    zero_pad = ((0, 0), (0, 0), (2, 2))
+    div_radial = face_divergence(
+        jnp.pad(inner_density, zero_pad), jnp.pad(inner_radial, zero_pad), 2
+    )
+    divergence = div_azimuth + div_radial
+    dust = interior[:, :-1]
+    upper = lax.axis_index("species") % 2 == 1
+    new_density, rate, keep, send = drag_sums(
+        step_time, stop_times, upper, dust, inner_density[-1], divergence, total_species
+    )
+    gas_density = density[-1]
+    inner_gas = gas_density[2:-2]
+    grad_azimuth = 0.5 * (gas_density[3:-1] - gas_density[1:-3])
+    edge_gas = jnp.pad(inner_gas, ((0, 0), (1, 1)), mode="edge")
+    grad_radial = 0.5 * (edge_gas[:, 2:] - edge_gas[:, :-2])
+    push = step_time * sound_sq / inner_gas
+    gas_velocity = jnp.stack(
+        [inner_radial[-1] - push * grad_radial, azimuth[-1, 2:-2] - push * grad_azimuth]
+    )
+    dust_velocity = jnp.stack([inner_radial[:-1], azimuth[:-1, 2:-2]])
+    part = keep + lax.ppermute(send, "species", xor_pairs(lax.axis_size("species"), 1))
+    totals = species_sum(part, "species", first_done=[(1, 0)])
+    totals = totals.reshape(3, tile_rows, -1)
     gas_next = coupled_gas(gas_velocity, totals)
     return assemble(new_density, dust_velocity, gas_next, rate)
 

time: 142 us -> 141 us (level)
  other arithmetic: 20.8 us -> 16.3 us
  waiting for transfers between devices: 54.6 us -> 57 us
    ppermute x4 -> x2, waiting for transfers between devices: 9.94 us -> 7.46 us  [split_rounds(): part = keep + lax.ppermute(send, axis, xor_pairs(lax.axis_size(axis), bit))]
    ppermute x0 -> x2, waiting for transfers between devices: none -> 2.48 us  [advance(): lax.ppermute(send, 'species', xor_pairs(lax.axis_size('species'), 1))]
    ppermute x0 -> x2, starting transfers between devices: none -> 2.05 us  [advance(): lax.ppermute(send, 'species', xor_pairs(lax.axis_size('species'), 1))]
    ppermute x4 -> x2, starting transfers between devices: 2.78 us -> 0.73 us  [split_rounds(): part = keep + lax.ppermute(send, axis, xor_pairs(lax.axis_size(axis), bit))]
    ppermute x4, waiting for transfers between devices: 6.85 us -> 8.67 us  [join_rounds(): other = lax.ppermute(part, axis, xor_pairs(lax.axis_size(axis), bit))]
    add x0 -> x4, other arithmetic: none -> 1.67 us  [the longest x2 1.19 us: advance(): keep + lax.ppermute(send, 'species', xor_pairs(lax.axis_size('species'), 1))]
    sub x3 -> x1, other arithmetic: 1.7 us -> 0.07 us  [advance(): azimuth[-1, 2:-2] - push * grad_azimuth]
    concatenate x0 -> x2, other arithmetic: none -> 1.58 us  [the longest x1 1.39 us: local(): fluid = jnp.concatenate([dust_state, gas_state[:, None]], axis=1)]
  transfers between devices with their start and end apart: 19 -> 19, of which waited for: 14 -> 15; matrix products, arithmetic and copies ran while one was open for 6% -> 4% of each run, Pallas kernels for 0% -> 0%
where the time goes in v6:
time: 141 us; the launch traced here: 140 us
  waiting for transfers between devices  57 us (40%)
  starting transfers between devices  39 us (28%)
  blocking collectives  21.3 us (15%)
  other arithmetic  16.3 us (12%)
  local copies, waits for them, and re-layouts  4.45 us (3%)
  between operations  2.54 us (2%)
    ppermute x6, waiting for transfers between devices, species_sum(): other = lax.ppermute(part, axis, pairs)  25.7 us
    all_to_all x1, blocking collectives, global_max(): return jnp.max(lax.all_to_all(spread, axes, 0, 0, tiled=True))  21.3 us
    all_to_all x1, waiting for transfers between devices, global_max(): return jnp.max(lax.all_to_all(spread, axes, 0, 0, tiled=True))  12.7 us
    all_to_all x1, starting transfers between devices, global_max(): return jnp.max(lax.all_to_all(spread, axes, 0, 0, tiled=True))  12.6 us
    ppermute x4, starting transfers between devices, join_rounds(): other = lax.ppermute(part, axis, xor_pairs(lax.axis_size(axis), bit))  12 us
    ppermute x4, waiting for transfers between devices, join_rounds(): other = lax.ppermute(part, axis, xor_pairs(lax.axis_size(axis), bit))  8.67 us
    ppermute x2, waiting for transfers between devices, split_rounds(): part = keep + lax.ppermute(send, axis, xor_pairs(lax.axis_size(axis), bit))  7.46 us
    ppermute x2, starting transfers between devices, padded(): lax.ppermute(lax.slice_in_dim(block, 0, width, axis=dim), axis, backward)  5.41 us
  transfers between devices with their start and end apart: 19, of which 15 were waited for; matrix products, arithmetic and copies ran while one was open for 4% of the time, Pallas kernels for 0%

profile of v6, /device:TPU:1, one launch (start us, length us, event | category | flops | bytes accessed | tf_op | source)
XLA Modules:
  0.0 140.5 jit_solution(13088596579011891979)
XLA Ops:
  0.7 1.4 fusion.59
  2.1 2.2 %collective-permute-start = (f32[3,5,2,1024]{3,2,1,0:T(2,128)S(1)}, f32[3,5,2,1024]{3,2,1,0:T(2,128)S(1)}, u32[]{:S(2)}, u32[]{:S(2)}) collective-permute-start(f32[3,5,2,1024]{3,2,1,0:T(2,128)S(1)} %get-tuple-element.22), channel_id=1, source_target_pairs={{0,32},{32,64},{64,96},{96,128},{128,160},{160,192},{192,224},{224... | collective-permute-start | bytes 368648 | tf_op jit(solution)/shard_map/ppermute | solution.py:22
  4.3 4.0 %collective-permute-start.1 = (f32[3,5,2,1024]{3,2,1,0:T(2,128)S(1)}, f32[3,5,2,1024]{3,2,1,0:T(2,128)S(1)}, u32[]{:S(2)}, u32[]{:S(2)}) collective-permute-start(f32[3,5,2,1024]{3,2,1,0:T(2,128)S(1)} %get-tuple-element.23), channel_id=1, source_target_pairs={{32,0},{64,32},{96,64},{128,96},{160,128},{192,160},{224,192},{0,2... | collective-permute-start | bytes 368648 | tf_op jit(solution)/shard_map/ppermute | solution.py:25
  8.3 0.8 fusion.17
  9.0 1.4 broadcast_in_dim.13
  10.4 12.6 %all-to-all-start = ((f32[256,1,1]{2,1,0:T(1,128)}), f32[256,1,1]{2,1,0:T(1,128)S(1)}, u32[]{:S(2)}, u32[]{:S(2)}) async-start(f32[256,1,1]{2,1,0:T(1,128)} %broadcast_in_dim.13), calls=%async_computation | async-start | bytes 262144 | tf_op jit(solution)/shard_map/all_to_all | solution.py:111
  23.0 12.7 %all-to-all-done = f32[256,1,1]{2,1,0:T(1,128)S(1)} async-done(((f32[256,1,1]{2,1,0:T(1,128)}), f32[256,1,1]{2,1,0:T(1,128)S(1)}, u32[]{:S(2)}, u32[]{:S(2)}) %all-to-all-start) | async-done | bytes 1056 | tf_op jit(solution)/shard_map/all_to_all | solution.py:111
  35.7 0.9 reduce_max.37
  37.3 0.4 pad_maximum_fusion
  37.7 0.3 copy-done.9
  37.9 0.2 slice_bitcast_fusion.5
  38.3 0.6 fusion.10
  38.9 0.2 copy-done.2
  39.2 0.8 multiply_add_fusion.1
  40.0 0.2 fusion.23
  40.3 1.2 multiply_divide_fusion.1
  41.7 0.6 copy-done.6
  42.3 0.7 fusion.57
  43.0 1.0 collective-permute-start.2
  44.0 1.4 %collective-permute-done.2 = f32[48,1024]{1,0:T(8,128)} collective-permute-done((f32[48,1024]{1,0:T(8,128)}, f32[48,1024]{1,0:T(8,128)}, u32[]{:S(2)}, u32[]{:S(2)}) %collective-permute-start.2) | collective-permute-done | bytes 196640 | tf_op jit(solution)/shard_map/ppermute | solution.py:209
  45.4 1.2 select_add_fusion.1
  46.6 0.4 collective-permute-start.3
  47.0 3.7 %collective-permute-done.3 = f32[24,1024]{1,0:T(8,128)S(1)} collective-permute-done((f32[24,1024]{1,0:T(8,128)S(1)}, f32[24,1024]{1,0:T(8,128)S(1)}, u32[]{:S(2)}, u32[]{:S(2)}) %collective-permute-start.3) | collective-permute-done | bytes 98336 | tf_op jit(solution)/shard_map/ppermute | solution.py:125
  50.7 0.9 collective-permute-start.4
  51.7 2.6 %collective-permute-done.4 = f32[24,1024]{1,0:T(8,128)S(1)} collective-permute-done((f32[24,1024]{1,0:T(8,128)S(1)}, f32[24,1024]{1,0:T(8,128)S(1)}, u32[]{:S(2)}, u32[]{:S(2)}) %collective-permute-start.4) | collective-permute-done | bytes 98336 | tf_op jit(solution)/shard_map/ppermute | solution.py:154
  54.3 0.7 collective-permute-start.5
  55.1 4.7 %collective-permute-done.5 = f32[24,1024]{1,0:T(8,128)S(1)} collective-permute-done((f32[24,1024]{1,0:T(8,128)S(1)}, f32[24,1024]{1,0:T(8,128)S(1)}, u32[]{:S(2)}, u32[]{:S(2)}) %collective-permute-start.5) | collective-permute-done | bytes 98336 | tf_op jit(solution)/shard_map/ppermute | solution.py:154
  59.8 0.2 collective-permute-start.6
  60.1 5.5 %collective-permute-done.6 = f32[24,1024]{1,0:T(8,128)S(1)} collective-permute-done((f32[24,1024]{1,0:T(8,128)S(1)}, f32[24,1024]{1,0:T(8,128)S(1)}, u32[]{:S(2)}, u32[]{:S(2)}) %collective-permute-start.6) | collective-permute-done | bytes 98336 | tf_op jit(solution)/shard_map/ppermute | solution.py:154
  65.7 0.4 collective-permute-start.7
  66.1 3.4 %collective-permute-done.7 = f32[24,1024]{1,0:T(8,128)S(1)} collective-permute-done((f32[24,1024]{1,0:T(8,128)S(1)}, f32[24,1024]{1,0:T(8,128)S(1)}, u32[]{:S(2)}, u32[]{:S(2)}) %collective-permute-start.7) | collective-permute-done | bytes 98336 | tf_op jit(solution)/shard_map/ppermute | solution.py:133
  69.5 5.6 %collective-permute-start.8 = (f32[48,1024]{1,0:T(8,128)S(1)}, f32[48,1024]{1,0:T(8,128)S(1)}, u32[]{:S(2)}, u32[]{:S(2)}) collective-permute-start(f32[48,1024]{1,0:T(8,128)S(1)} %maximum_select_fusion.2), channel_id=1, source_target_pairs={{0,1},{1,0},{2,3},{3,2},{4,5},{5,4},{6,7},{7,6},{8,9},{9,8},{10,11... | collective-permute-start | bytes 589832 | tf_op jit(solution)/shard_map/ppermute | solution.py:133
  75.3 0.9 collective-permute-done.8
  76.4 0.3 fusion
  76.7 0.2 pad_maximum_fusion.2
  77.0 1.4 %collective-permute-start.10 = (f32[3,5,2,1024]{3,2,1,0:T(2,128)S(1)}, f32[3,5,2,1024]{3,2,1,0:T(2,128)S(1)}, u32[]{:S(2)}, u32[]{:S(2)}) collective-permute-start(f32[3,5,2,1024]{3,2,1,0:T(2,128)S(1)} %get-tuple-element.21), channel_id=1, source_target_pairs={{32,0},{64,32},{96,64},{128,96},{160,128},{192,160},{224,192},{0,2... | collective-permute-start | bytes 368648 | tf_op jit(solution)/shard_map/ppermute | solution.py:25
  78.4 0.3 collective-permute-start.9
  78.7 0.8 fusion.22
  79.5 0.7 broadcast_in_dim.16
  80.2 21.3 %all_to_all.12 = f32[256,1,1]{2,1,0:T(1,128)S(1)} all-to-all(f32[256,1,1]{2,1,0:T(1,128)S(1)} %broadcast_in_dim.16), channel_id=1, replica_groups=mesh['space'=8,'species'=32] {'space','species'}, dimensions={0} | all-to-all | bytes 2048 | tf_op jit(solution)/shard_map/all_to_all | solution.py:111
  101.6 0.9 reduce_max.39
  103.1 0.4 pad_maximum_fusion.1
  103.5 0.3 slice_bitcast_fusion.1
  103.9 0.6 fusion.4
  104.6 0.8 multiply_add_fusion
  105.4 0.2 fusion.20
  105.7 0.3 fusion.34
  106.2 1.1 collective-permute-start.11
  107.3 1.1 collective-permute-done.11
  108.4 0.4 collective-permute-start.12
  108.8 3.7 %collective-permute-done.12 = f32[24,1024]{1,0:T(8,128)S(1)} collective-permute-done((f32[24,1024]{1,0:T(8,128)S(1)}, f32[24,1024]{1,0:T(8,128)S(1)}, u32[]{:S(2)}, u32[]{:S(2)}) %collective-permute-start.12) | collective-permute-done | bytes 98336 | tf_op jit(solution)/shard_map/ppermute | solution.py:125
  112.5 0.9 collective-permute-start.13
  113.6 2.5 %collective-permute-done.13 = f32[24,1024]{1,0:T(8,128)S(1)} collective-permute-done((f32[24,1024]{1,0:T(8,128)S(1)}, f32[24,1024]{1,0:T(8,128)S(1)}, u32[]{:S(2)}, u32[]{:S(2)}) %collective-permute-start.13) | collective-permute-done | bytes 98336 | tf_op jit(solution)/shard_map/ppermute | solution.py:154
  116.1 0.7 collective-permute-start.14
  116.9 4.8 %collective-permute-done.14 = f32[24,1024]{1,0:T(8,128)S(1)} collective-permute-done((f32[24,1024]{1,0:T(8,128)S(1)}, f32[24,1024]{1,0:T(8,128)S(1)}, u32[]{:S(2)}, u32[]{:S(2)}) %collective-permute-start.14) | collective-permute-done | bytes 98336 | tf_op jit(solution)/shard_map/ppermute | solution.py:154
  121.6 0.2 collective-permute-start.15
  121.9 5.5 %collective-permute-done.15 = f32[24,1024]{1,0:T(8,128)S(1)} collective-permute-done((f32[24,1024]{1,0:T(8,128)S(1)}, f32[24,1024]{1,0:T(8,128)S(1)}, u32[]{:S(2)}, u32[]{:S(2)}) %collective-permute-start.15) | collective-permute-done | bytes 98336 | tf_op jit(solution)/shard_map/ppermute | solution.py:154
  127.5 0.4 collective-permute-start.16
  128.0 3.3 %collective-permute-done.16 = f32[24,1024]{1,0:T(8,128)S(1)} collective-permute-done((f32[24,1024]{1,0:T(8,128)S(1)}, f32[24,1024]{1,0:T(8,128)S(1)}, u32[]{:S(2)}, u32[]{:S(2)}) %collective-permute-start.16) | collective-permute-done | bytes 98336 | tf_op jit(solution)/shard_map/ppermute | solution.py:133
  131.3 5.6 %collective-permute-start.17 = (f32[48,1024]{1,0:T(8,128)S(1)}, f32[48,1024]{1,0:T(8,128)S(1)}, u32[]{:S(2)}, u32[]{:S(2)}) collective-permute-start(f32[48,1024]{1,0:T(8,128)S(1)} %maximum_select_fusion.3), channel_id=1, source_target_pairs={{0,1},{1,0},{2,3},{3,2},{4,5},{5,4},{6,7},{7,6},{8,9},{9,8},{10,11... | collective-permute-start | bytes 589832 | tf_op jit(solution)/shard_map/ppermute | solution.py:133
  137.1 1.0 collective-permute-done.17
  138.2 0.8 pad_maximum_fusion.4
  139.0 0.3 fusion.1
  139.2 1.2 pad_maximum_fusion.3
  (73 shorter events, 2.2 us)
Async XLA Ops:
  0.6 7.6 %copy-start.1 = (f32[3,32,1024]{2,1,0:T(8,128)S(1)}, f32[3,32,1024]{2,1,0:T(8,128)}, u32[]{:S(2)}) copy-start(f32[3,32,1024]{2,1,0:T(8,128)} %param.4) | copy-start | bytes 1179652
  0.6 7.6 %copy-start = (f32[3,4,32,1024]{3,2,1,0:T(8,128)S(1)}, f32[3,4,32,1024]{3,2,1,0:T(8,128)}, u32[]{:S(2)}) copy-start(f32[3,4,32,1024]{3,2,1,0:T(8,128)} %param.3) | copy-start | bytes 4718596
  0.6 22.3 %copy-start.13 = (s32[4]{0:T(128)S(1)}, s32[4]{0:T(128)}, u32[]{:S(2)}) copy-start(s32[4]{0:T(128)} %param.5) | copy-start | bytes 52
  2.1 35.2 %collective-permute-start = (f32[3,5,2,1024]{3,2,1,0:T(2,128)S(1)}, f32[3,5,2,1024]{3,2,1,0:T(2,128)S(1)}, u32[]{:S(2)}, u32[]{:S(2)}) collective-permute-start(f32[3,5,2,1024]{3,2,1,0:T(2,128)S(1)} %get-tuple-element.22), channel_id=1, source_target_pairs={{0,32},{32,64},{64,96},{96,128},{128,160},{160,192},{192,224},{224... | collective-permute-start | bytes 368648 | tf_op jit(solution)/shard_map/ppermute | solution.py:22
  4.3 33.0 %collective-permute-start.1 = (f32[3,5,2,1024]{3,2,1,0:T(2,128)S(1)}, f32[3,5,2,1024]{3,2,1,0:T(2,128)S(1)}, u32[]{:S(2)}, u32[]{:S(2)}) collective-permute-start(f32[3,5,2,1024]{3,2,1,0:T(2,128)S(1)} %get-tuple-element.23), channel_id=1, source_target_pairs={{32,0},{64,32},{96,64},{128,96},{160,128},{192,160},{224,192},{0,2... | collective-permute-start | bytes 368648 | tf_op jit(solution)/shard_map/ppermute | solution.py:25
  10.4 25.3 %all-to-all-start = ((f32[256,1,1]{2,1,0:T(1,128)}), f32[256,1,1]{2,1,0:T(1,128)S(1)}, u32[]{:S(2)}, u32[]{:S(2)}) async-start(f32[256,1,1]{2,1,0:T(1,128)} %broadcast_in_dim.13), calls=%async_computation | async-start | bytes 262144 | tf_op jit(solution)/shard_map/all_to_all | solution.py:111
  37.3 0.7 copy-start.9
  37.3 0.7 copy-start.11
  38.2 0.9 copy-start.2
  41.7 0.7 copy-start.6
  41.7 1.3 copy-start.7
  41.7 1.3 copy-start.8
  43.0 2.4 %collective-permute-start.2 = (f32[48,1024]{1,0:T(8,128)}, f32[48,1024]{1,0:T(8,128)}, u32[]{:S(2)}, u32[]{:S(2)}) collective-permute-start(f32[48,1024]{1,0:T(8,128)} %fusion.57), channel_id=1, source_target_pairs={{0,1},{1,0},{2,3},{3,2},{4,5},{5,4},{6,7},{7,6},{8,9},{9,8},{10,11... | collective-permute-start | bytes 589832 | tf_op jit(solution)/shard_map/ppermute | solution.py:209
  44.0 11.0 %copy-start.3 = (f32[5,36,1024]{2,1,0:T(8,128)S(1)}, f32[5,36,1024]{2,1,0:T(8,128)}, u32[]{:S(2)}) copy-start(f32[5,36,1024]{2,1,0:T(8,128)} %copy-done.2) | copy-start | bytes 2211844
  44.0 16.0 %copy-start.10 = (f32[3,5,2,1024]{3,2,1,0:T(2,128)S(1)}, f32[3,5,2,1024]{3,2,1,0:T(2,128)}, u32[]{:S(2)}) copy-start(f32[3,5,2,1024]{3,2,1,0:T(2,128)} %copy-done.9) | copy-start | bytes 368644
  44.0 16.0 %copy-start.12 = (f32[3,5,2,1024]{3,2,1,0:T(2,128)S(1)}, f32[3,5,2,1024]{3,2,1,0:T(2,128)}, u32[]{:S(2)}) copy-start(f32[3,5,2,1024]{3,2,1,0:T(2,128)} %copy-done.11) | copy-start | bytes 368644
  46.6 4.1 %collective-permute-start.3 = (f32[24,1024]{1,0:T(8,128)S(1)}, f32[24,1024]{1,0:T(8,128)S(1)}, u32[]{:S(2)}, u32[]{:S(2)}) collective-permute-start(f32[24,1024]{1,0:T(8,128)S(1)} %slice_select_fusion.1), channel_id=1, source_target_pairs={{0,2},{1,3},{2,0},{3,1},{4,6},{5,7},{6,4},{7,5},{8,10},{9,11},{10,... | collective-permute-start | bytes 294920 | tf_op jit(solution)/shard_map/ppermute | solution.py:125
  50.7 3.6 %collective-permute-start.4 = (f32[24,1024]{1,0:T(8,128)S(1)}, f32[24,1024]{1,0:T(8,128)S(1)}, u32[]{:S(2)}, u32[]{:S(2)}) collective-permute-start(f32[24,1024]{1,0:T(8,128)S(1)} %select_add_fusion.3), channel_id=1, source_target_pairs={{0,4},{1,5},{2,6},{3,7},{4,0},{5,1},{6,2},{7,3},{8,12},{9,13},{10,... | collective-permute-start | bytes 294920 | tf_op jit(solution)/shard_map/ppermute | solution.py:154
  54.3 5.5 %collective-permute-start.5 = (f32[24,1024]{1,0:T(8,128)S(1)}, f32[24,1024]{1,0:T(8,128)S(1)}, u32[]{:S(2)}, u32[]{:S(2)}) collective-permute-start(f32[24,1024]{1,0:T(8,128)S(1)} %add.169), channel_id=1, source_target_pairs={{0,8},{1,9},{2,10},{3,11},{4,12},{5,13},{6,14},{7,15},{8,0},{9,1},... | collective-permute-start | bytes 294920 | tf_op jit(solution)/shard_map/ppermute | solution.py:154
  59.8 5.8 %collective-permute-start.6 = (f32[24,1024]{1,0:T(8,128)S(1)}, f32[24,1024]{1,0:T(8,128)S(1)}, u32[]{:S(2)}, u32[]{:S(2)}) collective-permute-start(f32[24,1024]{1,0:T(8,128)S(1)} %add.170), channel_id=1, source_target_pairs={{0,28},{1,29},{2,30},{3,31},{4,24},{5,25},{6,26},{7,27},{8,20},{9,... | collective-permute-start | bytes 294920 | tf_op jit(solution)/shard_map/ppermute | solution.py:154
  65.7 3.8 %collective-permute-start.7 = (f32[24,1024]{1,0:T(8,128)S(1)}, f32[24,1024]{1,0:T(8,128)S(1)}, u32[]{:S(2)}, u32[]{:S(2)}) collective-permute-start(f32[24,1024]{1,0:T(8,128)S(1)} %add.171), channel_id=1, source_target_pairs={{0,2},{1,3},{2,0},{3,1},{4,6},{5,7},{6,4},{7,5},{8,10},{9,11},{10,... | collective-permute-start | bytes 294920 | tf_op jit(solution)/shard_map/ppermute | solution.py:133
  66.1 10.3 %copy-start.4 = (f32[4,32,1024]{2,1,0:T(8,128)S(1)}, f32[4,32,1024]{2,1,0:T(8,128)}, u32[]{:S(2)}) copy-start(f32[4,32,1024]{2,1,0:T(8,128)} %get-tuple-element.30) | copy-start | bytes 1572868
  66.1 10.3 %copy-start.5 = (f32[4,32,1024]{2,1,0:T(8,128)S(1)}, f32[4,32,1024]{2,1,0:T(8,128)}, u32[]{:S(2)}) copy-start(f32[4,32,1024]{2,1,0:T(8,128)} %get-tuple-element.31) | copy-start | bytes 1572868
  69.5 6.7 %collective-permute-start.8 = (f32[48,1024]{1,0:T(8,128)S(1)}, f32[48,1024]{1,0:T(8,128)S(1)}, u32[]{:S(2)}, u32[]{:S(2)}) collective-permute-start(f32[48,1024]{1,0:T(8,128)S(1)} %maximum_select_fusion.2), channel_id=1, source_target_pairs={{0,1},{1,0},{2,3},{3,2},{4,5},{5,4},{6,7},{7,6},{8,9},{9,8},{10,11... | collective-permute-start | bytes 589832 | tf_op jit(solution)/shard_map/ppermute | solution.py:133
  77.0 26.1 %collective-permute-start.10 = (f32[3,5,2,1024]{3,2,1,0:T(2,128)S(1)}, f32[3,5,2,1024]{3,2,1,0:T(2,128)S(1)}, u32[]{:S(2)}, u32[]{:S(2)}) collective-permute-start(f32[3,5,2,1024]{3,2,1,0:T(2,128)S(1)} %get-tuple-element.21), channel_id=1, source_target_pairs={{32,0},{64,32},{96,64},{128,96},{160,128},{192,160},{224,192},{0,2... | collective-permute-start | bytes 368648 | tf_op jit(solution)/shard_map/ppermute | solution.py:25
  78.4 24.7 %collective-permute-start.9 = (f32[3,5,2,1024]{3,2,1,0:T(2,128)S(1)}, f32[3,5,2,1024]{3,2,1,0:T(2,128)S(1)}, u32[]{:S(2)}, u32[]{:S(2)}) collective-permute-start(f32[3,5,2,1024]{3,2,1,0:T(2,128)S(1)} %get-tuple-element.20), channel_id=1, source_target_pairs={{0,32},{32,64},{64,96},{96,128},{128,160},{160,192},{192,224},{224... | collective-permute-start | bytes 368648 | tf_op jit(solution)/shard_map/ppermute | solution.py:22
  106.2 2.1 %collective-permute-start.11 = (f32[48,1024]{1,0:T(8,128)S(1)}, f32[48,1024]{1,0:T(8,128)S(1)}, u32[]{:S(2)}, u32[]{:S(2)}) collective-permute-start(f32[48,1024]{1,0:T(8,128)S(1)} %fusion.58), channel_id=1, source_target_pairs={{0,1},{1,0},{2,3},{3,2},{4,5},{5,4},{6,7},{7,6},{8,9},{9,8},{10,11... | collective-permute-start | bytes 589832 | tf_op jit(solution)/shard_map/ppermute | solution.py:209
  108.4 4.1 %collective-permute-start.12 = (f32[24,1024]{1,0:T(8,128)S(1)}, f32[24,1024]{1,0:T(8,128)S(1)}, u32[]{:S(2)}, u32[]{:S(2)}) collective-permute-start(f32[24,1024]{1,0:T(8,128)S(1)} %slice_select_fusion), channel_id=1, source_target_pairs={{0,2},{1,3},{2,0},{3,1},{4,6},{5,7},{6,4},{7,5},{8,10},{9,11},{10,... | collective-permute-start | bytes 294920 | tf_op jit(solution)/shard_map/ppermute | solution.py:125
  112.5 3.6 %collective-permute-start.13 = (f32[24,1024]{1,0:T(8,128)S(1)}, f32[24,1024]{1,0:T(8,128)S(1)}, u32[]{:S(2)}, u32[]{:S(2)}) collective-permute-start(f32[24,1024]{1,0:T(8,128)S(1)} %select_add_fusion.2), channel_id=1, source_target_pairs={{0,4},{1,5},{2,6},{3,7},{4,0},{5,1},{6,2},{7,3},{8,12},{9,13},{10,... | collective-permute-start | bytes 294920 | tf_op jit(solution)/shard_map/ppermute | solution.py:154
  116.1 5.5 %collective-permute-start.14 = (f32[24,1024]{1,0:T(8,128)S(1)}, f32[24,1024]{1,0:T(8,128)S(1)}, u32[]{:S(2)}, u32[]{:S(2)}) collective-permute-start(f32[24,1024]{1,0:T(8,128)S(1)} %add.185), channel_id=1, source_target_pairs={{0,8},{1,9},{2,10},{3,11},{4,12},{5,13},{6,14},{7,15},{8,0},{9,1},... | collective-permute-start | bytes 294920 | tf_op jit(solution)/shard_map/ppermute | solution.py:154
  121.6 5.8 %collective-permute-start.15 = (f32[24,1024]{1,0:T(8,128)S(1)}, f32[24,1024]{1,0:T(8,128)S(1)}, u32[]{:S(2)}, u32[]{:S(2)}) collective-permute-start(f32[24,1024]{1,0:T(8,128)S(1)} %add.186), channel_id=1, source_target_pairs={{0,28},{1,29},{2,30},{3,31},{4,24},{5,25},{6,26},{7,27},{8,20},{9,... | collective-permute-start | bytes 294920 | tf_op jit(solution)/shard_map/ppermute | solution.py:154
  127.5 3.8 %collective-permute-start.16 = (f32[24,1024]{1,0:T(8,128)S(1)}, f32[24,1024]{1,0:T(8,128)S(1)}, u32[]{:S(2)}, u32[]{:S(2)}) collective-permute-start(f32[24,1024]{1,0:T(8,128)S(1)} %add.187), channel_id=1, source_target_pairs={{0,2},{1,3},{2,0},{3,1},{4,6},{5,7},{6,4},{7,5},{8,10},{9,11},{10,... | collective-permute-start | bytes 294920 | tf_op jit(solution)/shard_map/ppermute | solution.py:133
  131.3 6.7 %collective-permute-start.17 = (f32[48,1024]{1,0:T(8,128)S(1)}, f32[48,1024]{1,0:T(8,128)S(1)}, u32[]{:S(2)}, u32[]{:S(2)}) collective-permute-start(f32[48,1024]{1,0:T(8,128)S(1)} %maximum_select_fusion.3), channel_id=1, source_target_pairs={{0,1},{1,0},{2,3},{3,2},{4,5},{5,4},{6,7},{7,6},{8,9},{9,8},{10,11... | collective-permute-start | bytes 589832 | tf_op jit(solution)/shard_map/ppermute | solution.py:133

commit v7 on v6

--- a/solution.py
+++ b/solution.py
@@ -14,16 +14,21 @@
 
 
 def padded(block, sides, width):
+    moving = jnp.stack([block[0], block[2]])
     for axis, dim in sides:
         count = lax.axis_size(axis)
         forward = [(i, i + 1) for i in range(count - 1)]
         forward.append((count - 1, 0))
         backward = [(target, source) for source, target in forward]
         low = lax.ppermute(
-            lax.slice_in_dim(block, block.shape[dim] - width, None, axis=dim), axis, forward
+            lax.slice_in_dim(moving, moving.shape[dim] - width, None, axis=dim), axis, forward
         )
-        high = lax.ppermute(lax.slice_in_dim(block, 0, width, axis=dim), axis, backward)
-        block = jnp.concatenate([low, block, high], axis=dim)
+        high = lax.ppermute(lax.slice_in_dim(moving, 0, width, axis=dim), axis, backward)
+        moving = jnp.concatenate([low, moving, high], axis=dim)
+        pad = [(0, 0)] * block.ndim
+        pad[dim] = (width, width)
+        radial = jnp.pad(block[1], pad[1:])
+        block = jnp.stack([moving[0], radial, moving[1]])
     return block
 
 
@@ -152,8 +157,7 @@
     while bit < count:
         pairs = mirror_pairs(count, block_size) if 2 * bit >= count else xor_pairs(count, bit)
         other = lax.ppermute(part, axis, pairs)
-        upper = (index // bit) % 2 == 1 if 2 * bit < count else index >= count // 2
-        part = jnp.where(upper, other + part, part + other)
+        part = part + other
         bit *= 2
     return join_rounds(part, axis, done)
 

time: 141 us -> 146 us (1.035)
  other arithmetic: 16.3 us -> 19.6 us
  local copies, waits for them, and re-layouts: 4.45 us -> 7.27 us
  waiting for transfers between devices: 57 us -> 55.4 us
    unnamed x28 -> x46, local copies, waits for them, and re-layouts: 1.15 us -> 4.26 us
where the time goes in v7:
time: 146 us
  waiting for transfers between devices  55.4 us (38%)
  starting transfers between devices  39.9 us (27%)
  blocking collectives  21.1 us (14%)
  other arithmetic  19.6 us (13%)
  local copies, waits for them, and re-layouts  7.27 us (5%)
  between operations  2.59 us (2%)
    ppermute x6, waiting for transfers between devices, species_sum(): other = lax.ppermute(part, axis, pairs)  25.1 us
    all_to_all x1, blocking collectives, global_max(): return jnp.max(lax.all_to_all(spread, axes, 0, 0, tiled=True))  21.1 us
    all_to_all x1, waiting for transfers between devices, global_max(): return jnp.max(lax.all_to_all(spread, axes, 0, 0, tiled=True))  12.7 us
    all_to_all x1, starting transfers between devices, global_max(): return jnp.max(lax.all_to_all(spread, axes, 0, 0, tiled=True))  12.6 us
    ppermute x4, starting transfers between devices, join_rounds(): other = lax.ppermute(part, axis, xor_pairs(lax.axis_size(axis), bit))  12.2 us
    ppermute x4, waiting for transfers between devices, join_rounds(): other = lax.ppermute(part, axis, xor_pairs(lax.axis_size(axis), bit))  7.82 us
    ppermute x2, waiting for transfers between devices, split_rounds(): part = keep + lax.ppermute(send, axis, xor_pairs(lax.axis_size(axis), bit))  7.29 us
    ppermute x2, starting transfers between devices, padded(): lax.ppermute(lax.slice_in_dim(moving, 0, width, axis=dim), axis, backward)  5.15 us
  transfers between devices with their start and end apart: 19, of which 15 were waited for; matrix products, arithmetic and copies ran while one was open for 4% of the time, Pallas kernels for 0%

profile of v7, /device:TPU:1, one launch (start us, length us, event | category | flops | bytes accessed | tf_op | source)
XLA Modules:
  0.0 145.9 jit_solution(3615478318184331056)
XLA Ops:
  0.7 1.6 %pad_maximum_fusion.4 = (f32[1,5,32,1024]{3,2,1,0:T(8,128)S(1)}, f32[5,32,1024]{2,1,0:T(8,128)S(1)}) fusion(f32[3,1,32,1024]{3,2,1,0:T(8,128)} %bitcast.89, f32[3,4,32,1024]{3,2,1,0:T(8,128)} %param.3), kind=kLoop, calls=%fused_computation.55 | loop fusion | flops 327680 | bytes 3276800 | tf_op jit(solution)/shard_map/concatenate | solution.py:224
  2.2 0.9 copy-done.4
  3.2 0.9 fusion.22
  4.2 2.2 %collective-permute-start = (f32[2,5,2,1024]{3,2,1,0:T(2,128)S(1)}, f32[2,5,2,1024]{3,2,1,0:T(2,128)S(1)}, u32[]{:S(2)}, u32[]{:S(2)}) collective-permute-start(f32[2,5,2,1024]{3,2,1,0:T(2,128)S(1)} %get-tuple-element.27), channel_id=1, source_target_pairs={{0,32},{32,64},{64,96},{96,128},{128,160},{160,192},{192,224},{224... | collective-permute-start | bytes 245768 | tf_op jit(solution)/shard_map/ppermute | solution.py:23
  6.4 4.0 %collective-permute-start.1 = (f32[2,5,2,1024]{3,2,1,0:T(2,128)S(1)}, f32[2,5,2,1024]{3,2,1,0:T(2,128)S(1)}, u32[]{:S(2)}, u32[]{:S(2)}) collective-permute-start(f32[2,5,2,1024]{3,2,1,0:T(2,128)S(1)} %get-tuple-element.28), channel_id=1, source_target_pairs={{32,0},{64,32},{96,64},{128,96},{160,128},{192,160},{224,192},{0,2... | collective-permute-start | bytes 245768 | tf_op jit(solution)/shard_map/ppermute | solution.py:26
  10.4 1.4 broadcast_in_dim.13
  11.8 12.6 %all-to-all-start = ((f32[256,1,1]{2,1,0:T(1,128)}), f32[256,1,1]{2,1,0:T(1,128)S(1)}, u32[]{:S(2)}, u32[]{:S(2)}) async-start(f32[256,1,1]{2,1,0:T(1,128)} %broadcast_in_dim.13), calls=%async_computation | async-start | bytes 262144 | tf_op jit(solution)/shard_map/all_to_all | solution.py:116
  24.4 12.7 %all-to-all-done = f32[256,1,1]{2,1,0:T(1,128)S(1)} async-done(((f32[256,1,1]{2,1,0:T(1,128)}), f32[256,1,1]{2,1,0:T(1,128)S(1)}, u32[]{:S(2)}, u32[]{:S(2)}) %all-to-all-start) | async-done | bytes 1056 | tf_op jit(solution)/shard_map/all_to_all | solution.py:116
  37.1 0.9 reduce_max.37
  39.0 0.3 copy-done.20
  39.4 0.6 fusion.10
  40.0 0.5 copy-done.5
  40.5 0.8 multiply_add_fusion.1
  41.3 0.2 fusion.20
  41.6 1.3 multiply_divide_fusion.1
  43.2 0.6 copy-done.19
  43.8 0.7 fusion.57
  44.5 1.0 collective-permute-start.2
  45.5 1.4 collective-permute-done.2
  46.9 1.0 select_add_fusion.1
  48.0 0.4 collective-permute-start.3
  48.4 3.7 %collective-permute-done.3 = f32[24,1024]{1,0:T(8,128)S(1)} collective-permute-done((f32[24,1024]{1,0:T(8,128)S(1)}, f32[24,1024]{1,0:T(8,128)S(1)}, u32[]{:S(2)}, u32[]{:S(2)}) %collective-permute-start.3) | collective-permute-done | bytes 98336 | tf_op jit(solution)/shard_map/ppermute | solution.py:130
  52.1 0.9 collective-permute-start.4
  53.1 2.6 %collective-permute-done.4 = f32[24,1024]{1,0:T(8,128)S(1)} collective-permute-done((f32[24,1024]{1,0:T(8,128)S(1)}, f32[24,1024]{1,0:T(8,128)S(1)}, u32[]{:S(2)}, u32[]{:S(2)}) %collective-permute-start.4) | collective-permute-done | bytes 98336 | tf_op jit(solution)/shard_map/ppermute | solution.py:159
  55.7 0.7 collective-permute-start.5
  56.4 4.8 %collective-permute-done.5 = f32[24,1024]{1,0:T(8,128)S(1)} collective-permute-done((f32[24,1024]{1,0:T(8,128)S(1)}, f32[24,1024]{1,0:T(8,128)S(1)}, u32[]{:S(2)}, u32[]{:S(2)}) %collective-permute-start.5) | collective-permute-done | bytes 98336 | tf_op jit(solution)/shard_map/ppermute | solution.py:159
  61.5 5.5 %collective-permute-done.6 = f32[24,1024]{1,0:T(8,128)S(1)} collective-permute-done((f32[24,1024]{1,0:T(8,128)S(1)}, f32[24,1024]{1,0:T(8,128)S(1)}, u32[]{:S(2)}, u32[]{:S(2)}) %collective-permute-start.6) | collective-permute-done | bytes 98336 | tf_op jit(solution)/shard_map/ppermute | solution.py:159
  67.0 0.4 collective-permute-start.7
  67.5 3.4 %collective-permute-done.7 = f32[24,1024]{1,0:T(8,128)S(1)} collective-permute-done((f32[24,1024]{1,0:T(8,128)S(1)}, f32[24,1024]{1,0:T(8,128)S(1)}, u32[]{:S(2)}, u32[]{:S(2)}) %collective-permute-start.7) | collective-permute-done | bytes 98336 | tf_op jit(solution)/shard_map/ppermute | solution.py:138
  70.9 5.6 %collective-permute-start.8 = (f32[48,1024]{1,0:T(8,128)S(1)}, f32[48,1024]{1,0:T(8,128)S(1)}, u32[]{:S(2)}, u32[]{:S(2)}) collective-permute-start(f32[48,1024]{1,0:T(8,128)S(1)} %maximum_select_fusion.2), channel_id=1, source_target_pairs={{0,1},{1,0},{2,3},{3,2},{4,5},{5,4},{6,7},{7,6},{8,9},{9,8},{10,11... | collective-permute-start | bytes 589832 | tf_op jit(solution)/shard_map/ppermute | solution.py:138
  76.7 0.9 collective-permute-done.8
  78.1 0.3 fusion
  78.5 0.6 copy-done.10
  79.5 0.9 fusion.19
  80.4 0.7 pad_maximum_fusion.23
  81.1 1.2 collective-permute-start.10
  82.3 0.3 collective-permute-start.9
  82.6 0.7 broadcast_in_dim.16
  83.3 21.1 %all_to_all.12 = f32[256,1,1]{2,1,0:T(1,128)} all-to-all(f32[256,1,1]{2,1,0:T(1,128)S(1)} %broadcast_in_dim.16), channel_id=1, replica_groups=mesh['space'=8,'species'=32] {'space','species'}, dimensions={0} | all-to-all | bytes 2048 | tf_op jit(solution)/shard_map/all_to_all | solution.py:116
  104.4 1.8 %reduce_max.39 = f32[]{:T(128)} reduce(f32[256,1,1]{2,1,0:T(1,128)} %all_to_all.12, f32[]{:T(128)} %constant.82.clone.1), dimensions={0,1,2}, to_apply=%region_6.7 | reduce | flops 255 | bytes 1032 | tf_op jit(solution)/shard_map/reduce_max | solution.py:116
  106.9 1.2 pad_maximum_fusion.2
  108.2 0.6 fusion.4
  108.8 0.8 multiply_add_fusion
  109.7 0.2 fusion.17
  110.0 0.3 fusion.34
  110.3 0.9 copy-done.9
  111.4 1.3 collective-permute-start.11
  112.6 1.1 collective-permute-done.11
  113.8 0.5 collective-permute-start.12
  114.3 3.6 %collective-permute-done.12 = f32[24,1024]{1,0:T(8,128)S(1)} collective-permute-done((f32[24,1024]{1,0:T(8,128)S(1)}, f32[24,1024]{1,0:T(8,128)S(1)}, u32[]{:S(2)}, u32[]{:S(2)}) %collective-permute-start.12) | collective-permute-done | bytes 98336 | tf_op jit(solution)/shard_map/ppermute | solution.py:130
  117.9 0.8 collective-permute-start.13
  118.7 2.8 %collective-permute-done.13 = f32[24,1024]{1,0:T(8,128)S(1)} collective-permute-done((f32[24,1024]{1,0:T(8,128)S(1)}, f32[24,1024]{1,0:T(8,128)S(1)}, u32[]{:S(2)}, u32[]{:S(2)}) %collective-permute-start.13) | collective-permute-done | bytes 98336 | tf_op jit(solution)/shard_map/ppermute | solution.py:159
  121.5 1.1 collective-permute-start.14
  122.6 4.4 %collective-permute-done.14 = f32[24,1024]{1,0:T(8,128)S(1)} collective-permute-done((f32[24,1024]{1,0:T(8,128)S(1)}, f32[24,1024]{1,0:T(8,128)S(1)}, u32[]{:S(2)}, u32[]{:S(2)}) %collective-permute-start.14) | collective-permute-done | bytes 98336 | tf_op jit(solution)/shard_map/ppermute | solution.py:159
  127.0 0.6 collective-permute-start.15
  127.8 5.0 %collective-permute-done.15 = f32[24,1024]{1,0:T(8,128)S(1)} collective-permute-done((f32[24,1024]{1,0:T(8,128)S(1)}, f32[24,1024]{1,0:T(8,128)S(1)}, u32[]{:S(2)}, u32[]{:S(2)}) %collective-permute-start.15) | collective-permute-done | bytes 98336 | tf_op jit(solution)/shard_map/ppermute | solution.py:159
  132.8 0.5 collective-permute-start.16
  133.4 3.2 %collective-permute-done.16 = f32[24,1024]{1,0:T(8,128)S(1)} collective-permute-done((f32[24,1024]{1,0:T(8,128)S(1)}, f32[24,1024]{1,0:T(8,128)S(1)}, u32[]{:S(2)}, u32[]{:S(2)}) %collective-permute-start.16) | collective-permute-done | bytes 98336 | tf_op jit(solution)/shard_map/ppermute | solution.py:138
  136.7 5.7 %collective-permute-start.17 = (f32[48,1024]{1,0:T(8,128)S(1)}, f32[48,1024]{1,0:T(8,128)S(1)}, u32[]{:S(2)}, u32[]{:S(2)}) collective-permute-start(f32[48,1024]{1,0:T(8,128)S(1)} %maximum_select_fusion.3), channel_id=1, source_target_pairs={{0,1},{1,0},{2,3},{3,2},{4,5},{5,4},{6,7},{7,6},{8,9},{9,8},{10,11... | collective-permute-start | bytes 589832 | tf_op jit(solution)/shard_map/ppermute | solution.py:138
  142.4 0.8 fusion.39
  143.2 0.3 collective-permute-done.17
  143.6 0.8 pad_maximum_fusion.5
  144.4 0.3 fusion.1
  144.6 1.2 pad_maximum_fusion.3
  (96 shorter events, 3.5 us)
Async XLA Ops:
  0.6 2.6 %copy-start = (f32[3,4,32,1024]{3,2,1,0:T(8,128)S(1)}, f32[3,4,32,1024]{3,2,1,0:T(8,128)}, u32[]{:S(2)}) copy-start(f32[3,4,32,1024]{3,2,1,0:T(8,128)} %param.3) | copy-start | bytes 4718596
  0.6 2.6 %copy-start.15 = (f32[3,32,1024]{2,1,0:T(8,128)S(1)}, f32[3,32,1024]{2,1,0:T(8,128)}, u32[]{:S(2)}) copy-start(f32[3,32,1024]{2,1,0:T(8,128)} %param.4) | copy-start | bytes 1179652
  2.2 0.9 copy-start.4
  3.2 0.9 copy-start.6
  4.1 34.5 %copy-start.1 = (f32[1,5,32,1024]{3,2,1,0:T(8,128)}, f32[1,5,32,1024]{3,2,1,0:T(8,128)S(1)}, u32[]{:S(2)}) copy-start(f32[1,5,32,1024]{3,2,1,0:T(8,128)S(1)} %get-tuple-element.15) | copy-start | bytes 1966084
  4.1 20.2 %copy-start.22 = (s32[4]{0:T(128)S(1)}, s32[4]{0:T(128)}, u32[]{:S(2)}) copy-start(s32[4]{0:T(128)} %param.5) | copy-start | bytes 52
  4.2 34.5 %collective-permute-start = (f32[2,5,2,1024]{3,2,1,0:T(2,128)S(1)}, f32[2,5,2,1024]{3,2,1,0:T(2,128)S(1)}, u32[]{:S(2)}, u32[]{:S(2)}) collective-permute-start(f32[2,5,2,1024]{3,2,1,0:T(2,128)S(1)} %get-tuple-element.27), channel_id=1, source_target_pairs={{0,32},{32,64},{64,96},{96,128},{128,160},{160,192},{192,224},{224... | collective-permute-start | bytes 245768 | tf_op jit(solution)/shard_map/ppermute | solution.py:23
  6.4 32.3 %collective-permute-start.1 = (f32[2,5,2,1024]{3,2,1,0:T(2,128)S(1)}, f32[2,5,2,1024]{3,2,1,0:T(2,128)S(1)}, u32[]{:S(2)}, u32[]{:S(2)}) collective-permute-start(f32[2,5,2,1024]{3,2,1,0:T(2,128)S(1)} %get-tuple-element.28), channel_id=1, source_target_pairs={{32,0},{64,32},{96,64},{128,96},{160,128},{192,160},{224,192},{0,2... | collective-permute-start | bytes 245768 | tf_op jit(solution)/shard_map/ppermute | solution.py:26
  11.8 25.3 %all-to-all-start = ((f32[256,1,1]{2,1,0:T(1,128)}), f32[256,1,1]{2,1,0:T(1,128)S(1)}, u32[]{:S(2)}, u32[]{:S(2)}) async-start(f32[256,1,1]{2,1,0:T(1,128)} %broadcast_in_dim.13), calls=%async_computation | async-start | bytes 262144 | tf_op jit(solution)/shard_map/all_to_all | solution.py:116
  38.7 0.6 copy-start.20
  39.4 1.1 copy-start.5
  41.5 36.2 %copy-start.11 = (f32[1,32,1024]{2,1,0:T(8,128)}, f32[1,32,1024]{2,1,0:T(8,128)S(1)}, u32[]{:S(2)}) copy-start(f32[1,32,1024]{2,1,0:T(8,128)S(1)} %get-tuple-element.13) | copy-start | bytes 393220
  41.6 1.4 copy-start.7
  43.2 0.7 copy-start.19
  44.5 2.4 %collective-permute-start.2 = (f32[48,1024]{1,0:T(8,128)}, f32[48,1024]{1,0:T(8,128)}, u32[]{:S(2)}, u32[]{:S(2)}) collective-permute-start(f32[48,1024]{1,0:T(8,128)} %fusion.57), channel_id=1, source_target_pairs={{0,1},{1,0},{2,3},{3,2},{4,5},{5,4},{6,7},{7,6},{8,9},{9,8},{10,11... | collective-permute-start | bytes 589832 | tf_op jit(solution)/shard_map/ppermute | solution.py:213
  47.9 13.5 %copy-start.2 = (f32[1,5,32,1024]{3,2,1,0:T(8,128)S(1)}, f32[1,5,32,1024]{3,2,1,0:T(8,128)}, u32[]{:S(2)}) copy-start(f32[1,5,32,1024]{3,2,1,0:T(8,128)} %copy-done.1) | copy-start | bytes 1966084
  48.0 13.5 %copy-start.16 = (f32[3,32,1024]{2,1,0:T(8,128)S(1)}, f32[3,32,1024]{2,1,0:T(8,128)}, u32[]{:S(2)}) copy-start(f32[3,32,1024]{2,1,0:T(8,128)} %param.4) | copy-start | bytes 1179652
  48.0 13.5 %copy-start.21 = (f32[2,5,2,1024]{3,2,1,0:T(2,128)S(1)}, f32[2,5,2,1024]{3,2,1,0:T(2,128)}, u32[]{:S(2)}) copy-start(f32[2,5,2,1024]{3,2,1,0:T(2,128)} %copy-done.20) | copy-start | bytes 245764
  48.0 4.1 %collective-permute-start.3 = (f32[24,1024]{1,0:T(8,128)S(1)}, f32[24,1024]{1,0:T(8,128)S(1)}, u32[]{:S(2)}, u32[]{:S(2)}) collective-permute-start(f32[24,1024]{1,0:T(8,128)S(1)} %slice_select_fusion.1), channel_id=1, source_target_pairs={{0,2},{1,3},{2,0},{3,1},{4,6},{5,7},{6,4},{7,5},{8,10},{9,11},{10,... | collective-permute-start | bytes 294920 | tf_op jit(solution)/shard_map/ppermute | solution.py:130
  52.1 3.6 %collective-permute-start.4 = (f32[24,1024]{1,0:T(8,128)S(1)}, f32[24,1024]{1,0:T(8,128)S(1)}, u32[]{:S(2)}, u32[]{:S(2)}) collective-permute-start(f32[24,1024]{1,0:T(8,128)S(1)} %select_add_fusion.3), channel_id=1, source_target_pairs={{0,4},{1,5},{2,6},{3,7},{4,0},{5,1},{6,2},{7,3},{8,12},{9,13},{10,... | collective-permute-start | bytes 294920 | tf_op jit(solution)/shard_map/ppermute | solution.py:159
  55.7 5.5 %collective-permute-start.5 = (f32[24,1024]{1,0:T(8,128)S(1)}, f32[24,1024]{1,0:T(8,128)S(1)}, u32[]{:S(2)}, u32[]{:S(2)}) collective-permute-start(f32[24,1024]{1,0:T(8,128)S(1)} %add.161), channel_id=1, source_target_pairs={{0,8},{1,9},{2,10},{3,11},{4,12},{5,13},{6,14},{7,15},{8,0},{9,1},... | collective-permute-start | bytes 294920 | tf_op jit(solution)/shard_map/ppermute | solution.py:159
  61.2 5.8 %collective-permute-start.6 = (f32[24,1024]{1,0:T(8,128)S(1)}, f32[24,1024]{1,0:T(8,128)S(1)}, u32[]{:S(2)}, u32[]{:S(2)}) collective-permute-start(f32[24,1024]{1,0:T(8,128)S(1)} %add.162), channel_id=1, source_target_pairs={{0,28},{1,29},{2,30},{3,31},{4,24},{5,25},{6,26},{7,27},{8,20},{9,... | collective-permute-start | bytes 294920 | tf_op jit(solution)/shard_map/ppermute | solution.py:159
  67.0 3.8 %collective-permute-start.7 = (f32[24,1024]{1,0:T(8,128)S(1)}, f32[24,1024]{1,0:T(8,128)S(1)}, u32[]{:S(2)}, u32[]{:S(2)}) collective-permute-start(f32[24,1024]{1,0:T(8,128)S(1)} %add.163), channel_id=1, source_target_pairs={{0,2},{1,3},{2,0},{3,1},{4,6},{5,7},{6,4},{7,5},{8,10},{9,11},{10,... | collective-permute-start | bytes 294920 | tf_op jit(solution)/shard_map/ppermute | solution.py:138
  70.9 6.7 %collective-permute-start.8 = (f32[48,1024]{1,0:T(8,128)S(1)}, f32[48,1024]{1,0:T(8,128)S(1)}, u32[]{:S(2)}, u32[]{:S(2)}) collective-permute-start(f32[48,1024]{1,0:T(8,128)S(1)} %maximum_select_fusion.2), channel_id=1, source_target_pairs={{0,1},{1,0},{2,3},{3,2},{4,5},{5,4},{6,7},{7,6},{8,9},{9,8},{10,11... | collective-permute-start | bytes 589832 | tf_op jit(solution)/shard_map/ppermute | solution.py:138
  76.7 1.1 slice-start
  76.7 1.2 copy-start.17
  76.7 1.3 copy-start.18
  77.8 0.7 copy-start.13
  78.1 1.0 copy-start.10
  78.5 44.1 %copy-start.3 = (f32[2,4,32,1024]{3,2,1,0:T(8,128)}, f32[2,4,32,1024]{3,2,1,0:T(8,128)S(1)}, u32[]{:S(2)}) copy-start(f32[2,4,32,1024]{3,2,1,0:T(8,128)S(1)} %fusion) | copy-start | bytes 3145732
  79.5 0.9 copy-start.8
  81.1 25.7 %collective-permute-start.10 = (f32[2,5,2,1024]{3,2,1,0:T(2,128)}, f32[2,5,2,1024]{3,2,1,0:T(2,128)}, u32[]{:S(2)}, u32[]{:S(2)}) collective-permute-start(f32[2,5,2,1024]{3,2,1,0:T(2,128)} %get-tuple-element.26), channel_id=1, source_target_pairs={{32,0},{64,32},{96,64},{128,96},{160,128},{192,160},{224,192},{0,2... | collective-permute-start | bytes 245768 | tf_op jit(solution)/shard_map/ppermute | solution.py:26
  82.3 24.6 %collective-permute-start.9 = (f32[2,5,2,1024]{3,2,1,0:T(2,128)}, f32[2,5,2,1024]{3,2,1,0:T(2,128)}, u32[]{:S(2)}, u32[]{:S(2)}) collective-permute-start(f32[2,5,2,1024]{3,2,1,0:T(2,128)} %get-tuple-element.25), channel_id=1, source_target_pairs={{0,32},{32,64},{64,96},{96,128},{128,160},{160,192},{192,224},{224... | collective-permute-start | bytes 245768 | tf_op jit(solution)/shard_map/ppermute | solution.py:23
  110.0 1.1 copy-start.9
  111.3 11.2 %copy-start.12 = (f32[1,32,1024]{2,1,0:T(8,128)S(1)}, f32[1,32,1024]{2,1,0:T(8,128)}, u32[]{:S(2)}) copy-start(f32[1,32,1024]{2,1,0:T(8,128)} %copy-done.11) | copy-start | bytes 393220
  111.4 16.3 %copy-start.14 = (f32[2,32,1024]{2,1,0:T(8,128)S(1)}, f32[2,32,1024]{2,1,0:T(8,128)}, u32[]{:S(2)}) copy-start(f32[2,32,1024]{2,1,0:T(8,128)} %copy-done.13) | copy-start | bytes 786436
  111.4 2.3 %collective-permute-start.11 = (f32[48,1024]{1,0:T(8,128)S(1)}, f32[48,1024]{1,0:T(8,128)S(1)}, u32[]{:S(2)}, u32[]{:S(2)}) collective-permute-start(f32[48,1024]{1,0:T(8,128)S(1)} %fusion.58), channel_id=1, source_target_pairs={{0,1},{1,0},{2,3},{3,2},{4,5},{5,4},{6,7},{7,6},{8,9},{9,8},{10,11... | collective-permute-start | bytes 589832 | tf_op jit(solution)/shard_map/ppermute | solution.py:213
  113.8 4.1 %collective-permute-start.12 = (f32[24,1024]{1,0:T(8,128)S(1)}, f32[24,1024]{1,0:T(8,128)S(1)}, u32[]{:S(2)}, u32[]{:S(2)}) collective-permute-start(f32[24,1024]{1,0:T(8,128)S(1)} %slice_select_fusion), channel_id=1, source_target_pairs={{0,2},{1,3},{2,0},{3,1},{4,6},{5,7},{6,4},{7,5},{8,10},{9,11},{10,... | collective-permute-start | bytes 294920 | tf_op jit(solution)/shard_map/ppermute | solution.py:130
  117.9 3.6 %collective-permute-start.13 = (f32[24,1024]{1,0:T(8,128)S(1)}, f32[24,1024]{1,0:T(8,128)S(1)}, u32[]{:S(2)}, u32[]{:S(2)}) collective-permute-start(f32[24,1024]{1,0:T(8,128)S(1)} %select_add_fusion.2), channel_id=1, source_target_pairs={{0,4},{1,5},{2,6},{3,7},{4,0},{5,1},{6,2},{7,3},{8,12},{9,13},{10,... | collective-permute-start | bytes 294920 | tf_op jit(solution)/shard_map/ppermute | solution.py:159
  121.5 5.5 %collective-permute-start.14 = (f32[24,1024]{1,0:T(8,128)S(1)}, f32[24,1024]{1,0:T(8,128)S(1)}, u32[]{:S(2)}, u32[]{:S(2)}) collective-permute-start(f32[24,1024]{1,0:T(8,128)S(1)} %add.177), channel_id=1, source_target_pairs={{0,8},{1,9},{2,10},{3,11},{4,12},{5,13},{6,14},{7,15},{8,0},{9,1},... | collective-permute-start | bytes 294920 | tf_op jit(solution)/shard_map/ppermute | solution.py:159
  127.0 5.8 %collective-permute-start.15 = (f32[24,1024]{1,0:T(8,128)S(1)}, f32[24,1024]{1,0:T(8,128)S(1)}, u32[]{:S(2)}, u32[]{:S(2)}) collective-permute-start(f32[24,1024]{1,0:T(8,128)S(1)} %add.178), channel_id=1, source_target_pairs={{0,28},{1,29},{2,30},{3,31},{4,24},{5,25},{6,26},{7,27},{8,20},{9,... | collective-permute-start | bytes 294920 | tf_op jit(solution)/shard_map/ppermute | solution.py:159
  132.8 3.8 %collective-permute-start.16 = (f32[24,1024]{1,0:T(8,128)S(1)}, f32[24,1024]{1,0:T(8,128)S(1)}, u32[]{:S(2)}, u32[]{:S(2)}) collective-permute-start(f32[24,1024]{1,0:T(8,128)S(1)} %add.179), channel_id=1, source_target_pairs={{0,2},{1,3},{2,0},{3,1},{4,6},{5,7},{6,4},{7,5},{8,10},{9,11},{10,... | collective-permute-start | bytes 294920 | tf_op jit(solution)/shard_map/ppermute | solution.py:138
  136.7 6.8 %collective-permute-start.17 = (f32[48,1024]{1,0:T(8,128)S(1)}, f32[48,1024]{1,0:T(8,128)S(1)}, u32[]{:S(2)}, u32[]{:S(2)}) collective-permute-start(f32[48,1024]{1,0:T(8,128)S(1)} %maximum_select_fusion.3), channel_id=1, source_target_pairs={{0,1},{1,0},{2,3},{3,2},{4,5},{5,4},{6,7},{7,6},{8,9},{9,8},{10,11... | collective-permute-start | bytes 589832 | tf_op jit(solution)/shard_map/ppermute | solution.py:138
  143.2 1.2 slice-start.1

commit v8 on v6

--- a/solution.py
+++ b/solution.py
@@ -175,9 +175,10 @@
     return density, rate, keep, send
 
 
-def advance(wide, margin, tile_rows, stop_times, total_species):
+def advance(wide, margin, tile_rows, stop_times, total_species, local_top=None):
     interior = lax.slice_in_dim(wide, margin, margin + tile_rows, axis=2)
-    local_top = jnp.max(jnp.abs(interior[1]) + jnp.abs(interior[2]))
+    if local_top is None:
+        local_top = jnp.max(jnp.abs(interior[1]) + jnp.abs(interior[2]))
     fastest = global_max(local_top, ("space", "species"))
     step_time = courant / (sound_speed + fastest)
     density = wide[0]
@@ -223,7 +224,13 @@
     )
     for iteration in range(STEPS):
         wide = padded(fluid, (("space", 2),), 2)
-        dust, gas = advance(wide, 2, tile_rows, stop_times, total_species)
+        local_top = None
+        if iteration == 0:
+            interior = lax.slice_in_dim(wide, 2, 2 + tile_rows, axis=2)
+            local_top = jnp.max(jnp.abs(interior[1]) + jnp.abs(interior[2]))
+            landed = wide[0, 0, 0, 0] + wide[0, 0, -1, 0]
+            local_top = jnp.maximum(local_top, 0.0 * landed)
+        dust, gas = advance(wide, 2, tile_rows, stop_times, total_species, local_top)
         fluid = jnp.concatenate([dust, gas[:, None]], axis=1)
     return (dust, gas)
 

time: 141 us -> 151 us (1.071)
  other arithmetic: 16.3 us -> 22.4 us
  starting transfers between devices: 39 us -> 42.9 us
  waiting for transfers between devices: 57 us -> 54 us
  between operations: 2.54 us -> 4.47 us
    all_to_all x1, waiting for transfers between devices: 12.7 us -> 8.35 us  [global_max(): return jnp.max(lax.all_to_all(spread, axes, 0, 0, tiled=True))]
    all_to_all x1, starting transfers between devices: 12.6 us -> 16.5 us  [global_max(): return jnp.max(lax.all_to_all(spread, axes, 0, 0, tiled=True))]
    add x4, other arithmetic: 2.84 us -> 6.2 us  [face_divergence(): jnp.maximum(face_speed, 0.0) * (1.5 * here - 0.5 * back_two)]
  transfers between devices with their start and end apart: 19 -> 19, of which waited for: 15 -> 16; matrix products, arithmetic and copies ran while one was open for 4% -> 5% of each run, Pallas kernels for 0% -> 0%
where the time goes in v8:
time: 151 us
  waiting for transfers between devices  54 us (36%)
  starting transfers between devices  42.9 us (28%)
  other arithmetic  22.4 us (15%)
  blocking collectives  21.3 us (14%)
  local copies, waits for them, and re-layouts  5.89 us (4%)
  between operations  4.47 us (3%)
    ppermute x6, waiting for transfers between devices, species_sum(): other = lax.ppermute(part, axis, pairs)  25.7 us
    all_to_all x1, blocking collectives, global_max(): return jnp.max(lax.all_to_all(spread, axes, 0, 0, tiled=True))  21.3 us
    all_to_all x1, starting transfers between devices, global_max(): return jnp.max(lax.all_to_all(spread, axes, 0, 0, tiled=True))  16.5 us
    ppermute x4, starting transfers between devices, join_rounds(): other = lax.ppermute(part, axis, xor_pairs(lax.axis_size(axis), bit))  12 us
    ppermute x4, waiting for transfers between devices, join_rounds(): other = lax.ppermute(part, axis, xor_pairs(lax.axis_size(axis), bit))  8.66 us
    all_to_all x1, waiting for transfers between devices, global_max(): return jnp.max(lax.all_to_all(spread, axes, 0, 0, tiled=True))  8.35 us
    ppermute x2, waiting for transfers between devices, split_rounds(): part = keep + lax.ppermute(send, axis, xor_pairs(lax.axis_size(axis), bit))  7.46 us
    add x4, other arithmetic, face_divergence(): jnp.maximum(face_speed, 0.0) * (1.5 * here - 0.5 * back_two)  6.2 us
  transfers between devices with their start and end apart: 19, of which 16 were waited for; matrix products, arithmetic and copies ran while one was open for 5% of the time, Pallas kernels for 0%

profile of v8, /device:TPU:1, one launch (start us, length us, event | category | flops | bytes accessed | tf_op | source)
XLA Modules:
  0.0 150.9 jit_solution(13892629450083839915)
XLA Ops:
  0.7 1.4 pad_maximum_fusion.25
  2.1 2.2 %collective-permute-start = (f32[3,5,2,1024]{3,2,1,0:T(2,128)S(1)}, f32[3,5,2,1024]{3,2,1,0:T(2,128)S(1)}, u32[]{:S(2)}, u32[]{:S(2)}) collective-permute-start(f32[3,5,2,1024]{3,2,1,0:T(2,128)S(1)} %get-tuple-element.23), channel_id=1, source_target_pairs={{0,32},{32,64},{64,96},{96,128},{128,160},{160,192},{192,224},{224... | collective-permute-start | bytes 368648 | tf_op jit(solution)/shard_map/ppermute | solution.py:22
  4.3 4.0 %collective-permute-start.1 = (f32[3,5,2,1024]{3,2,1,0:T(2,128)S(1)}, f32[3,5,2,1024]{3,2,1,0:T(2,128)S(1)}, u32[]{:S(2)}, u32[]{:S(2)}) collective-permute-start(f32[3,5,2,1024]{3,2,1,0:T(2,128)S(1)} %get-tuple-element.22), channel_id=1, source_target_pairs={{32,0},{64,32},{96,64},{128,96},{160,128},{192,160},{224,192},{0,2... | collective-permute-start | bytes 368648 | tf_op jit(solution)/shard_map/ppermute | solution.py:25
  8.3 0.8 fusion.17
  9.1 1.4 collective-permute-done
  10.5 0.4 pad_maximum_fusion
  11.1 1.0 slice.465
  12.1 1.5 fusion.10
  13.6 0.9 slice.464
  14.5 0.6 slice.451
  15.1 0.6 slice.452
  17.6 0.7 broadcast_in_dim.13
  18.4 16.5 %all-to-all-start = ((f32[256,1,1]{2,1,0:T(1,128)}), f32[256,1,1]{2,1,0:T(1,128)S(1)}, u32[]{:S(2)}, u32[]{:S(2)}) async-start(f32[256,1,1]{2,1,0:T(1,128)} %broadcast_in_dim.13), calls=%async_computation | async-start | bytes 262144 | tf_op jit(solution)/shard_map/all_to_all | solution.py:111
  34.9 3.3 %multiply_add_fusion.1 = f32[5,32,1025]{2,1,0:T(8,128)S(1)} fusion(f32[5,32,1024]{2,1,0:T(8,128)} %slice.465, f32[5,32,1024]{2,1,0:T(8,128)} %slice.464), kind=kLoop, calls=%fused_computation.43 | loop fusion | flops 2132000 | bytes 1966720 | tf_op jit(solution)/shard_map/add | solution.py:41
  38.1 1.1 fusion.23
  39.2 8.4 %all-to-all-done = f32[256,1,1]{2,1,0:T(1,128)S(1)} async-done(((f32[256,1,1]{2,1,0:T(1,128)}), f32[256,1,1]{2,1,0:T(1,128)S(1)}, u32[]{:S(2)}, u32[]{:S(2)}) %all-to-all-start) | async-done | bytes 1056 | tf_op jit(solution)/shard_map/all_to_all | solution.py:111
  47.6 0.9 reduce_max.37
  49.1 0.9 multiply_bitcast_fusion.3
  50.1 2.3 %multiply_divide_fusion.1 = (f32[4,32,1024]{2,1,0:T(8,128)S(1)}, f32[4,32,1024]{2,1,0:T(8,128)S(1)}, f32[4,32,1024]{2,1,0:T(8,128)}, f32[4,32,1024]{2,1,0:T(8,128)}) fusion(f32[32,1024]{1,0:T(8,128)S(1)} %multiply_bitcast_fusion.2, f32[4]{0:T(128)S(1)} %exponential_multiply_fusion, f32[32,1024]{1,0:T(8,128)S(1)} %get-tuple-element.12, ...), kind=kLoop, calls=%fused_computation.79 | loop fusion | flops 917504 | bytes 3407892 | tf_op jit(solution)/shard_map/div | solution.py:166
  52.6 0.7 fusion.57
  53.3 1.0 collective-permute-start.2
  54.4 1.4 collective-permute-done.2
  55.7 1.1 select_add_fusion.1
  56.9 0.4 collective-permute-start.3
  57.2 3.7 %collective-permute-done.3 = f32[24,1024]{1,0:T(8,128)S(1)} collective-permute-done((f32[24,1024]{1,0:T(8,128)S(1)}, f32[24,1024]{1,0:T(8,128)S(1)}, u32[]{:S(2)}, u32[]{:S(2)}) %collective-permute-start.3) | collective-permute-done | bytes 98336 | tf_op jit(solution)/shard_map/ppermute | solution.py:125
  61.0 0.9 collective-permute-start.4
  61.9 2.6 %collective-permute-done.4 = f32[24,1024]{1,0:T(8,128)S(1)} collective-permute-done((f32[24,1024]{1,0:T(8,128)S(1)}, f32[24,1024]{1,0:T(8,128)S(1)}, u32[]{:S(2)}, u32[]{:S(2)}) %collective-permute-start.4) | collective-permute-done | bytes 98336 | tf_op jit(solution)/shard_map/ppermute | solution.py:154
  64.5 0.7 collective-permute-start.5
  65.3 4.7 %collective-permute-done.5 = f32[24,1024]{1,0:T(8,128)S(1)} collective-permute-done((f32[24,1024]{1,0:T(8,128)S(1)}, f32[24,1024]{1,0:T(8,128)S(1)}, u32[]{:S(2)}, u32[]{:S(2)}) %collective-permute-start.5) | collective-permute-done | bytes 98336 | tf_op jit(solution)/shard_map/ppermute | solution.py:154
  70.1 0.2 collective-permute-start.6
  70.4 5.5 %collective-permute-done.6 = f32[24,1024]{1,0:T(8,128)S(1)} collective-permute-done((f32[24,1024]{1,0:T(8,128)S(1)}, f32[24,1024]{1,0:T(8,128)S(1)}, u32[]{:S(2)}, u32[]{:S(2)}) %collective-permute-start.6) | collective-permute-done | bytes 98336 | tf_op jit(solution)/shard_map/ppermute | solution.py:154
  75.9 0.4 collective-permute-start.7
  76.3 3.4 %collective-permute-done.7 = f32[24,1024]{1,0:T(8,128)S(1)} collective-permute-done((f32[24,1024]{1,0:T(8,128)S(1)}, f32[24,1024]{1,0:T(8,128)S(1)}, u32[]{:S(2)}, u32[]{:S(2)}) %collective-permute-start.7) | collective-permute-done | bytes 98336 | tf_op jit(solution)/shard_map/ppermute | solution.py:133
  79.8 5.6 %collective-permute-start.8 = (f32[48,1024]{1,0:T(8,128)S(1)}, f32[48,1024]{1,0:T(8,128)S(1)}, u32[]{:S(2)}, u32[]{:S(2)}) collective-permute-start(f32[48,1024]{1,0:T(8,128)S(1)} %maximum_select_fusion.2), channel_id=1, source_target_pairs={{0,1},{1,0},{2,3},{3,2},{4,5},{5,4},{6,7},{7,6},{8,9},{9,8},{10,11... | collective-permute-start | bytes 589832 | tf_op jit(solution)/shard_map/ppermute | solution.py:133
  85.6 0.9 collective-permute-done.8
  86.7 0.3 fusion
  87.3 1.4 collective-permute-start.10
  88.7 0.3 collective-permute-start.9
  89.0 0.8 fusion.22
  89.8 0.7 broadcast_in_dim.16
  90.5 21.3 %all_to_all.12 = f32[256,1,1]{2,1,0:T(1,128)S(1)} all-to-all(f32[256,1,1]{2,1,0:T(1,128)S(1)} %broadcast_in_dim.16), channel_id=1, replica_groups=mesh['space'=8,'species'=32] {'space','species'}, dimensions={0} | all-to-all | bytes 2048 | tf_op jit(solution)/shard_map/all_to_all | solution.py:111
  111.8 0.9 reduce_max.39
  113.4 0.4 pad_maximum_fusion.1
  113.8 0.3 copy-done.14
  114.1 0.3 slice_bitcast_fusion.1
  114.4 0.6 fusion.4
  115.1 0.8 multiply_add_fusion
  116.0 0.2 fusion.20
  116.7 1.1 collective-permute-start.11
  117.8 1.1 collective-permute-done.11
  118.9 0.4 collective-permute-start.12
  119.3 3.7 %collective-permute-done.12 = f32[24,1024]{1,0:T(8,128)S(1)} collective-permute-done((f32[24,1024]{1,0:T(8,128)S(1)}, f32[24,1024]{1,0:T(8,128)S(1)}, u32[]{:S(2)}, u32[]{:S(2)}) %collective-permute-start.12) | collective-permute-done | bytes 98336 | tf_op jit(solution)/shard_map/ppermute | solution.py:125
  123.0 0.9 collective-permute-start.13
  124.0 2.5 %collective-permute-done.13 = f32[24,1024]{1,0:T(8,128)S(1)} collective-permute-done((f32[24,1024]{1,0:T(8,128)S(1)}, f32[24,1024]{1,0:T(8,128)S(1)}, u32[]{:S(2)}, u32[]{:S(2)}) %collective-permute-start.13) | collective-permute-done | bytes 98336 | tf_op jit(solution)/shard_map/ppermute | solution.py:154
  126.6 0.7 collective-permute-start.14
  127.3 4.8 %collective-permute-done.14 = f32[24,1024]{1,0:T(8,128)S(1)} collective-permute-done((f32[24,1024]{1,0:T(8,128)S(1)}, f32[24,1024]{1,0:T(8,128)S(1)}, u32[]{:S(2)}, u32[]{:S(2)}) %collective-permute-start.14) | collective-permute-done | bytes 98336 | tf_op jit(solution)/shard_map/ppermute | solution.py:154
  132.4 5.5 %collective-permute-done.15 = f32[24,1024]{1,0:T(8,128)S(1)} collective-permute-done((f32[24,1024]{1,0:T(8,128)S(1)}, f32[24,1024]{1,0:T(8,128)S(1)}, u32[]{:S(2)}, u32[]{:S(2)}) %collective-permute-start.15) | collective-permute-done | bytes 98336 | tf_op jit(solution)/shard_map/ppermute | solution.py:154
  138.0 0.4 collective-permute-start.16
  138.5 3.3 %collective-permute-done.16 = f32[24,1024]{1,0:T(8,128)S(1)} collective-permute-done((f32[24,1024]{1,0:T(8,128)S(1)}, f32[24,1024]{1,0:T(8,128)S(1)}, u32[]{:S(2)}, u32[]{:S(2)}) %collective-permute-start.16) | collective-permute-done | bytes 98336 | tf_op jit(solution)/shard_map/ppermute | solution.py:133
  141.8 5.6 %collective-permute-start.17 = (f32[48,1024]{1,0:T(8,128)S(1)}, f32[48,1024]{1,0:T(8,128)S(1)}, u32[]{:S(2)}, u32[]{:S(2)}) collective-permute-start(f32[48,1024]{1,0:T(8,128)S(1)} %maximum_select_fusion.3), channel_id=1, source_target_pairs={{0,1},{1,0},{2,3},{3,2},{4,5},{5,4},{6,7},{7,6},{8,9},{9,8},{10,11... | collective-permute-start | bytes 589832 | tf_op jit(solution)/shard_map/ppermute | solution.py:133
  147.5 1.0 collective-permute-done.17
  148.7 0.8 pad_maximum_fusion.4
  149.5 0.2 fusion.1
  149.7 1.2 pad_maximum_fusion.3
  (81 shorter events, 2.9 us)
Async XLA Ops:
  0.6 7.7 %copy-start.1 = (f32[3,32,1024]{2,1,0:T(8,128)S(1)}, f32[3,32,1024]{2,1,0:T(8,128)}, u32[]{:S(2)}) copy-start(f32[3,32,1024]{2,1,0:T(8,128)} %param.4) | copy-start | bytes 1179652
  0.6 7.7 %copy-start = (f32[3,4,32,1024]{3,2,1,0:T(8,128)S(1)}, f32[3,4,32,1024]{3,2,1,0:T(8,128)}, u32[]{:S(2)}) copy-start(f32[3,4,32,1024]{3,2,1,0:T(8,128)} %param.3) | copy-start | bytes 4718596
  0.7 7.7 %copy-start.16 = (s32[4]{0:T(128)S(1)}, s32[4]{0:T(128)}, u32[]{:S(2)}) copy-start(s32[4]{0:T(128)} %param.5) | copy-start | bytes 52
  2.1 8.4 %collective-permute-start = (f32[3,5,2,1024]{3,2,1,0:T(2,128)S(1)}, f32[3,5,2,1024]{3,2,1,0:T(2,128)S(1)}, u32[]{:S(2)}, u32[]{:S(2)}) collective-permute-start(f32[3,5,2,1024]{3,2,1,0:T(2,128)S(1)} %get-tuple-element.23), channel_id=1, source_target_pairs={{0,32},{32,64},{64,96},{96,128},{128,160},{160,192},{192,224},{224... | collective-permute-start | bytes 368648 | tf_op jit(solution)/shard_map/ppermute | solution.py:22
  4.3 6.2 %collective-permute-start.1 = (f32[3,5,2,1024]{3,2,1,0:T(2,128)S(1)}, f32[3,5,2,1024]{3,2,1,0:T(2,128)S(1)}, u32[]{:S(2)}, u32[]{:S(2)}) collective-permute-start(f32[3,5,2,1024]{3,2,1,0:T(2,128)S(1)} %get-tuple-element.22), channel_id=1, source_target_pairs={{32,0},{64,32},{96,64},{128,96},{160,128},{192,160},{224,192},{0,2... | collective-permute-start | bytes 368648 | tf_op jit(solution)/shard_map/ppermute | solution.py:25
  10.5 4.0 %copy-start.10 = (f32[3,5,2,1024]{3,2,1,0:T(2,128)}, f32[3,5,2,1024]{3,2,1,0:T(2,128)S(1)}, u32[]{:S(2)}) copy-start(f32[3,5,2,1024]{3,2,1,0:T(2,128)S(1)} %collective-permute-done) | copy-start | bytes 368644
  10.5 4.6 %copy-start.12 = (f32[3,5,2,1024]{3,2,1,0:T(2,128)}, f32[3,5,2,1024]{3,2,1,0:T(2,128)S(1)}, u32[]{:S(2)}) copy-start(f32[3,5,2,1024]{3,2,1,0:T(2,128)S(1)} %collective-permute-done.1) | copy-start | bytes 368644
  11.1 2.5 %copy-start.3 = (f32[5,36,1024]{2,1,0:T(8,128)}, f32[5,36,1024]{2,1,0:T(8,128)S(1)}, u32[]{:S(2)}) copy-start(f32[5,36,1024]{2,1,0:T(8,128)S(1)} %get-tuple-element.18) | copy-start | bytes 2211844
  18.4 29.2 %all-to-all-start = ((f32[256,1,1]{2,1,0:T(1,128)}), f32[256,1,1]{2,1,0:T(1,128)S(1)}, u32[]{:S(2)}, u32[]{:S(2)}) async-start(f32[256,1,1]{2,1,0:T(1,128)} %broadcast_in_dim.13), calls=%async_computation | async-start | bytes 262144 | tf_op jit(solution)/shard_map/all_to_all | solution.py:111
  34.8 3.3 %copy-start.5 = (f32[5,33,1024]{2,1,0:T(8,128)S(1)}, f32[5,33,1024]{2,1,0:T(8,128)}, u32[]{:S(2)}) copy-start(f32[5,33,1024]{2,1,0:T(8,128)} %fusion.10) | copy-start | bytes 2027524
  52.6 1.8 %copy-start.8 = (f32[32,1024]{1,0:T(8,128)}, f32[32,1024]{1,0:T(8,128)S(1)}, u32[]{:S(2)}) copy-start(f32[32,1024]{1,0:T(8,128)S(1)} %get-tuple-element.3) | copy-start | bytes 393220
  52.6 1.7 %copy-start.9 = (f32[32,1024]{1,0:T(8,128)}, f32[32,1024]{1,0:T(8,128)S(1)}, u32[]{:S(2)}) copy-start(f32[32,1024]{1,0:T(8,128)S(1)} %get-tuple-element.7) | copy-start | bytes 393220
  53.3 2.4 %collective-permute-start.2 = (f32[48,1024]{1,0:T(8,128)}, f32[48,1024]{1,0:T(8,128)}, u32[]{:S(2)}, u32[]{:S(2)}) collective-permute-start(f32[48,1024]{1,0:T(8,128)} %fusion.57), channel_id=1, source_target_pairs={{0,1},{1,0},{2,3},{3,2},{4,5},{5,4},{6,7},{7,6},{8,9},{9,8},{10,11... | collective-permute-start | bytes 589832 | tf_op jit(solution)/shard_map/ppermute | solution.py:210
  54.3 10.9 %copy-start.4 = (f32[5,36,1024]{2,1,0:T(8,128)S(1)}, f32[5,36,1024]{2,1,0:T(8,128)}, u32[]{:S(2)}) copy-start(f32[5,36,1024]{2,1,0:T(8,128)} %copy-done.3) | copy-start | bytes 2211844
  54.3 16.0 %copy-start.2 = (f32[3,32,1024]{2,1,0:T(8,128)S(1)}, f32[3,32,1024]{2,1,0:T(8,128)}, u32[]{:S(2)}) copy-start(f32[3,32,1024]{2,1,0:T(8,128)} %param.4) | copy-start | bytes 1179652
  54.3 16.0 %copy-start.11 = (f32[3,5,2,1024]{3,2,1,0:T(2,128)S(1)}, f32[3,5,2,1024]{3,2,1,0:T(2,128)}, u32[]{:S(2)}) copy-start(f32[3,5,2,1024]{3,2,1,0:T(2,128)} %copy-done.10) | copy-start | bytes 368644
  54.3 16.0 %copy-start.13 = (f32[3,5,2,1024]{3,2,1,0:T(2,128)S(1)}, f32[3,5,2,1024]{3,2,1,0:T(2,128)}, u32[]{:S(2)}) copy-start(f32[3,5,2,1024]{3,2,1,0:T(2,128)} %copy-done.12) | copy-start | bytes 368644
  56.9 4.1 %collective-permute-start.3 = (f32[24,1024]{1,0:T(8,128)S(1)}, f32[24,1024]{1,0:T(8,128)S(1)}, u32[]{:S(2)}, u32[]{:S(2)}) collective-permute-start(f32[24,1024]{1,0:T(8,128)S(1)} %slice_select_fusion.1), channel_id=1, source_target_pairs={{0,2},{1,3},{2,0},{3,1},{4,6},{5,7},{6,4},{7,5},{8,10},{9,11},{10,... | collective-permute-start | bytes 294920 | tf_op jit(solution)/shard_map/ppermute | solution.py:125
  61.0 3.6 %collective-permute-start.4 = (f32[24,1024]{1,0:T(8,128)S(1)}, f32[24,1024]{1,0:T(8,128)S(1)}, u32[]{:S(2)}, u32[]{:S(2)}) collective-permute-start(f32[24,1024]{1,0:T(8,128)S(1)} %select_add_fusion.3), channel_id=1, source_target_pairs={{0,4},{1,5},{2,6},{3,7},{4,0},{5,1},{6,2},{7,3},{8,12},{9,13},{10,... | collective-permute-start | bytes 294920 | tf_op jit(solution)/shard_map/ppermute | solution.py:154
  64.5 5.5 %collective-permute-start.5 = (f32[24,1024]{1,0:T(8,128)S(1)}, f32[24,1024]{1,0:T(8,128)S(1)}, u32[]{:S(2)}, u32[]{:S(2)}) collective-permute-start(f32[24,1024]{1,0:T(8,128)S(1)} %add.174), channel_id=1, source_target_pairs={{0,8},{1,9},{2,10},{3,11},{4,12},{5,13},{6,14},{7,15},{8,0},{9,1},... | collective-permute-start | bytes 294920 | tf_op jit(solution)/shard_map/ppermute | solution.py:154
  70.1 5.8 %collective-permute-start.6 = (f32[24,1024]{1,0:T(8,128)S(1)}, f32[24,1024]{1,0:T(8,128)S(1)}, u32[]{:S(2)}, u32[]{:S(2)}) collective-permute-start(f32[24,1024]{1,0:T(8,128)S(1)} %add.175), channel_id=1, source_target_pairs={{0,28},{1,29},{2,30},{3,31},{4,24},{5,25},{6,26},{7,27},{8,20},{9,... | collective-permute-start | bytes 294920 | tf_op jit(solution)/shard_map/ppermute | solution.py:154
  75.9 3.8 %collective-permute-start.7 = (f32[24,1024]{1,0:T(8,128)S(1)}, f32[24,1024]{1,0:T(8,128)S(1)}, u32[]{:S(2)}, u32[]{:S(2)}) collective-permute-start(f32[24,1024]{1,0:T(8,128)S(1)} %add.176), channel_id=1, source_target_pairs={{0,2},{1,3},{2,0},{3,1},{4,6},{5,7},{6,4},{7,5},{8,10},{9,11},{10,... | collective-permute-start | bytes 294920 | tf_op jit(solution)/shard_map/ppermute | solution.py:133
  76.3 10.3 %copy-start.6 = (f32[4,32,1024]{2,1,0:T(8,128)S(1)}, f32[4,32,1024]{2,1,0:T(8,128)}, u32[]{:S(2)}) copy-start(f32[4,32,1024]{2,1,0:T(8,128)} %get-tuple-element.30) | copy-start | bytes 1572868
  76.3 10.3 %copy-start.7 = (f32[4,32,1024]{2,1,0:T(8,128)S(1)}, f32[4,32,1024]{2,1,0:T(8,128)}, u32[]{:S(2)}) copy-start(f32[4,32,1024]{2,1,0:T(8,128)} %get-tuple-element.31) | copy-start | bytes 1572868
  79.8 6.7 %collective-permute-start.8 = (f32[48,1024]{1,0:T(8,128)S(1)}, f32[48,1024]{1,0:T(8,128)S(1)}, u32[]{:S(2)}, u32[]{:S(2)}) collective-permute-start(f32[48,1024]{1,0:T(8,128)S(1)} %maximum_select_fusion.2), channel_id=1, source_target_pairs={{0,1},{1,0},{2,3},{3,2},{4,5},{5,4},{6,7},{7,6},{8,9},{9,8},{10,11... | collective-permute-start | bytes 589832 | tf_op jit(solution)/shard_map/ppermute | solution.py:133
  87.3 26.1 %collective-permute-start.10 = (f32[3,5,2,1024]{3,2,1,0:T(2,128)S(1)}, f32[3,5,2,1024]{3,2,1,0:T(2,128)S(1)}, u32[]{:S(2)}, u32[]{:S(2)}) collective-permute-start(f32[3,5,2,1024]{3,2,1,0:T(2,128)S(1)} %get-tuple-element.21), channel_id=1, source_target_pairs={{32,0},{64,32},{96,64},{128,96},{160,128},{192,160},{224,192},{0,2... | collective-permute-start | bytes 368648 | tf_op jit(solution)/shard_map/ppermute | solution.py:25
  88.7 24.7 %collective-permute-start.9 = (f32[3,5,2,1024]{3,2,1,0:T(2,128)S(1)}, f32[3,5,2,1024]{3,2,1,0:T(2,128)S(1)}, u32[]{:S(2)}, u32[]{:S(2)}) collective-permute-start(f32[3,5,2,1024]{3,2,1,0:T(2,128)S(1)} %get-tuple-element.20), channel_id=1, source_target_pairs={{0,32},{32,64},{64,96},{96,128},{128,160},{160,192},{192,224},{224... | collective-permute-start | bytes 368648 | tf_op jit(solution)/shard_map/ppermute | solution.py:22
  113.4 0.6 copy-start.14
  116.7 2.1 %collective-permute-start.11 = (f32[48,1024]{1,0:T(8,128)S(1)}, f32[48,1024]{1,0:T(8,128)S(1)}, u32[]{:S(2)}, u32[]{:S(2)}) collective-permute-start(f32[48,1024]{1,0:T(8,128)S(1)} %fusion.58), channel_id=1, source_target_pairs={{0,1},{1,0},{2,3},{3,2},{4,5},{5,4},{6,7},{7,6},{8,9},{9,8},{10,11... | collective-permute-start | bytes 589832 | tf_op jit(solution)/shard_map/ppermute | solution.py:210
  118.9 4.1 %collective-permute-start.12 = (f32[24,1024]{1,0:T(8,128)S(1)}, f32[24,1024]{1,0:T(8,128)S(1)}, u32[]{:S(2)}, u32[]{:S(2)}) collective-permute-start(f32[24,1024]{1,0:T(8,128)S(1)} %slice_select_fusion), channel_id=1, source_target_pairs={{0,2},{1,3},{2,0},{3,1},{4,6},{5,7},{6,4},{7,5},{8,10},{9,11},{10,... | collective-permute-start | bytes 294920 | tf_op jit(solution)/shard_map/ppermute | solution.py:125
  123.0 24.4 %copy-start.15 = (f32[3,5,2,1024]{3,2,1,0:T(2,128)S(1)}, f32[3,5,2,1024]{3,2,1,0:T(2,128)}, u32[]{:S(2)}) copy-start(f32[3,5,2,1024]{3,2,1,0:T(2,128)} %copy-done.14) | copy-start | bytes 368644
  123.0 3.6 %collective-permute-start.13 = (f32[24,1024]{1,0:T(8,128)S(1)}, f32[24,1024]{1,0:T(8,128)S(1)}, u32[]{:S(2)}, u32[]{:S(2)}) collective-permute-start(f32[24,1024]{1,0:T(8,128)S(1)} %select_add_fusion.2), channel_id=1, source_target_pairs={{0,4},{1,5},{2,6},{3,7},{4,0},{5,1},{6,2},{7,3},{8,12},{9,13},{10,... | collective-permute-start | bytes 294920 | tf_op jit(solution)/shard_map/ppermute | solution.py:154
  126.6 5.5 %collective-permute-start.14 = (f32[24,1024]{1,0:T(8,128)S(1)}, f32[24,1024]{1,0:T(8,128)S(1)}, u32[]{:S(2)}, u32[]{:S(2)}) collective-permute-start(f32[24,1024]{1,0:T(8,128)S(1)} %add.190), channel_id=1, source_target_pairs={{0,8},{1,9},{2,10},{3,11},{4,12},{5,13},{6,14},{7,15},{8,0},{9,1},... | collective-permute-start | bytes 294920 | tf_op jit(solution)/shard_map/ppermute | solution.py:154
  132.1 5.8 %collective-permute-start.15 = (f32[24,1024]{1,0:T(8,128)S(1)}, f32[24,1024]{1,0:T(8,128)S(1)}, u32[]{:S(2)}, u32[]{:S(2)}) collective-permute-start(f32[24,1024]{1,0:T(8,128)S(1)} %add.191), channel_id=1, source_target_pairs={{0,28},{1,29},{2,30},{3,31},{4,24},{5,25},{6,26},{7,27},{8,20},{9,... | collective-permute-start | bytes 294920 | tf_op jit(solution)/shard_map/ppermute | solution.py:154
  138.0 3.8 %collective-permute-start.16 = (f32[24,1024]{1,0:T(8,128)S(1)}, f32[24,1024]{1,0:T(8,128)S(1)}, u32[]{:S(2)}, u32[]{:S(2)}) collective-permute-start(f32[24,1024]{1,0:T(8,128)S(1)} %add.192), channel_id=1, source_target_pairs={{0,2},{1,3},{2,0},{3,1},{4,6},{5,7},{6,4},{7,5},{8,10},{9,11},{10,... | collective-permute-start | bytes 294920 | tf_op jit(solution)/shard_map/ppermute | solution.py:133
  141.8 6.7 %collective-permute-start.17 = (f32[48,1024]{1,0:T(8,128)S(1)}, f32[48,1024]{1,0:T(8,128)S(1)}, u32[]{:S(2)}, u32[]{:S(2)}) collective-permute-start(f32[48,1024]{1,0:T(8,128)S(1)} %maximum_select_fusion.3), channel_id=1, source_target_pairs={{0,1},{1,0},{2,3},{3,2},{4,5},{5,4},{6,7},{7,6},{8,9},{9,8},{10,11... | collective-permute-start | bytes 589832 | tf_op jit(solution)/shard_map/ppermute | solution.py:133

commit v9 on v6

--- a/solution.py
+++ b/solution.py
@@ -148,6 +148,16 @@
     part, done = split_rounds(block, axis, [bit for bit in low_bits if bit not in taken])
     done = list(first_done) + done
     block_size = 2 * low_bits[-1] if low_bits else 1
+    if count // block_size == 8:
+        rounds = (
+            lambda z: z ^ 1,
+            lambda z: (z + 1 if z % 2 == 1 else z - 1) % 8,
+            lambda z: (3 - z) % 8 if z % 4 in (0, 3) else 7 - z,
+        )
+        for partner in rounds:
+            pairs = [(i, partner(i // block_size) * block_size + i % block_size) for i in range(count)]
+            part = part + lax.ppermute(part, axis, pairs)
+        return join_rounds(part, axis, done)
     bit = block_size
     while bit < count:
         pairs = mirror_pairs(count, block_size) if 2 * bit >= count else xor_pairs(count, bit)

time: 141 us -> 139 us (0.986)
  waiting for transfers between devices: 57 us -> 54.8 us
    ppermute x6, waiting for transfers between devices: 25.7 us -> 23.5 us  [species_sum(): part = part + lax.ppermute(part, axis, pairs)]
where the time goes in v9:
time: 139 us
  waiting for transfers between devices  54.8 us (39%)
  starting transfers between devices  39.2 us (28%)
  blocking collectives  21.8 us (16%)
  other arithmetic  16.3 us (12%)
  local copies, waits for them, and re-layouts  4.45 us (3%)
  between operations  2.54 us (2%)
    ppermute x6, waiting for transfers between devices, species_sum(): part = part + lax.ppermute(part, axis, pairs)  23.5 us
    all_to_all x1, blocking collectives, global_max(): return jnp.max(lax.all_to_all(spread, axes, 0, 0, tiled=True))  21.8 us
    all_to_all x1, waiting for transfers between devices, global_max(): return jnp.max(lax.all_to_all(spread, axes, 0, 0, tiled=True))  12.7 us
    all_to_all x1, starting transfers between devices, global_max(): return jnp.max(lax.all_to_all(spread, axes, 0, 0, tiled=True))  12.6 us
    ppermute x4, starting transfers between devices, join_rounds(): other = lax.ppermute(part, axis, xor_pairs(lax.axis_size(axis), bit))  11.8 us
    ppermute x4, waiting for transfers between devices, join_rounds(): other = lax.ppermute(part, axis, xor_pairs(lax.axis_size(axis), bit))  8.64 us
    ppermute x2, waiting for transfers between devices, split_rounds(): part = keep + lax.ppermute(send, axis, xor_pairs(lax.axis_size(axis), bit))  7.46 us
    ppermute x2, starting transfers between devices, padded(): lax.ppermute(lax.slice_in_dim(block, 0, width, axis=dim), axis, backward)  5.34 us
  transfers between devices with their start and end apart: 19, of which 15 were waited for; matrix products, arithmetic and copies ran while one was open for 4% of the time, Pallas kernels for 0%

profile of v9, /device:TPU:1, one launch (start us, length us, event | category | flops | bytes accessed | tf_op | source)
XLA Modules:
  0.0 139.0 jit_solution(3357400871513267282)
XLA Ops:
  0.7 1.4 %fusion.59 = (f32[3,5,2,1024]{3,2,1,0:T(2,128)S(1)}, f32[3,5,2,1024]{3,2,1,0:T(2,128)S(1)}) fusion(f32[3,4,32,1024]{3,2,1,0:T(8,128)} %param.3, f32[3,1,32,1024]{3,2,1,0:T(8,128)} %bitcast.92), kind=kLoop, calls=%fused_computation.150 | loop fusion | flops 61440 | bytes 2211840 | tf_op jit(solution)/shard_map/concatenate | solution.py:230
  2.1 2.2 %collective-permute-start = (f32[3,5,2,1024]{3,2,1,0:T(2,128)S(1)}, f32[3,5,2,1024]{3,2,1,0:T(2,128)S(1)}, u32[]{:S(2)}, u32[]{:S(2)}) collective-permute-start(f32[3,5,2,1024]{3,2,1,0:T(2,128)S(1)} %get-tuple-element.22), channel_id=1, source_target_pairs={{0,32},{32,64},{64,96},{96,128},{128,160},{160,192},{192,224},{224... | collective-permute-start | bytes 368648 | tf_op jit(solution)/shard_map/ppermute | solution.py:22
  4.3 4.0 %collective-permute-start.1 = (f32[3,5,2,1024]{3,2,1,0:T(2,128)S(1)}, f32[3,5,2,1024]{3,2,1,0:T(2,128)S(1)}, u32[]{:S(2)}, u32[]{:S(2)}) collective-permute-start(f32[3,5,2,1024]{3,2,1,0:T(2,128)S(1)} %get-tuple-element.23), channel_id=1, source_target_pairs={{32,0},{64,32},{96,64},{128,96},{160,128},{192,160},{224,192},{0,2... | collective-permute-start | bytes 368648 | tf_op jit(solution)/shard_map/ppermute | solution.py:25
  8.3 0.8 fusion.17
  9.0 1.4 broadcast_in_dim.13
  10.4 12.6 %all-to-all-start = ((f32[256,1,1]{2,1,0:T(1,128)}), f32[256,1,1]{2,1,0:T(1,128)S(1)}, u32[]{:S(2)}, u32[]{:S(2)}) async-start(f32[256,1,1]{2,1,0:T(1,128)} %broadcast_in_dim.13), calls=%async_computation | async-start | bytes 262144 | tf_op jit(solution)/shard_map/all_to_all | solution.py:111
  23.0 12.7 %all-to-all-done = f32[256,1,1]{2,1,0:T(1,128)S(1)} async-done(((f32[256,1,1]{2,1,0:T(1,128)}), f32[256,1,1]{2,1,0:T(1,128)S(1)}, u32[]{:S(2)}, u32[]{:S(2)}) %all-to-all-start) | async-done | bytes 1056 | tf_op jit(solution)/shard_map/all_to_all | solution.py:111
  35.7 0.9 reduce_max.37
  37.3 0.4 pad_maximum_fusion
  37.7 0.3 copy-done.9
  37.9 0.2 slice_bitcast_fusion.5
  38.3 0.6 fusion.10
  38.9 0.2 copy-done.2
  39.2 0.8 multiply_add_fusion.1
  40.0 0.2 fusion.23
  40.3 1.2 multiply_divide_fusion.1
  41.7 0.6 copy-done.6
  42.3 0.7 fusion.57
  43.0 1.0 collective-permute-start.2
  44.0 1.4 %collective-permute-done.2 = f32[48,1024]{1,0:T(8,128)} collective-permute-done((f32[48,1024]{1,0:T(8,128)}, f32[48,1024]{1,0:T(8,128)}, u32[]{:S(2)}, u32[]{:S(2)}) %collective-permute-start.2) | collective-permute-done | bytes 196640 | tf_op jit(solution)/shard_map/ppermute | solution.py:219
  45.4 1.2 select_add_fusion.1
  46.6 0.4 collective-permute-start.3
  47.0 3.7 %collective-permute-done.3 = f32[24,1024]{1,0:T(8,128)S(1)} collective-permute-done((f32[24,1024]{1,0:T(8,128)S(1)}, f32[24,1024]{1,0:T(8,128)S(1)}, u32[]{:S(2)}, u32[]{:S(2)}) %collective-permute-start.3) | collective-permute-done | bytes 98336 | tf_op jit(solution)/shard_map/ppermute | solution.py:125
  50.7 0.9 collective-permute-start.4
  51.7 2.6 %collective-permute-done.4 = f32[24,1024]{1,0:T(8,128)S(1)} collective-permute-done((f32[24,1024]{1,0:T(8,128)S(1)}, f32[24,1024]{1,0:T(8,128)S(1)}, u32[]{:S(2)}, u32[]{:S(2)}) %collective-permute-start.4) | collective-permute-done | bytes 98336 | tf_op jit(solution)/shard_map/ppermute | solution.py:159
  54.3 0.5 collective-permute-start.5
  54.9 4.2 %collective-permute-done.5 = f32[24,1024]{1,0:T(8,128)S(1)} collective-permute-done((f32[24,1024]{1,0:T(8,128)S(1)}, f32[24,1024]{1,0:T(8,128)S(1)}, u32[]{:S(2)}, u32[]{:S(2)}) %collective-permute-start.5) | collective-permute-done | bytes 98336 | tf_op jit(solution)/shard_map/ppermute | solution.py:159
  59.1 0.7 collective-permute-start.6
  59.8 4.9 %collective-permute-done.6 = f32[24,1024]{1,0:T(8,128)S(1)} collective-permute-done((f32[24,1024]{1,0:T(8,128)S(1)}, f32[24,1024]{1,0:T(8,128)S(1)}, u32[]{:S(2)}, u32[]{:S(2)}) %collective-permute-start.6) | collective-permute-done | bytes 98336 | tf_op jit(solution)/shard_map/ppermute | solution.py:159
  64.8 0.4 collective-permute-start.7
  65.2 3.4 %collective-permute-done.7 = f32[24,1024]{1,0:T(8,128)S(1)} collective-permute-done((f32[24,1024]{1,0:T(8,128)S(1)}, f32[24,1024]{1,0:T(8,128)S(1)}, u32[]{:S(2)}, u32[]{:S(2)}) %collective-permute-start.7) | collective-permute-done | bytes 98336 | tf_op jit(solution)/shard_map/ppermute | solution.py:133
  68.6 5.5 %collective-permute-start.8 = (f32[48,1024]{1,0:T(8,128)S(1)}, f32[48,1024]{1,0:T(8,128)S(1)}, u32[]{:S(2)}, u32[]{:S(2)}) collective-permute-start(f32[48,1024]{1,0:T(8,128)S(1)} %maximum_select_fusion.2), channel_id=1, source_target_pairs={{0,1},{1,0},{2,3},{3,2},{4,5},{5,4},{6,7},{7,6},{8,9},{9,8},{10,11... | collective-permute-start | bytes 589832 | tf_op jit(solution)/shard_map/ppermute | solution.py:133
  74.3 0.9 collective-permute-done.8
  75.4 0.3 fusion
  75.7 0.2 pad_maximum_fusion.2
  76.0 1.4 collective-permute-start.10
  77.4 0.4 collective-permute-start.9
  77.8 0.8 fusion.22
  78.5 0.7 broadcast_in_dim.16
  79.2 21.8 %all_to_all.12 = f32[256,1,1]{2,1,0:T(1,128)S(1)} all-to-all(f32[256,1,1]{2,1,0:T(1,128)S(1)} %broadcast_in_dim.16), channel_id=1, replica_groups=mesh['space'=8,'species'=32] {'space','species'}, dimensions={0} | all-to-all | bytes 2048 | tf_op jit(solution)/shard_map/all_to_all | solution.py:111
  101.0 0.9 reduce_max.39
  102.6 0.4 pad_maximum_fusion.1
  103.0 0.3 slice_bitcast_fusion.1
  103.4 0.6 fusion.4
  104.1 0.8 multiply_add_fusion
  104.9 0.2 fusion.20
  105.2 0.3 fusion.34
  105.7 1.1 collective-permute-start.11
  106.8 1.1 collective-permute-done.11
  107.9 0.4 collective-permute-start.12
  108.2 3.7 %collective-permute-done.12 = f32[24,1024]{1,0:T(8,128)S(1)} collective-permute-done((f32[24,1024]{1,0:T(8,128)S(1)}, f32[24,1024]{1,0:T(8,128)S(1)}, u32[]{:S(2)}, u32[]{:S(2)}) %collective-permute-start.12) | collective-permute-done | bytes 98336 | tf_op jit(solution)/shard_map/ppermute | solution.py:125
  112.0 0.9 collective-permute-start.13
  113.0 2.5 %collective-permute-done.13 = f32[24,1024]{1,0:T(8,128)S(1)} collective-permute-done((f32[24,1024]{1,0:T(8,128)S(1)}, f32[24,1024]{1,0:T(8,128)S(1)}, u32[]{:S(2)}, u32[]{:S(2)}) %collective-permute-start.13) | collective-permute-done | bytes 98336 | tf_op jit(solution)/shard_map/ppermute | solution.py:159
  115.6 0.4 collective-permute-start.14
  116.1 4.3 %collective-permute-done.14 = f32[24,1024]{1,0:T(8,128)S(1)} collective-permute-done((f32[24,1024]{1,0:T(8,128)S(1)}, f32[24,1024]{1,0:T(8,128)S(1)}, u32[]{:S(2)}, u32[]{:S(2)}) %collective-permute-start.14) | collective-permute-done | bytes 98336 | tf_op jit(solution)/shard_map/ppermute | solution.py:159
  120.4 0.7 collective-permute-start.15
  121.1 4.9 %collective-permute-done.15 = f32[24,1024]{1,0:T(8,128)S(1)} collective-permute-done((f32[24,1024]{1,0:T(8,128)S(1)}, f32[24,1024]{1,0:T(8,128)S(1)}, u32[]{:S(2)}, u32[]{:S(2)}) %collective-permute-start.15) | collective-permute-done | bytes 98336 | tf_op jit(solution)/shard_map/ppermute | solution.py:159
  126.0 0.4 collective-permute-start.16
  126.6 3.3 %collective-permute-done.16 = f32[24,1024]{1,0:T(8,128)S(1)} collective-permute-done((f32[24,1024]{1,0:T(8,128)S(1)}, f32[24,1024]{1,0:T(8,128)S(1)}, u32[]{:S(2)}, u32[]{:S(2)}) %collective-permute-start.16) | collective-permute-done | bytes 98336 | tf_op jit(solution)/shard_map/ppermute | solution.py:133
  129.9 5.5 %collective-permute-start.17 = (f32[48,1024]{1,0:T(8,128)S(1)}, f32[48,1024]{1,0:T(8,128)S(1)}, u32[]{:S(2)}, u32[]{:S(2)}) collective-permute-start(f32[48,1024]{1,0:T(8,128)S(1)} %maximum_select_fusion.3), channel_id=1, source_target_pairs={{0,1},{1,0},{2,3},{3,2},{4,5},{5,4},{6,7},{7,6},{8,9},{9,8},{10,11... | collective-permute-start | bytes 589832 | tf_op jit(solution)/shard_map/ppermute | solution.py:133
  135.5 1.0 collective-permute-done.17
  136.7 0.8 pad_maximum_fusion.4
  137.4 0.3 fusion.1
  137.7 1.2 pad_maximum_fusion.3
  (73 shorter events, 2.2 us)
Async XLA Ops:
  0.6 7.6 %copy-start.1 = (f32[3,32,1024]{2,1,0:T(8,128)S(1)}, f32[3,32,1024]{2,1,0:T(8,128)}, u32[]{:S(2)}) copy-start(f32[3,32,1024]{2,1,0:T(8,128)} %param.4) | copy-start | bytes 1179652
  0.6 7.6 %copy-start = (f32[3,4,32,1024]{3,2,1,0:T(8,128)S(1)}, f32[3,4,32,1024]{3,2,1,0:T(8,128)}, u32[]{:S(2)}) copy-start(f32[3,4,32,1024]{3,2,1,0:T(8,128)} %param.3) | copy-start | bytes 4718596
  0.6 22.3 %copy-start.13 = (s32[4]{0:T(128)S(1)}, s32[4]{0:T(128)}, u32[]{:S(2)}) copy-start(s32[4]{0:T(128)} %param.5) | copy-start | bytes 52
  2.1 35.2 %collective-permute-start = (f32[3,5,2,1024]{3,2,1,0:T(2,128)S(1)}, f32[3,5,2,1024]{3,2,1,0:T(2,128)S(1)}, u32[]{:S(2)}, u32[]{:S(2)}) collective-permute-start(f32[3,5,2,1024]{3,2,1,0:T(2,128)S(1)} %get-tuple-element.22), channel_id=1, source_target_pairs={{0,32},{32,64},{64,96},{96,128},{128,160},{160,192},{192,224},{224... | collective-permute-start | bytes 368648 | tf_op jit(solution)/shard_map/ppermute | solution.py:22
  4.3 33.0 %collective-permute-start.1 = (f32[3,5,2,1024]{3,2,1,0:T(2,128)S(1)}, f32[3,5,2,1024]{3,2,1,0:T(2,128)S(1)}, u32[]{:S(2)}, u32[]{:S(2)}) collective-permute-start(f32[3,5,2,1024]{3,2,1,0:T(2,128)S(1)} %get-tuple-element.23), channel_id=1, source_target_pairs={{32,0},{64,32},{96,64},{128,96},{160,128},{192,160},{224,192},{0,2... | collective-permute-start | bytes 368648 | tf_op jit(solution)/shard_map/ppermute | solution.py:25
  10.4 25.3 %all-to-all-start = ((f32[256,1,1]{2,1,0:T(1,128)}), f32[256,1,1]{2,1,0:T(1,128)S(1)}, u32[]{:S(2)}, u32[]{:S(2)}) async-start(f32[256,1,1]{2,1,0:T(1,128)} %broadcast_in_dim.13), calls=%async_computation | async-start | bytes 262144 | tf_op jit(solution)/shard_map/all_to_all | solution.py:111
  37.3 0.7 copy-start.9
  37.3 0.7 copy-start.11
  38.2 0.9 copy-start.2
  41.7 0.7 copy-start.6
  41.7 1.3 copy-start.7
  41.7 1.3 copy-start.8
  43.0 2.4 %collective-permute-start.2 = (f32[48,1024]{1,0:T(8,128)}, f32[48,1024]{1,0:T(8,128)}, u32[]{:S(2)}, u32[]{:S(2)}) collective-permute-start(f32[48,1024]{1,0:T(8,128)} %fusion.57), channel_id=1, source_target_pairs={{0,1},{1,0},{2,3},{3,2},{4,5},{5,4},{6,7},{7,6},{8,9},{9,8},{10,11... | collective-permute-start | bytes 589832 | tf_op jit(solution)/shard_map/ppermute | solution.py:219
  44.0 10.7 %copy-start.3 = (f32[5,36,1024]{2,1,0:T(8,128)S(1)}, f32[5,36,1024]{2,1,0:T(8,128)}, u32[]{:S(2)}) copy-start(f32[5,36,1024]{2,1,0:T(8,128)} %copy-done.2) | copy-start | bytes 2211844
  44.0 15.7 %copy-start.10 = (f32[3,5,2,1024]{3,2,1,0:T(2,128)S(1)}, f32[3,5,2,1024]{3,2,1,0:T(2,128)}, u32[]{:S(2)}) copy-start(f32[3,5,2,1024]{3,2,1,0:T(2,128)} %copy-done.9) | copy-start | bytes 368644
  44.0 15.7 %copy-start.12 = (f32[3,5,2,1024]{3,2,1,0:T(2,128)S(1)}, f32[3,5,2,1024]{3,2,1,0:T(2,128)}, u32[]{:S(2)}) copy-start(f32[3,5,2,1024]{3,2,1,0:T(2,128)} %copy-done.11) | copy-start | bytes 368644
  46.6 4.1 %collective-permute-start.3 = (f32[24,1024]{1,0:T(8,128)S(1)}, f32[24,1024]{1,0:T(8,128)S(1)}, u32[]{:S(2)}, u32[]{:S(2)}) collective-permute-start(f32[24,1024]{1,0:T(8,128)S(1)} %slice_select_fusion.1), channel_id=1, source_target_pairs={{0,2},{1,3},{2,0},{3,1},{4,6},{5,7},{6,4},{7,5},{8,10},{9,11},{10,... | collective-permute-start | bytes 294920 | tf_op jit(solution)/shard_map/ppermute | solution.py:125
  50.7 3.6 %collective-permute-start.4 = (f32[24,1024]{1,0:T(8,128)S(1)}, f32[24,1024]{1,0:T(8,128)S(1)}, u32[]{:S(2)}, u32[]{:S(2)}) collective-permute-start(f32[24,1024]{1,0:T(8,128)S(1)} %select_add_fusion.3), channel_id=1, source_target_pairs={{0,4},{1,5},{2,6},{3,7},{4,0},{5,1},{6,2},{7,3},{8,12},{9,13},{10,... | collective-permute-start | bytes 294920 | tf_op jit(solution)/shard_map/ppermute | solution.py:159
  54.3 4.8 %collective-permute-start.5 = (f32[24,1024]{1,0:T(8,128)S(1)}, f32[24,1024]{1,0:T(8,128)S(1)}, u32[]{:S(2)}, u32[]{:S(2)}) collective-permute-start(f32[24,1024]{1,0:T(8,128)S(1)} %add.157), channel_id=1, source_target_pairs={{0,28},{1,29},{2,30},{3,31},{4,8},{5,9},{6,10},{7,11},{8,4},{9,5},... | collective-permute-start | bytes 294920 | tf_op jit(solution)/shard_map/ppermute | solution.py:159
  59.1 5.7 %collective-permute-start.6 = (f32[24,1024]{1,0:T(8,128)S(1)}, f32[24,1024]{1,0:T(8,128)S(1)}, u32[]{:S(2)}, u32[]{:S(2)}) collective-permute-start(f32[24,1024]{1,0:T(8,128)S(1)} %add.158), channel_id=1, source_target_pairs={{0,12},{1,13},{2,14},{3,15},{4,24},{5,25},{6,26},{7,27},{8,20},{9,... | collective-permute-start | bytes 294920 | tf_op jit(solution)/shard_map/ppermute | solution.py:159
  64.8 3.8 %collective-permute-start.7 = (f32[24,1024]{1,0:T(8,128)S(1)}, f32[24,1024]{1,0:T(8,128)S(1)}, u32[]{:S(2)}, u32[]{:S(2)}) collective-permute-start(f32[24,1024]{1,0:T(8,128)S(1)} %add.159), channel_id=1, source_target_pairs={{0,2},{1,3},{2,0},{3,1},{4,6},{5,7},{6,4},{7,5},{8,10},{9,11},{10,... | collective-permute-start | bytes 294920 | tf_op jit(solution)/shard_map/ppermute | solution.py:133
  65.2 10.2 %copy-start.4 = (f32[4,32,1024]{2,1,0:T(8,128)S(1)}, f32[4,32,1024]{2,1,0:T(8,128)}, u32[]{:S(2)}) copy-start(f32[4,32,1024]{2,1,0:T(8,128)} %get-tuple-element.30) | copy-start | bytes 1572868
  65.2 10.2 %copy-start.5 = (f32[4,32,1024]{2,1,0:T(8,128)S(1)}, f32[4,32,1024]{2,1,0:T(8,128)}, u32[]{:S(2)}) copy-start(f32[4,32,1024]{2,1,0:T(8,128)} %get-tuple-element.31) | copy-start | bytes 1572868
  68.6 6.6 %collective-permute-start.8 = (f32[48,1024]{1,0:T(8,128)S(1)}, f32[48,1024]{1,0:T(8,128)S(1)}, u32[]{:S(2)}, u32[]{:S(2)}) collective-permute-start(f32[48,1024]{1,0:T(8,128)S(1)} %maximum_select_fusion.2), channel_id=1, source_target_pairs={{0,1},{1,0},{2,3},{3,2},{4,5},{5,4},{6,7},{7,6},{8,9},{9,8},{10,11... | collective-permute-start | bytes 589832 | tf_op jit(solution)/shard_map/ppermute | solution.py:133
  76.0 26.6 %collective-permute-start.10 = (f32[3,5,2,1024]{3,2,1,0:T(2,128)S(1)}, f32[3,5,2,1024]{3,2,1,0:T(2,128)S(1)}, u32[]{:S(2)}, u32[]{:S(2)}) collective-permute-start(f32[3,5,2,1024]{3,2,1,0:T(2,128)S(1)} %get-tuple-element.21), channel_id=1, source_target_pairs={{32,0},{64,32},{96,64},{128,96},{160,128},{192,160},{224,192},{0,2... | collective-permute-start | bytes 368648 | tf_op jit(solution)/shard_map/ppermute | solution.py:25
  77.4 25.2 %collective-permute-start.9 = (f32[3,5,2,1024]{3,2,1,0:T(2,128)S(1)}, f32[3,5,2,1024]{3,2,1,0:T(2,128)S(1)}, u32[]{:S(2)}, u32[]{:S(2)}) collective-permute-start(f32[3,5,2,1024]{3,2,1,0:T(2,128)S(1)} %get-tuple-element.20), channel_id=1, source_target_pairs={{0,32},{32,64},{64,96},{96,128},{128,160},{160,192},{192,224},{224... | collective-permute-start | bytes 368648 | tf_op jit(solution)/shard_map/ppermute | solution.py:22
  105.7 2.1 %collective-permute-start.11 = (f32[48,1024]{1,0:T(8,128)S(1)}, f32[48,1024]{1,0:T(8,128)S(1)}, u32[]{:S(2)}, u32[]{:S(2)}) collective-permute-start(f32[48,1024]{1,0:T(8,128)S(1)} %fusion.58), channel_id=1, source_target_pairs={{0,1},{1,0},{2,3},{3,2},{4,5},{5,4},{6,7},{7,6},{8,9},{9,8},{10,11... | collective-permute-start | bytes 589832 | tf_op jit(solution)/shard_map/ppermute | solution.py:219
  107.9 4.1 %collective-permute-start.12 = (f32[24,1024]{1,0:T(8,128)S(1)}, f32[24,1024]{1,0:T(8,128)S(1)}, u32[]{:S(2)}, u32[]{:S(2)}) collective-permute-start(f32[24,1024]{1,0:T(8,128)S(1)} %slice_select_fusion), channel_id=1, source_target_pairs={{0,2},{1,3},{2,0},{3,1},{4,6},{5,7},{6,4},{7,5},{8,10},{9,11},{10,... | collective-permute-start | bytes 294920 | tf_op jit(solution)/shard_map/ppermute | solution.py:125
  112.0 3.6 %collective-permute-start.13 = (f32[24,1024]{1,0:T(8,128)S(1)}, f32[24,1024]{1,0:T(8,128)S(1)}, u32[]{:S(2)}, u32[]{:S(2)}) collective-permute-start(f32[24,1024]{1,0:T(8,128)S(1)} %select_add_fusion.2), channel_id=1, source_target_pairs={{0,4},{1,5},{2,6},{3,7},{4,0},{5,1},{6,2},{7,3},{8,12},{9,13},{10,... | collective-permute-start | bytes 294920 | tf_op jit(solution)/shard_map/ppermute | solution.py:159
  115.6 4.8 %collective-permute-start.14 = (f32[24,1024]{1,0:T(8,128)S(1)}, f32[24,1024]{1,0:T(8,128)S(1)}, u32[]{:S(2)}, u32[]{:S(2)}) collective-permute-start(f32[24,1024]{1,0:T(8,128)S(1)} %add.173), channel_id=1, source_target_pairs={{0,28},{1,29},{2,30},{3,31},{4,8},{5,9},{6,10},{7,11},{8,4},{9,5},... | collective-permute-start | bytes 294920 | tf_op jit(solution)/shard_map/ppermute | solution.py:159
  120.4 5.7 %collective-permute-start.15 = (f32[24,1024]{1,0:T(8,128)S(1)}, f32[24,1024]{1,0:T(8,128)S(1)}, u32[]{:S(2)}, u32[]{:S(2)}) collective-permute-start(f32[24,1024]{1,0:T(8,128)S(1)} %add.174), channel_id=1, source_target_pairs={{0,12},{1,13},{2,14},{3,15},{4,24},{5,25},{6,26},{7,27},{8,20},{9,... | collective-permute-start | bytes 294920 | tf_op jit(solution)/shard_map/ppermute | solution.py:159
  126.0 3.8 %collective-permute-start.16 = (f32[24,1024]{1,0:T(8,128)S(1)}, f32[24,1024]{1,0:T(8,128)S(1)}, u32[]{:S(2)}, u32[]{:S(2)}) collective-permute-start(f32[24,1024]{1,0:T(8,128)S(1)} %add.175), channel_id=1, source_target_pairs={{0,2},{1,3},{2,0},{3,1},{4,6},{5,7},{6,4},{7,5},{8,10},{9,11},{10,... | collective-permute-start | bytes 294920 | tf_op jit(solution)/shard_map/ppermute | solution.py:133
  129.9 6.6 %collective-permute-start.17 = (f32[48,1024]{1,0:T(8,128)S(1)}, f32[48,1024]{1,0:T(8,128)S(1)}, u32[]{:S(2)}, u32[]{:S(2)}) collective-permute-start(f32[48,1024]{1,0:T(8,128)S(1)} %maximum_select_fusion.3), channel_id=1, source_target_pairs={{0,1},{1,0},{2,3},{3,2},{4,5},{5,4},{6,7},{7,6},{8,9},{9,8},{10,11... | collective-permute-start | bytes 589832 | tf_op jit(solution)/shard_map/ppermute | solution.py:133

commit v10 on v9

--- a/solution.py
+++ b/solution.py
@@ -140,7 +140,7 @@
     return part
 
 
-def species_sum(block, axis, first_done=()):
+def species_sum(block, axis, first_done=(), finish=None):
     count = lax.axis_size(axis)
     index = lax.axis_index(axis)
     low_bits = [bit for bit in (1, 2) if bit < count]
@@ -157,6 +157,8 @@
         for partner in rounds:
             pairs = [(i, partner(i // block_size) * block_size + i % block_size) for i in range(count)]
             part = part + lax.ppermute(part, axis, pairs)
+        if finish is not None:
+            part = finish(part)
         return join_rounds(part, axis, done)
     bit = block_size
     while bit < count:
@@ -165,6 +167,8 @@
         upper = (index // bit) % 2 == 1 if 2 * bit < count else index >= count // 2
         part = jnp.where(upper, other + part, part + other)
         bit *= 2
+    if finish is not None:
+        part = finish(part)
     return join_rounds(part, axis, done)
 
 
@@ -174,9 +178,9 @@
     fresh = dust[0] - step_time * divergence[:local_species]
     rate = step_time * gas_new[None] / stop_times[:, None, None]
     weight = fresh / (total_species * gas_new[None]) * rate / (1.0 + rate)
-    totals = jnp.concatenate(
-        [jnp.sum(weight, 0), jnp.sum(weight * dust[1], 0), jnp.sum(weight * dust[2], 0)], axis=0
-    )
+    sums = jnp.stack([jnp.sum(weight, 0), jnp.sum(weight * dust[1], 0), jnp.sum(weight * dust[2], 0)])
+    rows, lanes = sums.shape[1:]
+    totals = sums.reshape(3, 4, rows // 4, lanes).transpose(1, 0, 2, 3).reshape(-1, lanes)
     half = totals.shape[0] // 2
     low, high = totals[:half], totals[half:]
     keep = jnp.where(upper, high, low)
@@ -217,9 +221,17 @@
     )
     dust_velocity = jnp.stack([inner_radial[:-1], azimuth[:-1, 2:-2]])
     part = keep + lax.ppermute(send, "species", xor_pairs(lax.axis_size("species"), 1))
-    totals = species_sum(part, "species", first_done=[(1, 0)])
-    totals = totals.reshape(3, tile_rows, -1)
-    gas_next = coupled_gas(gas_velocity, totals)
+    species = lax.axis_index("species")
+    quarter = 2 * (species % 2) + (species // 2) % 2
+    rows = tile_rows // 4
+
+    def finish(block):
+        own = block.reshape(3, rows, -1)
+        star = lax.dynamic_slice_in_dim(gas_velocity, quarter * rows, rows, axis=1)
+        return coupled_gas(star, own).reshape(2 * rows, -1)
+
+    joined = species_sum(part, "species", first_done=[(1, 0)], finish=finish)
+    gas_next = joined.reshape(4, 2, rows, -1).transpose(1, 0, 2, 3).reshape(2, tile_rows, -1)
     return assemble(new_density, dust_velocity, gas_next, rate)
 
 

time: 139 us -> 140 us (level)
  other arithmetic: 16.3 us -> 18.5 us
  transfers between devices with their start and end apart: 19 -> 19, of which waited for: 15 -> 15; matrix products, arithmetic and copies ran while one was open for 4% -> 5% of each run, Pallas kernels for 0% -> 0%
where the time goes in v10:
time: 140 us
  waiting for transfers between devices  53.4 us (38%)
  starting transfers between devices  39.1 us (28%)
  blocking collectives  21.8 us (16%)
  other arithmetic  18.5 us (13%)
  local copies, waits for them, and re-layouts  4.46 us (3%)
  between operations  2.54 us (2%)
    ppermute x6, waiting for transfers between devices, species_sum(): part = part + lax.ppermute(part, axis, pairs)  22.6 us
    all_to_all x1, blocking collectives, global_max(): return jnp.max(lax.all_to_all(spread, axes, 0, 0, tiled=True))  21.8 us
    all_to_all x1, waiting for transfers between devices, global_max(): return jnp.max(lax.all_to_all(spread, axes, 0, 0, tiled=True))  12.7 us
    all_to_all x1, starting transfers between devices, global_max(): return jnp.max(lax.all_to_all(spread, axes, 0, 0, tiled=True))  12.6 us
    ppermute x4, starting transfers between devices, join_rounds(): other = lax.ppermute(part, axis, xor_pairs(lax.axis_size(axis), bit))  11.8 us
    ppermute x4, waiting for transfers between devices, join_rounds(): other = lax.ppermute(part, axis, xor_pairs(lax.axis_size(axis), bit))  7.99 us
    ppermute x2, waiting for transfers between devices, split_rounds(): part = keep + lax.ppermute(send, axis, xor_pairs(lax.axis_size(axis), bit))  7.67 us
    ppermute x2, starting transfers between devices, padded(): lax.ppermute(lax.slice_in_dim(block, 0, width, axis=dim), axis, backward)  5.34 us
  transfers between devices with their start and end apart: 19, of which 15 were waited for; matrix products, arithmetic and copies ran while one was open for 5% of the time, Pallas kernels for 0%

profile of v10, /device:TPU:1, one launch (start us, length us, event | category | flops | bytes accessed | tf_op | source)
XLA Modules:
  0.0 139.7 jit_solution(16084857931151987882)
XLA Ops:
  0.7 1.4 fusion.55
  2.1 2.2 %collective-permute-start = (f32[3,5,2,1024]{3,2,1,0:T(2,128)S(1)}, f32[3,5,2,1024]{3,2,1,0:T(2,128)S(1)}, u32[]{:S(2)}, u32[]{:S(2)}) collective-permute-start(f32[3,5,2,1024]{3,2,1,0:T(2,128)S(1)} %get-tuple-element.22), channel_id=1, source_target_pairs={{0,32},{32,64},{64,96},{96,128},{128,160},{160,192},{192,224},{224... | collective-permute-start | bytes 368648 | tf_op jit(solution)/shard_map/ppermute | solution.py:22
  4.3 4.0 %collective-permute-start.1 = (f32[3,5,2,1024]{3,2,1,0:T(2,128)S(1)}, f32[3,5,2,1024]{3,2,1,0:T(2,128)S(1)}, u32[]{:S(2)}, u32[]{:S(2)}) collective-permute-start(f32[3,5,2,1024]{3,2,1,0:T(2,128)S(1)} %get-tuple-element.23), channel_id=1, source_target_pairs={{32,0},{64,32},{96,64},{128,96},{160,128},{192,160},{224,192},{0,2... | collective-permute-start | bytes 368648 | tf_op jit(solution)/shard_map/ppermute | solution.py:25
  8.3 0.8 fusion.17
  9.0 1.4 broadcast_in_dim.13
  10.4 12.6 %all-to-all-start = ((f32[256,1,1]{2,1,0:T(1,128)}), f32[256,1,1]{2,1,0:T(1,128)S(1)}, u32[]{:S(2)}, u32[]{:S(2)}) async-start(f32[256,1,1]{2,1,0:T(1,128)} %broadcast_in_dim.13), calls=%async_computation | async-start | bytes 262144 | tf_op jit(solution)/shard_map/all_to_all | solution.py:111
  23.0 12.7 %all-to-all-done = f32[256,1,1]{2,1,0:T(1,128)S(1)} async-done(((f32[256,1,1]{2,1,0:T(1,128)}), f32[256,1,1]{2,1,0:T(1,128)S(1)}, u32[]{:S(2)}, u32[]{:S(2)}) %all-to-all-start) | async-done | bytes 1056 | tf_op jit(solution)/shard_map/all_to_all | solution.py:111
  35.7 0.9 reduce_max.37
  37.3 0.4 pad_maximum_fusion
  37.7 0.2 copy-done.7
  37.9 0.2 slice_bitcast_fusion.5
  38.3 0.6 fusion.10
  39.2 0.8 multiply_add_fusion.1
  40.0 0.2 fusion.23
  40.3 1.2 multiply_divide_fusion.1
  41.7 0.8 slice_select_fusion.3
  42.5 1.0 collective-permute-start.2
  43.5 1.4 %collective-permute-done.2 = f32[48,1024]{1,0:T(8,128)} collective-permute-done((f32[48,1024]{1,0:T(8,128)}, f32[48,1024]{1,0:T(8,128)}, u32[]{:S(2)}, u32[]{:S(2)}) %collective-permute-start.2) | collective-permute-done | bytes 196640 | tf_op jit(solution)/shard_map/ppermute | solution.py:223
  44.9 1.0 bitcast_add_fusion.1
  46.0 0.7 copy-done.6
  46.6 0.7 slice_select_fusion.5
  47.3 0.3 collective-permute-start.3
  47.6 3.9 %collective-permute-done.3 = f32[24,1024]{1,0:T(8,128)S(1)} collective-permute-done((f32[24,1024]{1,0:T(8,128)}, f32[24,1024]{1,0:T(8,128)S(1)}, u32[]{:S(2)}, u32[]{:S(2)}) %collective-permute-start.3) | collective-permute-done | bytes 98336 | tf_op jit(solution)/shard_map/ppermute | solution.py:125
  51.5 1.0 select_add_fusion.1
  52.5 0.9 collective-permute-start.4
  53.4 0.8 slice_bitcast_fusion.14
  54.2 1.8 %collective-permute-done.4 = f32[24,1024]{1,0:T(8,128)S(1)} collective-permute-done((f32[24,1024]{1,0:T(8,128)S(1)}, f32[24,1024]{1,0:T(8,128)S(1)}, u32[]{:S(2)}, u32[]{:S(2)}) %collective-permute-start.4) | collective-permute-done | bytes 98336 | tf_op jit(solution)/shard_map/ppermute | solution.py:159
  56.0 0.5 collective-permute-start.5
  56.6 4.2 %collective-permute-done.5 = f32[24,1024]{1,0:T(8,128)S(1)} collective-permute-done((f32[24,1024]{1,0:T(8,128)S(1)}, f32[24,1024]{1,0:T(8,128)S(1)}, u32[]{:S(2)}, u32[]{:S(2)}) %collective-permute-start.5) | collective-permute-done | bytes 98336 | tf_op jit(solution)/shard_map/ppermute | solution.py:159
  60.8 0.7 collective-permute-start.6
  61.6 4.9 %collective-permute-done.6 = f32[24,1024]{1,0:T(8,128)S(1)} collective-permute-done((f32[24,1024]{1,0:T(8,128)S(1)}, f32[24,1024]{1,0:T(8,128)S(1)}, u32[]{:S(2)}, u32[]{:S(2)}) %collective-permute-start.6) | collective-permute-done | bytes 98336 | tf_op jit(solution)/shard_map/ppermute | solution.py:159
  66.5 0.4 collective-permute-start.7
  66.9 3.1 %collective-permute-done.7 = f32[16,1024]{1,0:T(8,128)S(1)} collective-permute-done((f32[16,1024]{1,0:T(8,128)S(1)}, f32[16,1024]{1,0:T(8,128)S(1)}, u32[]{:S(2)}, u32[]{:S(2)}) %collective-permute-start.7) | collective-permute-done | bytes 65568 | tf_op jit(solution)/shard_map/ppermute | solution.py:133
  70.1 5.5 %collective-permute-start.8 = (f32[32,1024]{1,0:T(8,128)S(1)}, f32[32,1024]{1,0:T(8,128)S(1)}, u32[]{:S(2)}, u32[]{:S(2)}) collective-permute-start(f32[32,1024]{1,0:T(8,128)S(1)} %maximum_select_fusion.2), channel_id=1, source_target_pairs={{0,1},{1,0},{2,3},{3,2},{4,5},{5,4},{6,7},{7,6},{8,9},{9,8},{10,11... | collective-permute-start | bytes 393224 | tf_op jit(solution)/shard_map/ppermute | solution.py:133
  75.7 0.9 collective-permute-done.8
  76.7 0.3 fusion
  77.3 1.4 collective-permute-start.10
  78.6 0.4 collective-permute-start.9
  79.0 0.8 fusion.22
  79.8 0.7 broadcast_in_dim.16
  80.5 21.8 %all_to_all.12 = f32[256,1,1]{2,1,0:T(1,128)S(1)} all-to-all(f32[256,1,1]{2,1,0:T(1,128)S(1)} %broadcast_in_dim.16), channel_id=1, replica_groups=mesh['space'=8,'species'=32] {'space','species'}, dimensions={0} | all-to-all | bytes 2048 | tf_op jit(solution)/shard_map/all_to_all | solution.py:111
  102.2 0.9 reduce_max.39
  103.8 0.4 pad_maximum_fusion.1
  104.2 0.3 slice_bitcast_fusion.1
  104.6 0.6 fusion.4
  105.3 0.8 multiply_add_fusion
  106.4 0.3 fusion.32
  107.0 1.1 collective-permute-start.11
  108.0 1.1 collective-permute-done.11
  109.1 0.4 collective-permute-start.12
  109.5 3.7 %collective-permute-done.12 = f32[24,1024]{1,0:T(8,128)S(1)} collective-permute-done((f32[24,1024]{1,0:T(8,128)S(1)}, f32[24,1024]{1,0:T(8,128)S(1)}, u32[]{:S(2)}, u32[]{:S(2)}) %collective-permute-start.12) | collective-permute-done | bytes 98336 | tf_op jit(solution)/shard_map/ppermute | solution.py:125
  113.3 0.9 collective-permute-start.13
  114.3 2.5 %collective-permute-done.13 = f32[24,1024]{1,0:T(8,128)S(1)} collective-permute-done((f32[24,1024]{1,0:T(8,128)S(1)}, f32[24,1024]{1,0:T(8,128)S(1)}, u32[]{:S(2)}, u32[]{:S(2)}) %collective-permute-start.13) | collective-permute-done | bytes 98336 | tf_op jit(solution)/shard_map/ppermute | solution.py:159
  116.8 0.4 collective-permute-start.14
  117.4 4.2 %collective-permute-done.14 = f32[24,1024]{1,0:T(8,128)S(1)} collective-permute-done((f32[24,1024]{1,0:T(8,128)S(1)}, f32[24,1024]{1,0:T(8,128)S(1)}, u32[]{:S(2)}, u32[]{:S(2)}) %collective-permute-start.14) | collective-permute-done | bytes 98336 | tf_op jit(solution)/shard_map/ppermute | solution.py:159
  121.6 0.7 collective-permute-start.15
  122.3 4.9 %collective-permute-done.15 = f32[24,1024]{1,0:T(8,128)S(1)} collective-permute-done((f32[24,1024]{1,0:T(8,128)S(1)}, f32[24,1024]{1,0:T(8,128)S(1)}, u32[]{:S(2)}, u32[]{:S(2)}) %collective-permute-start.15) | collective-permute-done | bytes 98336 | tf_op jit(solution)/shard_map/ppermute | solution.py:159
  127.3 0.4 collective-permute-start.16
  127.8 3.1 %collective-permute-done.16 = f32[16,1024]{1,0:T(8,128)S(1)} collective-permute-done((f32[16,1024]{1,0:T(8,128)S(1)}, f32[16,1024]{1,0:T(8,128)S(1)}, u32[]{:S(2)}, u32[]{:S(2)}) %collective-permute-start.16) | collective-permute-done | bytes 65568 | tf_op jit(solution)/shard_map/ppermute | solution.py:133
  130.8 5.5 %collective-permute-start.17 = (f32[32,1024]{1,0:T(8,128)S(1)}, f32[32,1024]{1,0:T(8,128)S(1)}, u32[]{:S(2)}, u32[]{:S(2)}) collective-permute-start(f32[32,1024]{1,0:T(8,128)S(1)} %maximum_select_fusion.3), channel_id=1, source_target_pairs={{0,1},{1,0},{2,3},{3,2},{4,5},{5,4},{6,7},{7,6},{8,9},{9,8},{10,11... | collective-permute-start | bytes 393224 | tf_op jit(solution)/shard_map/ppermute | solution.py:133
  136.5 0.9 collective-permute-done.17
  137.4 0.8 pad_maximum_fusion.4
  138.2 0.3 fusion.1
  138.5 1.2 pad_maximum_fusion.3
  (67 shorter events, 2.6 us)
Async XLA Ops:
  0.6 7.6 %copy-start.1 = (f32[3,32,1024]{2,1,0:T(8,128)S(1)}, f32[3,32,1024]{2,1,0:T(8,128)}, u32[]{:S(2)}) copy-start(f32[3,32,1024]{2,1,0:T(8,128)} %param.4) | copy-start | bytes 1179652
  0.6 7.6 %copy-start = (f32[3,4,32,1024]{3,2,1,0:T(8,128)S(1)}, f32[3,4,32,1024]{3,2,1,0:T(8,128)}, u32[]{:S(2)}) copy-start(f32[3,4,32,1024]{3,2,1,0:T(8,128)} %param.3) | copy-start | bytes 4718596
  0.6 22.3 %copy-start.9 = (s32[4]{0:T(128)S(1)}, s32[4]{0:T(128)}, u32[]{:S(2)}) copy-start(s32[4]{0:T(128)} %param.5) | copy-start | bytes 52
  2.1 35.2 %collective-permute-start = (f32[3,5,2,1024]{3,2,1,0:T(2,128)S(1)}, f32[3,5,2,1024]{3,2,1,0:T(2,128)S(1)}, u32[]{:S(2)}, u32[]{:S(2)}) collective-permute-start(f32[3,5,2,1024]{3,2,1,0:T(2,128)S(1)} %get-tuple-element.22), channel_id=1, source_target_pairs={{0,32},{32,64},{64,96},{96,128},{128,160},{160,192},{192,224},{224... | collective-permute-start | bytes 368648 | tf_op jit(solution)/shard_map/ppermute | solution.py:22
  4.3 33.0 %collective-permute-start.1 = (f32[3,5,2,1024]{3,2,1,0:T(2,128)S(1)}, f32[3,5,2,1024]{3,2,1,0:T(2,128)S(1)}, u32[]{:S(2)}, u32[]{:S(2)}) collective-permute-start(f32[3,5,2,1024]{3,2,1,0:T(2,128)S(1)} %get-tuple-element.23), channel_id=1, source_target_pairs={{32,0},{64,32},{96,64},{128,96},{160,128},{192,160},{224,192},{0,2... | collective-permute-start | bytes 368648 | tf_op jit(solution)/shard_map/ppermute | solution.py:25
  10.4 25.3 %all-to-all-start = ((f32[256,1,1]{2,1,0:T(1,128)}), f32[256,1,1]{2,1,0:T(1,128)S(1)}, u32[]{:S(2)}, u32[]{:S(2)}) async-start(f32[256,1,1]{2,1,0:T(1,128)} %broadcast_in_dim.13), calls=%async_computation | async-start | bytes 262144 | tf_op jit(solution)/shard_map/all_to_all | solution.py:111
  37.3 0.7 copy-start.7
  37.3 0.7 copy-start.8
  38.2 0.9 copy-start.2
  42.5 2.4 %collective-permute-start.2 = (f32[48,1024]{1,0:T(8,128)}, f32[48,1024]{1,0:T(8,128)}, u32[]{:S(2)}, u32[]{:S(2)}) collective-permute-start(f32[48,1024]{1,0:T(8,128)} %bitcast.21), channel_id=1, source_target_pairs={{0,1},{1,0},{2,3},{3,2},{4,5},{5,4},{6,7},{7,6},{8,9},{9,8},{10,11... | collective-permute-start | bytes 589832 | tf_op jit(solution)/shard_map/ppermute | solution.py:223
  45.9 0.7 copy-start.6
  47.3 4.2 %collective-permute-start.3 = (f32[24,1024]{1,0:T(8,128)}, f32[24,1024]{1,0:T(8,128)S(1)}, u32[]{:S(2)}, u32[]{:S(2)}) collective-permute-start(f32[24,1024]{1,0:T(8,128)} %slice_select_fusion.5), channel_id=1, source_target_pairs={{0,2},{1,3},{2,0},{3,1},{4,6},{5,7},{6,4},{7,5},{8,10},{9,11},{10,... | collective-permute-start | bytes 294920 | tf_op jit(solution)/shard_map/ppermute | solution.py:125
  47.6 13.9 %copy-start.3 = (f32[5,36,1024]{2,1,0:T(8,128)S(1)}, f32[5,36,1024]{2,1,0:T(8,128)}, u32[]{:S(2)}) copy-start(f32[5,36,1024]{2,1,0:T(8,128)} %copy-done.2) | copy-start | bytes 2211844
  52.5 3.6 %collective-permute-start.4 = (f32[24,1024]{1,0:T(8,128)S(1)}, f32[24,1024]{1,0:T(8,128)S(1)}, u32[]{:S(2)}, u32[]{:S(2)}) collective-permute-start(f32[24,1024]{1,0:T(8,128)S(1)} %select_add_fusion.1), channel_id=1, source_target_pairs={{0,4},{1,5},{2,6},{3,7},{4,0},{5,1},{6,2},{7,3},{8,12},{9,13},{10,... | collective-permute-start | bytes 294920 | tf_op jit(solution)/shard_map/ppermute | solution.py:159
  56.0 4.8 %collective-permute-start.5 = (f32[24,1024]{1,0:T(8,128)S(1)}, f32[24,1024]{1,0:T(8,128)S(1)}, u32[]{:S(2)}, u32[]{:S(2)}) collective-permute-start(f32[24,1024]{1,0:T(8,128)S(1)} %add.163), channel_id=1, source_target_pairs={{0,28},{1,29},{2,30},{3,31},{4,8},{5,9},{6,10},{7,11},{8,4},{9,5},... | collective-permute-start | bytes 294920 | tf_op jit(solution)/shard_map/ppermute | solution.py:159
  60.8 5.7 %collective-permute-start.6 = (f32[24,1024]{1,0:T(8,128)S(1)}, f32[24,1024]{1,0:T(8,128)S(1)}, u32[]{:S(2)}, u32[]{:S(2)}) collective-permute-start(f32[24,1024]{1,0:T(8,128)S(1)} %add.164), channel_id=1, source_target_pairs={{0,12},{1,13},{2,14},{3,15},{4,24},{5,25},{6,26},{7,27},{8,20},{9,... | collective-permute-start | bytes 294920 | tf_op jit(solution)/shard_map/ppermute | solution.py:159
  66.5 3.5 %collective-permute-start.7 = (f32[16,1024]{1,0:T(8,128)S(1)}, f32[16,1024]{1,0:T(8,128)S(1)}, u32[]{:S(2)}, u32[]{:S(2)}) collective-permute-start(f32[16,1024]{1,0:T(8,128)S(1)} %fusion.62), channel_id=1, source_target_pairs={{0,2},{1,3},{2,0},{3,1},{4,6},{5,7},{6,4},{7,5},{8,10},{9,11},{10,... | collective-permute-start | bytes 196616 | tf_op jit(solution)/shard_map/ppermute | solution.py:133
  70.0 6.6 %copy-start.4 = (f32[4,32,1024]{2,1,0:T(8,128)S(1)}, f32[4,32,1024]{2,1,0:T(8,128)}, u32[]{:S(2)}) copy-start(f32[4,32,1024]{2,1,0:T(8,128)} %get-tuple-element.34) | copy-start | bytes 1572868
  70.1 6.6 %copy-start.5 = (f32[4,32,1024]{2,1,0:T(8,128)S(1)}, f32[4,32,1024]{2,1,0:T(8,128)}, u32[]{:S(2)}) copy-start(f32[4,32,1024]{2,1,0:T(8,128)} %get-tuple-element.35) | copy-start | bytes 1572868
  70.1 6.5 %collective-permute-start.8 = (f32[32,1024]{1,0:T(8,128)S(1)}, f32[32,1024]{1,0:T(8,128)S(1)}, u32[]{:S(2)}, u32[]{:S(2)}) collective-permute-start(f32[32,1024]{1,0:T(8,128)S(1)} %maximum_select_fusion.2), channel_id=1, source_target_pairs={{0,1},{1,0},{2,3},{3,2},{4,5},{5,4},{6,7},{7,6},{8,9},{9,8},{10,11... | collective-permute-start | bytes 393224 | tf_op jit(solution)/shard_map/ppermute | solution.py:133
  77.3 26.5 %collective-permute-start.10 = (f32[3,5,2,1024]{3,2,1,0:T(2,128)S(1)}, f32[3,5,2,1024]{3,2,1,0:T(2,128)S(1)}, u32[]{:S(2)}, u32[]{:S(2)}) collective-permute-start(f32[3,5,2,1024]{3,2,1,0:T(2,128)S(1)} %get-tuple-element.21), channel_id=1, source_target_pairs={{32,0},{64,32},{96,64},{128,96},{160,128},{192,160},{224,192},{0,2... | collective-permute-start | bytes 368648 | tf_op jit(solution)/shard_map/ppermute | solution.py:25
  78.6 25.2 %collective-permute-start.9 = (f32[3,5,2,1024]{3,2,1,0:T(2,128)S(1)}, f32[3,5,2,1024]{3,2,1,0:T(2,128)S(1)}, u32[]{:S(2)}, u32[]{:S(2)}) collective-permute-start(f32[3,5,2,1024]{3,2,1,0:T(2,128)S(1)} %get-tuple-element.20), channel_id=1, source_target_pairs={{0,32},{32,64},{64,96},{96,128},{128,160},{160,192},{192,224},{224... | collective-permute-start | bytes 368648 | tf_op jit(solution)/shard_map/ppermute | solution.py:22
  107.0 2.1 %collective-permute-start.11 = (f32[48,1024]{1,0:T(8,128)S(1)}, f32[48,1024]{1,0:T(8,128)S(1)}, u32[]{:S(2)}, u32[]{:S(2)}) collective-permute-start(f32[48,1024]{1,0:T(8,128)S(1)} %bitcast.150), channel_id=1, source_target_pairs={{0,1},{1,0},{2,3},{3,2},{4,5},{5,4},{6,7},{7,6},{8,9},{9,8},{10,11... | collective-permute-start | bytes 589832 | tf_op jit(solution)/shard_map/ppermute | solution.py:223
  109.1 4.1 %collective-permute-start.12 = (f32[24,1024]{1,0:T(8,128)S(1)}, f32[24,1024]{1,0:T(8,128)S(1)}, u32[]{:S(2)}, u32[]{:S(2)}) collective-permute-start(f32[24,1024]{1,0:T(8,128)S(1)} %slice_select_fusion.4), channel_id=1, source_target_pairs={{0,2},{1,3},{2,0},{3,1},{4,6},{5,7},{6,4},{7,5},{8,10},{9,11},{10,... | collective-permute-start | bytes 294920 | tf_op jit(solution)/shard_map/ppermute | solution.py:125
  113.3 3.6 %collective-permute-start.13 = (f32[24,1024]{1,0:T(8,128)S(1)}, f32[24,1024]{1,0:T(8,128)S(1)}, u32[]{:S(2)}, u32[]{:S(2)}) collective-permute-start(f32[24,1024]{1,0:T(8,128)S(1)} %select_add_fusion), channel_id=1, source_target_pairs={{0,4},{1,5},{2,6},{3,7},{4,0},{5,1},{6,2},{7,3},{8,12},{9,13},{10,... | collective-permute-start | bytes 294920 | tf_op jit(solution)/shard_map/ppermute | solution.py:159
  116.8 4.8 %collective-permute-start.14 = (f32[24,1024]{1,0:T(8,128)S(1)}, f32[24,1024]{1,0:T(8,128)S(1)}, u32[]{:S(2)}, u32[]{:S(2)}) collective-permute-start(f32[24,1024]{1,0:T(8,128)S(1)} %add.179), channel_id=1, source_target_pairs={{0,28},{1,29},{2,30},{3,31},{4,8},{5,9},{6,10},{7,11},{8,4},{9,5},... | collective-permute-start | bytes 294920 | tf_op jit(solution)/shard_map/ppermute | solution.py:159
  121.6 5.7 %collective-permute-start.15 = (f32[24,1024]{1,0:T(8,128)S(1)}, f32[24,1024]{1,0:T(8,128)S(1)}, u32[]{:S(2)}, u32[]{:S(2)}) collective-permute-start(f32[24,1024]{1,0:T(8,128)S(1)} %add.180), channel_id=1, source_target_pairs={{0,12},{1,13},{2,14},{3,15},{4,24},{5,25},{6,26},{7,27},{8,20},{9,... | collective-permute-start | bytes 294920 | tf_op jit(solution)/shard_map/ppermute | solution.py:159
  127.3 3.5 %collective-permute-start.16 = (f32[16,1024]{1,0:T(8,128)S(1)}, f32[16,1024]{1,0:T(8,128)S(1)}, u32[]{:S(2)}, u32[]{:S(2)}) collective-permute-start(f32[16,1024]{1,0:T(8,128)S(1)} %fusion.63), channel_id=1, source_target_pairs={{0,2},{1,3},{2,0},{3,1},{4,6},{5,7},{6,4},{7,5},{8,10},{9,11},{10,... | collective-permute-start | bytes 196616 | tf_op jit(solution)/shard_map/ppermute | solution.py:133
  130.8 6.5 %collective-permute-start.17 = (f32[32,1024]{1,0:T(8,128)S(1)}, f32[32,1024]{1,0:T(8,128)S(1)}, u32[]{:S(2)}, u32[]{:S(2)}) collective-permute-start(f32[32,1024]{1,0:T(8,128)S(1)} %maximum_select_fusion.3), channel_id=1, source_target_pairs={{0,1},{1,0},{2,3},{3,2},{4,5},{5,4},{6,7},{7,6},{8,9},{9,8},{10,11... | collective-permute-start | bytes 393224 | tf_op jit(solution)/shard_map/ppermute | solution.py:133

commit v11 on v9

--- a/solution.py
+++ b/solution.py
@@ -149,13 +149,17 @@
     done = list(first_done) + done
     block_size = 2 * low_bits[-1] if low_bits else 1
     if count // block_size == 8:
+        near = lambda z: z ^ 1
+        shifted = lambda z: (z + 1 if z % 2 == 1 else z - 1) % 8
         rounds = (
-            lambda z: z ^ 1,
-            lambda z: (z + 1 if z % 2 == 1 else z - 1) % 8,
-            lambda z: (3 - z) % 8 if z % 4 in (0, 3) else 7 - z,
+            (near, shifted, lambda z: (3 - z) % 8 if z % 4 in (0, 3) else 7 - z),
+            (shifted, near, lambda z: (5 - z) % 8 if z % 4 in (0, 1) else (9 - z) % 8),
         )
-        for partner in rounds:
-            pairs = [(i, partner(i // block_size) * block_size + i % block_size) for i in range(count)]
+        for step in range(3):
+            pairs = [
+                (i, rounds[i % 2][step](i // block_size) * block_size + i % block_size)
+                for i in range(count)
+            ]
             part = part + lax.ppermute(part, axis, pairs)
         return join_rounds(part, axis, done)
     bit = block_size

time: 139 us -> 139 us (level)
  starting transfers between devices: 39.2 us -> 34 us
  waiting for transfers between devices: 54.8 us -> 59.9 us
    ppermute x6, waiting for transfers between devices: 23.5 us -> 29.2 us  [species_sum(): part = part + lax.ppermute(part, axis, pairs)]
    ppermute x6, starting transfers between devices: 4.09 us -> 1.27 us  [species_sum(): part = part + lax.ppermute(part, axis, pairs)]
    ppermute x4, starting transfers between devices: 11.8 us -> 9.5 us  [join_rounds(): other = lax.ppermute(part, axis, xor_pairs(lax.axis_size(axis), bit))]
where the time goes in v11:
time: 139 us
  waiting for transfers between devices  59.9 us (43%)
  starting transfers between devices  34 us (24%)
  blocking collectives  21.9 us (16%)
  other arithmetic  16.3 us (12%)
  local copies, waits for them, and re-layouts  4.45 us (3%)
  between operations  2.6 us (2%)
    ppermute x6, waiting for transfers between devices, species_sum(): part = part + lax.ppermute(part, axis, pairs)  29.2 us
    all_to_all x1, blocking collectives, global_max(): return jnp.max(lax.all_to_all(spread, axes, 0, 0, tiled=True))  21.9 us
    all_to_all x1, waiting for transfers between devices, global_max(): return jnp.max(lax.all_to_all(spread, axes, 0, 0, tiled=True))  12.7 us
    all_to_all x1, starting transfers between devices, global_max(): return jnp.max(lax.all_to_all(spread, axes, 0, 0, tiled=True))  12.6 us
    ppermute x4, starting transfers between devices, join_rounds(): other = lax.ppermute(part, axis, xor_pairs(lax.axis_size(axis), bit))  9.5 us
    ppermute x4, waiting for transfers between devices, join_rounds(): other = lax.ppermute(part, axis, xor_pairs(lax.axis_size(axis), bit))  8.05 us
    ppermute x2, waiting for transfers between devices, split_rounds(): part = keep + lax.ppermute(send, axis, xor_pairs(lax.axis_size(axis), bit))  7.46 us
    ppermute x2, starting transfers between devices, padded(): lax.ppermute(lax.slice_in_dim(block, 0, width, axis=dim), axis, backward)  5.34 us
  transfers between devices with their start and end apart: 19, of which 15 were waited for; matrix products, arithmetic and copies ran while one was open for 4% of the time, Pallas kernels for 0%

profile of v11, /device:TPU:1, one launch (start us, length us, event | category | flops | bytes accessed | tf_op | source)
XLA Modules:
  0.0 139.1 jit_solution(7383885229070378546)
XLA Ops:
  0.7 1.4 %fusion.59 = (f32[3,5,2,1024]{3,2,1,0:T(2,128)S(1)}, f32[3,5,2,1024]{3,2,1,0:T(2,128)S(1)}) fusion(f32[3,4,32,1024]{3,2,1,0:T(8,128)} %param.3, f32[3,1,32,1024]{3,2,1,0:T(8,128)} %bitcast.92), kind=kLoop, calls=%fused_computation.150 | loop fusion | flops 61440 | bytes 2211840 | tf_op jit(solution)/shard_map/concatenate | solution.py:234
  2.1 2.2 %collective-permute-start = (f32[3,5,2,1024]{3,2,1,0:T(2,128)S(1)}, f32[3,5,2,1024]{3,2,1,0:T(2,128)S(1)}, u32[]{:S(2)}, u32[]{:S(2)}) collective-permute-start(f32[3,5,2,1024]{3,2,1,0:T(2,128)S(1)} %get-tuple-element.22), channel_id=1, source_target_pairs={{0,32},{32,64},{64,96},{96,128},{128,160},{160,192},{192,224},{224... | collective-permute-start | bytes 368648 | tf_op jit(solution)/shard_map/ppermute | solution.py:22
  4.3 4.0 %collective-permute-start.1 = (f32[3,5,2,1024]{3,2,1,0:T(2,128)S(1)}, f32[3,5,2,1024]{3,2,1,0:T(2,128)S(1)}, u32[]{:S(2)}, u32[]{:S(2)}) collective-permute-start(f32[3,5,2,1024]{3,2,1,0:T(2,128)S(1)} %get-tuple-element.23), channel_id=1, source_target_pairs={{32,0},{64,32},{96,64},{128,96},{160,128},{192,160},{224,192},{0,2... | collective-permute-start | bytes 368648 | tf_op jit(solution)/shard_map/ppermute | solution.py:25
  8.3 0.8 fusion.17
  9.0 1.4 broadcast_in_dim.13
  10.4 12.6 %all-to-all-start = ((f32[256,1,1]{2,1,0:T(1,128)}), f32[256,1,1]{2,1,0:T(1,128)S(1)}, u32[]{:S(2)}, u32[]{:S(2)}) async-start(f32[256,1,1]{2,1,0:T(1,128)} %broadcast_in_dim.13), calls=%async_computation | async-start | bytes 262144 | tf_op jit(solution)/shard_map/all_to_all | solution.py:111
  23.0 12.7 %all-to-all-done = f32[256,1,1]{2,1,0:T(1,128)S(1)} async-done(((f32[256,1,1]{2,1,0:T(1,128)}), f32[256,1,1]{2,1,0:T(1,128)S(1)}, u32[]{:S(2)}, u32[]{:S(2)}) %all-to-all-start) | async-done | bytes 1056 | tf_op jit(solution)/shard_map/all_to_all | solution.py:111
  35.7 0.9 reduce_max.37
  37.3 0.4 pad_maximum_fusion
  37.7 0.3 copy-done.9
  37.9 0.2 slice_bitcast_fusion.5
  38.3 0.6 fusion.10
  38.9 0.2 copy-done.2
  39.2 0.8 multiply_add_fusion.1
  40.0 0.2 fusion.23
  40.3 1.2 multiply_divide_fusion.1
  41.5 0.2 fusion.31
  41.7 0.6 copy-done.6
  42.3 0.7 fusion.57
  43.0 1.0 collective-permute-start.2
  44.0 1.4 %collective-permute-done.2 = f32[48,1024]{1,0:T(8,128)} collective-permute-done((f32[48,1024]{1,0:T(8,128)}, f32[48,1024]{1,0:T(8,128)}, u32[]{:S(2)}, u32[]{:S(2)}) %collective-permute-start.2) | collective-permute-done | bytes 196640 | tf_op jit(solution)/shard_map/ppermute | solution.py:223
  45.4 1.2 select_add_fusion.1
  46.6 0.4 collective-permute-start.3
  47.0 3.7 %collective-permute-done.3 = f32[24,1024]{1,0:T(8,128)S(1)} collective-permute-done((f32[24,1024]{1,0:T(8,128)S(1)}, f32[24,1024]{1,0:T(8,128)S(1)}, u32[]{:S(2)}, u32[]{:S(2)}) %collective-permute-start.3) | collective-permute-done | bytes 98336 | tf_op jit(solution)/shard_map/ppermute | solution.py:125
  50.7 0.5 collective-permute-start.4
  51.2 4.3 %collective-permute-done.4 = f32[24,1024]{1,0:T(8,128)S(1)} collective-permute-done((f32[24,1024]{1,0:T(8,128)S(1)}, f32[24,1024]{1,0:T(8,128)S(1)}, u32[]{:S(2)}, u32[]{:S(2)}) %collective-permute-start.4) | collective-permute-done | bytes 98336 | tf_op jit(solution)/shard_map/ppermute | solution.py:163
  55.7 3.3 %collective-permute-done.5 = f32[24,1024]{1,0:T(8,128)S(1)} collective-permute-done((f32[24,1024]{1,0:T(8,128)S(1)}, f32[24,1024]{1,0:T(8,128)S(1)}, u32[]{:S(2)}, u32[]{:S(2)}) %collective-permute-start.5) | collective-permute-done | bytes 98336 | tf_op jit(solution)/shard_map/ppermute | solution.py:163
  59.3 6.9 %collective-permute-done.6 = f32[24,1024]{1,0:T(8,128)S(1)} collective-permute-done((f32[24,1024]{1,0:T(8,128)S(1)}, f32[24,1024]{1,0:T(8,128)S(1)}, u32[]{:S(2)}, u32[]{:S(2)}) %collective-permute-start.6) | collective-permute-done | bytes 98336 | tf_op jit(solution)/shard_map/ppermute | solution.py:163
  66.2 0.4 collective-permute-start.7
  66.7 3.1 %collective-permute-done.7 = f32[24,1024]{1,0:T(8,128)S(1)} collective-permute-done((f32[24,1024]{1,0:T(8,128)S(1)}, f32[24,1024]{1,0:T(8,128)S(1)}, u32[]{:S(2)}, u32[]{:S(2)}) %collective-permute-start.7) | collective-permute-done | bytes 98336 | tf_op jit(solution)/shard_map/ppermute | solution.py:133
  69.8 4.4 %collective-permute-start.8 = (f32[48,1024]{1,0:T(8,128)S(1)}, f32[48,1024]{1,0:T(8,128)S(1)}, u32[]{:S(2)}, u32[]{:S(2)}) collective-permute-start(f32[48,1024]{1,0:T(8,128)S(1)} %maximum_select_fusion.2), channel_id=1, source_target_pairs={{0,1},{1,0},{2,3},{3,2},{4,5},{5,4},{6,7},{7,6},{8,9},{9,8},{10,11... | collective-permute-start | bytes 589832 | tf_op jit(solution)/shard_map/ppermute | solution.py:133
  74.2 0.1 fusion.55
  74.3 0.9 collective-permute-done.8
  75.4 0.3 fusion
  75.7 0.2 pad_maximum_fusion.2
  76.0 1.4 collective-permute-start.10
  77.4 0.4 collective-permute-start.9
  77.8 0.8 fusion.22
  78.5 0.7 broadcast_in_dim.16
  79.2 21.9 %all_to_all.12 = f32[256,1,1]{2,1,0:T(1,128)S(1)} all-to-all(f32[256,1,1]{2,1,0:T(1,128)S(1)} %broadcast_in_dim.16), channel_id=1, replica_groups=mesh['space'=8,'species'=32] {'space','species'}, dimensions={0} | all-to-all | bytes 2048 | tf_op jit(solution)/shard_map/all_to_all | solution.py:111
  101.2 0.9 reduce_max.39
  102.7 0.4 pad_maximum_fusion.1
  103.1 0.3 slice_bitcast_fusion.1
  103.5 0.6 fusion.4
  104.2 0.8 multiply_add_fusion
  105.0 0.2 fusion.20
  105.3 0.3 fusion.34
  105.6 0.2 fusion.27
  105.8 1.1 collective-permute-start.11
  106.9 1.1 collective-permute-done.11
  108.0 0.4 collective-permute-start.12
  108.4 3.7 %collective-permute-done.12 = f32[24,1024]{1,0:T(8,128)S(1)} collective-permute-done((f32[24,1024]{1,0:T(8,128)S(1)}, f32[24,1024]{1,0:T(8,128)S(1)}, u32[]{:S(2)}, u32[]{:S(2)}) %collective-permute-start.12) | collective-permute-done | bytes 98336 | tf_op jit(solution)/shard_map/ppermute | solution.py:125
  112.1 0.5 collective-permute-start.13
  112.7 4.2 %collective-permute-done.13 = f32[24,1024]{1,0:T(8,128)S(1)} collective-permute-done((f32[24,1024]{1,0:T(8,128)S(1)}, f32[24,1024]{1,0:T(8,128)S(1)}, u32[]{:S(2)}, u32[]{:S(2)}) %collective-permute-start.13) | collective-permute-done | bytes 98336 | tf_op jit(solution)/shard_map/ppermute | solution.py:163
  117.1 3.4 %collective-permute-done.14 = f32[24,1024]{1,0:T(8,128)S(1)} collective-permute-done((f32[24,1024]{1,0:T(8,128)S(1)}, f32[24,1024]{1,0:T(8,128)S(1)}, u32[]{:S(2)}, u32[]{:S(2)}) %collective-permute-start.14) | collective-permute-done | bytes 98336 | tf_op jit(solution)/shard_map/ppermute | solution.py:163
  120.7 7.0 %collective-permute-done.15 = f32[24,1024]{1,0:T(8,128)S(1)} collective-permute-done((f32[24,1024]{1,0:T(8,128)S(1)}, f32[24,1024]{1,0:T(8,128)S(1)}, u32[]{:S(2)}, u32[]{:S(2)}) %collective-permute-start.15) | collective-permute-done | bytes 98336 | tf_op jit(solution)/shard_map/ppermute | solution.py:163
  127.7 0.4 collective-permute-start.16
  128.0 0.1 fusion.44
  128.2 3.0 %collective-permute-done.16 = f32[24,1024]{1,0:T(8,128)S(1)} collective-permute-done((f32[24,1024]{1,0:T(8,128)S(1)}, f32[24,1024]{1,0:T(8,128)S(1)}, u32[]{:S(2)}, u32[]{:S(2)}) %collective-permute-start.16) | collective-permute-done | bytes 98336 | tf_op jit(solution)/shard_map/ppermute | solution.py:133
  131.2 4.4 %collective-permute-start.17 = (f32[48,1024]{1,0:T(8,128)S(1)}, f32[48,1024]{1,0:T(8,128)S(1)}, u32[]{:S(2)}, u32[]{:S(2)}) collective-permute-start(f32[48,1024]{1,0:T(8,128)S(1)} %maximum_select_fusion.3), channel_id=1, source_target_pairs={{0,1},{1,0},{2,3},{3,2},{4,5},{5,4},{6,7},{7,6},{8,9},{9,8},{10,11... | collective-permute-start | bytes 589832 | tf_op jit(solution)/shard_map/ppermute | solution.py:133
  135.7 1.0 collective-permute-done.17
  136.8 0.8 pad_maximum_fusion.4
  137.6 0.3 fusion.1
  137.9 1.2 pad_maximum_fusion.3
  (73 shorter events, 1.9 us)
Async XLA Ops:
  0.6 7.6 %copy-start.1 = (f32[3,32,1024]{2,1,0:T(8,128)S(1)}, f32[3,32,1024]{2,1,0:T(8,128)}, u32[]{:S(2)}) copy-start(f32[3,32,1024]{2,1,0:T(8,128)} %param.4) | copy-start | bytes 1179652
  0.6 7.6 %copy-start = (f32[3,4,32,1024]{3,2,1,0:T(8,128)S(1)}, f32[3,4,32,1024]{3,2,1,0:T(8,128)}, u32[]{:S(2)}) copy-start(f32[3,4,32,1024]{3,2,1,0:T(8,128)} %param.3) | copy-start | bytes 4718596
  0.6 22.3 %copy-start.13 = (s32[4]{0:T(128)S(1)}, s32[4]{0:T(128)}, u32[]{:S(2)}) copy-start(s32[4]{0:T(128)} %param.5) | copy-start | bytes 52
  2.1 35.2 %collective-permute-start = (f32[3,5,2,1024]{3,2,1,0:T(2,128)S(1)}, f32[3,5,2,1024]{3,2,1,0:T(2,128)S(1)}, u32[]{:S(2)}, u32[]{:S(2)}) collective-permute-start(f32[3,5,2,1024]{3,2,1,0:T(2,128)S(1)} %get-tuple-element.22), channel_id=1, source_target_pairs={{0,32},{32,64},{64,96},{96,128},{128,160},{160,192},{192,224},{224... | collective-permute-start | bytes 368648 | tf_op jit(solution)/shard_map/ppermute | solution.py:22
  4.3 33.0 %collective-permute-start.1 = (f32[3,5,2,1024]{3,2,1,0:T(2,128)S(1)}, f32[3,5,2,1024]{3,2,1,0:T(2,128)S(1)}, u32[]{:S(2)}, u32[]{:S(2)}) collective-permute-start(f32[3,5,2,1024]{3,2,1,0:T(2,128)S(1)} %get-tuple-element.23), channel_id=1, source_target_pairs={{32,0},{64,32},{96,64},{128,96},{160,128},{192,160},{224,192},{0,2... | collective-permute-start | bytes 368648 | tf_op jit(solution)/shard_map/ppermute | solution.py:25
  10.4 25.3 %all-to-all-start = ((f32[256,1,1]{2,1,0:T(1,128)}), f32[256,1,1]{2,1,0:T(1,128)S(1)}, u32[]{:S(2)}, u32[]{:S(2)}) async-start(f32[256,1,1]{2,1,0:T(1,128)} %broadcast_in_dim.13), calls=%async_computation | async-start | bytes 262144 | tf_op jit(solution)/shard_map/all_to_all | solution.py:111
  37.3 0.7 copy-start.9
  37.3 0.7 copy-start.11
  38.2 0.9 copy-start.2
  41.7 0.7 copy-start.6
  41.7 1.3 copy-start.7
  41.7 1.3 copy-start.8
  43.0 2.4 %collective-permute-start.2 = (f32[48,1024]{1,0:T(8,128)}, f32[48,1024]{1,0:T(8,128)}, u32[]{:S(2)}, u32[]{:S(2)}) collective-permute-start(f32[48,1024]{1,0:T(8,128)} %fusion.57), channel_id=1, source_target_pairs={{0,1},{1,0},{2,3},{3,2},{4,5},{5,4},{6,7},{7,6},{8,9},{9,8},{10,11... | collective-permute-start | bytes 589832 | tf_op jit(solution)/shard_map/ppermute | solution.py:223
  44.0 11.6 %copy-start.3 = (f32[5,36,1024]{2,1,0:T(8,128)S(1)}, f32[5,36,1024]{2,1,0:T(8,128)}, u32[]{:S(2)}) copy-start(f32[5,36,1024]{2,1,0:T(8,128)} %copy-done.2) | copy-start | bytes 2211844
  44.0 15.2 %copy-start.10 = (f32[3,5,2,1024]{3,2,1,0:T(2,128)S(1)}, f32[3,5,2,1024]{3,2,1,0:T(2,128)}, u32[]{:S(2)}) copy-start(f32[3,5,2,1024]{3,2,1,0:T(2,128)} %copy-done.9) | copy-start | bytes 368644
  44.0 15.2 %copy-start.12 = (f32[3,5,2,1024]{3,2,1,0:T(2,128)S(1)}, f32[3,5,2,1024]{3,2,1,0:T(2,128)}, u32[]{:S(2)}) copy-start(f32[3,5,2,1024]{3,2,1,0:T(2,128)} %copy-done.11) | copy-start | bytes 368644
  46.6 4.1 %collective-permute-start.3 = (f32[24,1024]{1,0:T(8,128)S(1)}, f32[24,1024]{1,0:T(8,128)S(1)}, u32[]{:S(2)}, u32[]{:S(2)}) collective-permute-start(f32[24,1024]{1,0:T(8,128)S(1)} %slice_select_fusion.1), channel_id=1, source_target_pairs={{0,2},{1,3},{2,0},{3,1},{4,6},{5,7},{6,4},{7,5},{8,10},{9,11},{10,... | collective-permute-start | bytes 294920 | tf_op jit(solution)/shard_map/ppermute | solution.py:125
  50.7 4.8 %collective-permute-start.4 = (f32[24,1024]{1,0:T(8,128)S(1)}, f32[24,1024]{1,0:T(8,128)S(1)}, u32[]{:S(2)}, u32[]{:S(2)}) collective-permute-start(f32[24,1024]{1,0:T(8,128)S(1)} %select_add_fusion.3), channel_id=1, source_target_pairs={{0,4},{1,29},{2,6},{3,31},{4,0},{5,9},{6,2},{7,11},{8,12},{9,5},{1... | collective-permute-start | bytes 294920 | tf_op jit(solution)/shard_map/ppermute | solution.py:163
  55.5 3.6 %collective-permute-start.5 = (f32[24,1024]{1,0:T(8,128)S(1)}, f32[24,1024]{1,0:T(8,128)S(1)}, u32[]{:S(2)}, u32[]{:S(2)}) collective-permute-start(f32[24,1024]{1,0:T(8,128)S(1)} %add.157), channel_id=1, source_target_pairs={{0,28},{1,5},{2,30},{3,7},{4,8},{5,1},{6,10},{7,3},{8,4},{9,13},{1... | collective-permute-start | bytes 294920 | tf_op jit(solution)/shard_map/ppermute | solution.py:163
  59.1 7.1 %collective-permute-start.6 = (f32[24,1024]{1,0:T(8,128)S(1)}, f32[24,1024]{1,0:T(8,128)S(1)}, u32[]{:S(2)}, u32[]{:S(2)}) collective-permute-start(f32[24,1024]{1,0:T(8,128)S(1)} %add.158), channel_id=1, source_target_pairs={{0,12},{1,21},{2,14},{3,23},{4,24},{5,17},{6,26},{7,19},{8,20},{9,... | collective-permute-start | bytes 294920 | tf_op jit(solution)/shard_map/ppermute | solution.py:163
  66.2 3.6 %collective-permute-start.7 = (f32[24,1024]{1,0:T(8,128)S(1)}, f32[24,1024]{1,0:T(8,128)S(1)}, u32[]{:S(2)}, u32[]{:S(2)}) collective-permute-start(f32[24,1024]{1,0:T(8,128)S(1)} %add.159), channel_id=1, source_target_pairs={{0,2},{1,3},{2,0},{3,1},{4,6},{5,7},{6,4},{7,5},{8,10},{9,11},{10,... | collective-permute-start | bytes 294920 | tf_op jit(solution)/shard_map/ppermute | solution.py:133
  66.7 8.7 %copy-start.4 = (f32[4,32,1024]{2,1,0:T(8,128)S(1)}, f32[4,32,1024]{2,1,0:T(8,128)}, u32[]{:S(2)}) copy-start(f32[4,32,1024]{2,1,0:T(8,128)} %get-tuple-element.30) | copy-start | bytes 1572868
  66.7 8.7 %copy-start.5 = (f32[4,32,1024]{2,1,0:T(8,128)S(1)}, f32[4,32,1024]{2,1,0:T(8,128)}, u32[]{:S(2)}) copy-start(f32[4,32,1024]{2,1,0:T(8,128)} %get-tuple-element.31) | copy-start | bytes 1572868
  69.8 5.4 %collective-permute-start.8 = (f32[48,1024]{1,0:T(8,128)S(1)}, f32[48,1024]{1,0:T(8,128)S(1)}, u32[]{:S(2)}, u32[]{:S(2)}) collective-permute-start(f32[48,1024]{1,0:T(8,128)S(1)} %maximum_select_fusion.2), channel_id=1, source_target_pairs={{0,1},{1,0},{2,3},{3,2},{4,5},{5,4},{6,7},{7,6},{8,9},{9,8},{10,11... | collective-permute-start | bytes 589832 | tf_op jit(solution)/shard_map/ppermute | solution.py:133
  76.0 26.7 %collective-permute-start.10 = (f32[3,5,2,1024]{3,2,1,0:T(2,128)S(1)}, f32[3,5,2,1024]{3,2,1,0:T(2,128)S(1)}, u32[]{:S(2)}, u32[]{:S(2)}) collective-permute-start(f32[3,5,2,1024]{3,2,1,0:T(2,128)S(1)} %get-tuple-element.21), channel_id=1, source_target_pairs={{32,0},{64,32},{96,64},{128,96},{160,128},{192,160},{224,192},{0,2... | collective-permute-start | bytes 368648 | tf_op jit(solution)/shard_map/ppermute | solution.py:25
  77.4 25.4 %collective-permute-start.9 = (f32[3,5,2,1024]{3,2,1,0:T(2,128)S(1)}, f32[3,5,2,1024]{3,2,1,0:T(2,128)S(1)}, u32[]{:S(2)}, u32[]{:S(2)}) collective-permute-start(f32[3,5,2,1024]{3,2,1,0:T(2,128)S(1)} %get-tuple-element.20), channel_id=1, source_target_pairs={{0,32},{32,64},{64,96},{96,128},{128,160},{160,192},{192,224},{224... | collective-permute-start | bytes 368648 | tf_op jit(solution)/shard_map/ppermute | solution.py:22
  105.8 2.1 %collective-permute-start.11 = (f32[48,1024]{1,0:T(8,128)S(1)}, f32[48,1024]{1,0:T(8,128)S(1)}, u32[]{:S(2)}, u32[]{:S(2)}) collective-permute-start(f32[48,1024]{1,0:T(8,128)S(1)} %fusion.58), channel_id=1, source_target_pairs={{0,1},{1,0},{2,3},{3,2},{4,5},{5,4},{6,7},{7,6},{8,9},{9,8},{10,11... | collective-permute-start | bytes 589832 | tf_op jit(solution)/shard_map/ppermute | solution.py:223
  108.0 4.1 %collective-permute-start.12 = (f32[24,1024]{1,0:T(8,128)S(1)}, f32[24,1024]{1,0:T(8,128)S(1)}, u32[]{:S(2)}, u32[]{:S(2)}) collective-permute-start(f32[24,1024]{1,0:T(8,128)S(1)} %slice_select_fusion), channel_id=1, source_target_pairs={{0,2},{1,3},{2,0},{3,1},{4,6},{5,7},{6,4},{7,5},{8,10},{9,11},{10,... | collective-permute-start | bytes 294920 | tf_op jit(solution)/shard_map/ppermute | solution.py:125
  112.1 4.8 %collective-permute-start.13 = (f32[24,1024]{1,0:T(8,128)S(1)}, f32[24,1024]{1,0:T(8,128)S(1)}, u32[]{:S(2)}, u32[]{:S(2)}) collective-permute-start(f32[24,1024]{1,0:T(8,128)S(1)} %select_add_fusion.2), channel_id=1, source_target_pairs={{0,4},{1,29},{2,6},{3,31},{4,0},{5,9},{6,2},{7,11},{8,12},{9,5},{1... | collective-permute-start | bytes 294920 | tf_op jit(solution)/shard_map/ppermute | solution.py:163
  116.9 3.6 %collective-permute-start.14 = (f32[24,1024]{1,0:T(8,128)S(1)}, f32[24,1024]{1,0:T(8,128)S(1)}, u32[]{:S(2)}, u32[]{:S(2)}) collective-permute-start(f32[24,1024]{1,0:T(8,128)S(1)} %add.173), channel_id=1, source_target_pairs={{0,28},{1,5},{2,30},{3,7},{4,8},{5,1},{6,10},{7,3},{8,4},{9,13},{1... | collective-permute-start | bytes 294920 | tf_op jit(solution)/shard_map/ppermute | solution.py:163
  120.5 7.1 %collective-permute-start.15 = (f32[24,1024]{1,0:T(8,128)S(1)}, f32[24,1024]{1,0:T(8,128)S(1)}, u32[]{:S(2)}, u32[]{:S(2)}) collective-permute-start(f32[24,1024]{1,0:T(8,128)S(1)} %add.174), channel_id=1, source_target_pairs={{0,12},{1,21},{2,14},{3,23},{4,24},{5,17},{6,26},{7,19},{8,20},{9,... | collective-permute-start | bytes 294920 | tf_op jit(solution)/shard_map/ppermute | solution.py:163
  127.7 3.6 %collective-permute-start.16 = (f32[24,1024]{1,0:T(8,128)S(1)}, f32[24,1024]{1,0:T(8,128)S(1)}, u32[]{:S(2)}, u32[]{:S(2)}) collective-permute-start(f32[24,1024]{1,0:T(8,128)S(1)} %add.175), channel_id=1, source_target_pairs={{0,2},{1,3},{2,0},{3,1},{4,6},{5,7},{6,4},{7,5},{8,10},{9,11},{10,... | collective-permute-start | bytes 294920 | tf_op jit(solution)/shard_map/ppermute | solution.py:133
  131.2 5.4 %collective-permute-start.17 = (f32[48,1024]{1,0:T(8,128)S(1)}, f32[48,1024]{1,0:T(8,128)S(1)}, u32[]{:S(2)}, u32[]{:S(2)}) collective-permute-start(f32[48,1024]{1,0:T(8,128)S(1)} %maximum_select_fusion.3), channel_id=1, source_target_pairs={{0,1},{1,0},{2,3},{3,2},{4,5},{5,4},{6,7},{7,6},{8,9},{9,8},{10,11... | collective-permute-start | bytes 589832 | tf_op jit(solution)/shard_map/ppermute | solution.py:133
